TPU v7x, 256 devices: a whole 4x4x8 slice. The times are simulated.
256 devices in a mesh: dp: 32 (over x, z), tensor: 8 (over y, core).
Axes of the slice: x: 4, y: 4, z: 8, core: 2. Of those that a mesh axis runs over, the one named last changes fastest.
Arguments:
- grads: bfloat16 [32, 8, 1024, 4096], P('dp', 'tensor'), may hold values from -8 to 8
- signs: int32 [8, 4096], P('tensor'), may hold values from 0 to 1
- shifts: int32 [32, 8, 1024], P('dp', 'tensor'), may hold values from 3 to 6
- first: float32 [8, 1024, 4096], P('tensor', 'dp'), may hold values from -1.8 to 1.8
- second: float32 [8, 1024, 4096], P('tensor', 'dp'), may hold values from 0.04 to 0.3
- weights: float32 [8, 1024, 4096], P('tensor', 'dp'), may hold values from -6 to 6
- slots: int32 [32, 8, 8, 16], P('dp', 'tensor'), may hold values from 0 to 31, as said below
- counts: int32 [32, 8, 8], P('dp', 'tensor'), may hold values from 1 to 16, as said below
Outputs:
- new_first: float32 [8, 1024, 4096], P('tensor', 'dp')
- new_second: float32 [8, 1024, 4096], P('tensor', 'dp')
- new_weights: float32 [8, 1024, 4096], P('tensor', 'dp')
- received: bfloat16 [32, 8, 8, 16, 512], P('dp', 'tensor')
Inputs may be any that keep to these rules, and one draw needn't show every extreme that they name: The same ids within one list are distinct; slots from the count on are ignored. For each worker row d one owner o has counts[d, t, o] = 16 for every source t.
All inputs are finite; a program needn't handle non-finite values.
Results may differ from a plain program's by a relative error of at most 0.0019.
Values may be sent and summed in bfloat16 or wider, within the bound.
No kernel may reach another device: no remote copies, remote signals or barrier semaphores. Data moves between devices by JAX's collectives and lax.ppermute only.
A program may use at most 128 MiB of HBM per device.

v0:
```python
import math

import jax
import jax.numpy as jnp
from jax import lax
from jax.sharding import PartitionSpec as P

HA = 32
HB = 128


first_keep = 0.9
first_take = 0.1
second_keep = 0.95
second_take = 0.05
first_fix = 1.0 - 0.9**10
second_fix = 1.0 - 0.95**10
adam_eps = 1e-08
learn_rate = 0.2


def walsh_table(table_order):
    positions = jnp.arange(table_order, dtype=jnp.int32)
    common_bits = jnp.bitwise_and(positions[:, None], positions[None, :])
    parity_sum = jnp.zeros((table_order, table_order), jnp.int32)
    for bit_level in range(max(table_order.bit_length() - 1, 1)):
        parity_sum = parity_sum + jnp.bitwise_and(jnp.right_shift(common_bits, bit_level), 1)
    return (1 - 2 * jnp.bitwise_and(parity_sum, 1)).astype(jnp.float32)


def rotate(flat_rows):
    count_rows = flat_rows.shape[0]
    cube_rows = flat_rows.reshape(count_rows, HA, HB)
    cube_rows = jnp.einsum(
        "rab,bc->rac", cube_rows, walsh_table(HB), precision=lax.Precision.HIGHEST
    )
    cube_rows = jnp.einsum(
        "ka,rac->rkc", walsh_table(HA), cube_rows, precision=lax.Precision.HIGHEST
    )
    return cube_rows.reshape(count_rows, HA * HB) / math.sqrt(HA * HB)


def half_power(shift_vals):
    unit_scale = jnp.ones(shift_vals.shape, jnp.float32)
    factor = 0.5
    for bit_level in range(5):
        chosen = jnp.bitwise_and(jnp.right_shift(shift_vals, bit_level), 1) == 1
        unit_scale = unit_scale * jnp.where(chosen, factor, 1.0).astype(jnp.float32)
        factor = factor * factor
    return unit_scale


def select_pieces(slab_view, slot_lists, used_counts):
    gathered = jnp.take_along_axis(slab_view, slot_lists[:, :, None], axis=1)
    live_slots = lax.broadcasted_iota(jnp.int32, slot_lists.shape, 1) < used_counts[:, None]
    return jnp.where(live_slots[:, :, None], gathered, jnp.zeros((), jnp.bfloat16))


def per_device(grads, signs, shifts, first, second, weights, slots, counts):
    sign_vec = (2 * signs[0] - 1).astype(jnp.float32)
    grad_rows = grads[0, 0]
    shift_rows = shifts[0, 0]
    blocks = first.shape[1]
    rotated = rotate(grad_rows.astype(jnp.float32) * sign_vec[None, :])
    unit_scale = half_power(shift_rows)[:, None]
    coded = jnp.clip(rotated / unit_scale, -127.0, 127.0).astype(jnp.bfloat16)
    summed = lax.psum_scatter(
        coded.astype(jnp.float32) * unit_scale, "dp", scatter_dimension=0, tiled=True
    )
    mean_grad = summed / lax.axis_size("dp")
    new_first = first_keep * first[0] + first_take * mean_grad
    new_second = second_keep * second[0] + second_take * mean_grad * mean_grad
    step_dir = new_first / first_fix / (jnp.sqrt(new_second / second_fix) + adam_eps)
    weight_step = rotate(step_dir) * sign_vec[None, :]
    new_weights = weights[0] - learn_rate * weight_step
    owners = lax.axis_size("tensor")
    piece_width = new_weights.shape[1] // owners
    narrow = new_weights.astype(jnp.bfloat16).reshape(blocks, owners, piece_width)
    slab_view = jnp.transpose(narrow, (1, 0, 2))
    slot_lists = slots[0, 0]
    used_counts = counts[0, 0]
    chosen_pieces = select_pieces(slab_view, slot_lists, used_counts)
    arrived = lax.all_to_all(chosen_pieces, "tensor", split_axis=0, concat_axis=0, tiled=True)
    return (new_first[None], new_second[None], new_weights[None], arrived[None, None])


def solution(mesh):
    return jax.shard_map(
        per_device,
        mesh=mesh,
        in_specs=(
            P("dp", "tensor", None, None),
            P("tensor", None),
            P("dp", "tensor", None),
            P("tensor", "dp", None),
            P("tensor", "dp", None),
            P("tensor", "dp", None),
            P("dp", "tensor", None, None),
            P("dp", "tensor", None),
        ),
        out_specs=(
            P("tensor", "dp", None),
            P("tensor", "dp", None),
            P("tensor", "dp", None),
            P("dp", "tensor", None, None, None),
        ),
        check_vma=False,
    )
```

profile of v0, /device:TPU:1, one launch (start us, length us, event | category | flops | bytes accessed | tf_op | source)
XLA Modules:
  0.0 365.9 jit_solution(9450548136910247016)
XLA Ops:
  7.2 0.0 reduce-scatter.2.cloned.1.call-start
  7.2 11.4 %convert_bitcast_fusion = f32[128,8,32,128]{3,1,2,0:T(8,128)} fusion(bf16[1,1,1024,4096]{3,2,1,0:T(8,128)(2,1)} %param.8), kind=kLoop, calls=%fused_computation.5 | loop fusion | flops 4194304 | bytes 25165824
  18.6 0.0 copy-start.3
  18.6 9.4 %copy.15 = f32[128,8,32,128]{3,2,1,0:T(8,128)S(1)} copy(f32[128,8,32,128]{3,1,2,0:T(8,128)} %convert_bitcast_fusion) | data formatting | bytes 33554432
  28.0 0.0 copy-done.3
  28.1 2.1 bitcast_multiply_fusion
  30.2 16.1 %fusion.9 = f32[1024,32,128]{2,1,0:T(8,128)} fusion(f32[1024,32,128]{2,1,0:T(8,128)S(1)} %bitcast_multiply_fusion), kind=kOutput, calls=%fused_computation.23 | convolution fusion | flops 6442860544 | bytes 33554432 | tf_op jit(solution)/shard_map/rab,bc->rac/dot_general | solution.py:34
  46.3 0.0 copy-start.5
  46.3 21.3 %convolution_multiply_fusion = f32[1024,128,32]{1,2,0:T(8,128)} fusion(f32[1024,32,128]{2,1,0:T(8,128)} %fusion.9), kind=kOutput, calls=%fused_computation.7 | convolution fusion | flops 1614826496 | bytes 33554432 | tf_op jit(solution)/shard_map/ka,rac->rkc/dot_general | solution.py:37
  67.6 0.0 copy-done.5
  67.7 22.2 %convert_multiply_fusion = f32[1024,4096]{1,0:T(8,128)} fusion(f32[128,8,32,128]{3,2,1,0:T(8,128)} %bitcast.70, f32[1024]{0:T(1024)S(1)} %bitcast.78), kind=kLoop, calls=%fused_computation.6 | loop fusion | flops 20971520 | bytes 33558528 | tf_op jit(solution)/shard_map/mul | solution.py:68
  89.9 0.0 copy-start
  89.9 0.0 copy-start.4
  89.9 0.0 copy-start.6
  89.9 0.0 copy-start.1
  89.9 0.0 copy-start.2
  89.9 0.0 reduce-scatter.2.cloned.1.call-update
  89.9 0.1 fusion.48
  90.0 0.9 copy-done
  90.9 0.3 copy.18
  91.2 0.0 copy-done.4
  91.3 0.1 reshape.238
  91.3 0.0 copy-done.6
  91.3 0.1 iota_compare_fusion
  91.4 245.9 %reduce-scatter.2.cloned.1.call-done = f32[32,4096]{1,0:T(8,128)} async-done(((f32[1024,4096]{1,0:T(8,128)}), f32[32,4096]{1,0:T(8,128)}) %reduce-scatter.2.cloned.1.call-update) | async-done | bytes 524304 | tf_op jit(solution)/shard_map/reduce_scatter | solution.py:67
  337.3 0.0 copy-done.1
  337.3 0.0 copy-done.2
  337.3 2.4 divide_bitcast_fusion
  339.6 0.1 copy.17
  339.7 0.6 fusion.7
  340.4 0.6 convolution_bitcast_fusion
  340.9 0.1 reshape.232
  341.0 0.1 reshape.231
  341.1 0.6 fusion.4
  341.7 1.3 gather_fusion
  343.1 0.8 select_select_fusion
  343.8 9.3 %all-to-all-start = ((bf16[8,16,512]{2,1,0:T(8,128)(2,1)}), bf16[8,16,512]{2,1,0:T(8,128)(2,1)S(1)}, u32[]{:S(2)}, u32[]{:S(2)}) async-start(bf16[8,16,512]{2,1,0:T(8,128)(2,1)} %select_select_fusion), calls=%async_computation.1 | async-start | bytes 262144 | tf_op jit(solution)/shard_map/all_to_all | solution.py:83
  353.2 0.9 multiply_subtract_fusion
  354.0 4.4 %all-to-all-done = bf16[8,16,512]{2,1,0:T(8,128)(2,1)S(1)} async-done(((bf16[8,16,512]{2,1,0:T(8,128)(2,1)}), bf16[8,16,512]{2,1,0:T(8,128)(2,1)S(1)}, u32[]{:S(2)}, u32[]{:S(2)}) %all-to-all-start) | async-done | bytes 131104 | tf_op jit(solution)/shard_map/all_to_all | solution.py:83
  358.4 0.7 copy.35
  (4 shorter events, 0.1 us)
Async XLA Ops:
  7.2 330.1 %reduce-scatter.2.cloned.1.call-start = ((), (), s32[]{:S(2)}) async-start(), calls=%async_computation.2 | async-start | bytes 17301504 | tf_op jit(solution)/shard_map/reduce_scatter | solution.py:67
  18.6 9.4 %copy-start.3 = (s32[1,4096]{1,0:T(1,128)S(1)}, s32[1,4096]{1,0:T(1,128)}, u32[]{:S(2)}) copy-start(s32[1,4096]{1,0:T(1,128)} %param.9) | copy-start | bytes 49156
  46.3 21.3 %copy-start.5 = (s32[1,1,1024]{2,1,0:T(1,128)S(1)}, s32[1,1,1024]{2,1,0:T(1,128)}, u32[]{:S(2)}) copy-start(s32[1,1,1024]{2,1,0:T(1,128)} %param.10) | copy-start | bytes 12292
  89.9 1.0 copy-start
  89.9 1.4 copy-start.4
  89.9 1.5 copy-start.6
  89.9 247.4 %copy-start.1 = (f32[1,32,4096]{2,1,0:T(8,128)S(1)}, f32[1,32,4096]{2,1,0:T(8,128)}, u32[]{:S(2)}) copy-start(f32[1,32,4096]{2,1,0:T(8,128)} %param.11) | copy-start | bytes 1572868
  89.9 247.4 %copy-start.2 = (f32[1,32,4096]{2,1,0:T(8,128)S(1)}, f32[1,32,4096]{2,1,0:T(8,128)}, u32[]{:S(2)}) copy-start(f32[1,32,4096]{2,1,0:T(8,128)} %param.12) | copy-start | bytes 1572868
  343.8 14.6 %all-to-all-start = ((bf16[8,16,512]{2,1,0:T(8,128)(2,1)}), bf16[8,16,512]{2,1,0:T(8,128)(2,1)S(1)}, u32[]{:S(2)}, u32[]{:S(2)}) async-start(bf16[8,16,512]{2,1,0:T(8,128)(2,1)} %select_select_fusion), calls=%async_computation.1 | async-start | bytes 262144 | tf_op jit(solution)/shard_map/all_to_all | solution.py:83
Sparse Core Ops, SparseCore 0:
  90.0 247.1 reduce-scatter.1
where the time goes:
time: 366 us
  waiting for transfers between devices  250 us (68%)
  other arithmetic  40.5 us (11%)
  matrix products  38.6 us (11%)
  between operations  14.2 us (4%)
  local copies, waits for them, and re-layouts  13 us (4%)
  starting transfers between devices  9.36 us (3%)
    reduce_scatter x1, waiting for transfers between devices, per_device(): lax.psum_scatter(coded.astype(jnp.float32) * unit_scale, 'dp', scatter_di...  246 us
    mul x1, other arithmetic, per_device(): coded.astype(jnp.float32) * unit_scale  22.2 us
    dot_general x2, matrix products, rotate(): jnp.einsum('ka,rac->rkc', walsh_table(HA), cube_rows, precision=lax.Preci...  21.9 us
    dot_general x2, matrix products, rotate(): jnp.einsum('rab,bc->rac', cube_rows, walsh_table(HB), precision=lax.Preci...  16.7 us
    unnamed x2, other arithmetic  13.7 us
    unnamed x18, local copies, waits for them, and re-layouts  11.4 us
    all_to_all x1, starting transfers between devices, per_device(): lax.all_to_all(chosen_pieces, 'tensor', split_axis=0, concat_axis=0, tile...  9.32 us
  transfers between devices with their start and end apart: 2, of which 2 were waited for; matrix products, arithmetic and copies ran while one was open for 0% of the time, Pallas kernels for 0%

commit v1 on v0

--- a/solution.py
+++ b/solution.py
@@ -3,10 +3,13 @@
 import jax
 import jax.numpy as jnp
 from jax import lax
+from jax.experimental import pallas as pl
+from jax.experimental.pallas import tpu as pltpu
 from jax.sharding import PartitionSpec as P
 
 HA = 32
 HB = 128
+ROW_TILE = 256
 
 
 first_keep = 0.9
@@ -50,6 +53,58 @@
     return unit_scale
 
 
+def butterfly(blocks):
+    blocks = list(blocks)
+    span = 1
+    while span < len(blocks):
+        for start in range(0, len(blocks), 2 * span):
+            for j in range(start, start + span):
+                u, v = blocks[j], blocks[j + span]
+                blocks[j], blocks[j + span] = u + v, u - v
+        span *= 2
+    return blocks
+
+
+def code_kernel(x_ref, w_ref, up_ref, dn_ref, o_ref, y_ref):
+    for a in range(HA):
+        cols = slice(a * HB, (a + 1) * HB)
+        y_ref[:, cols] = jnp.dot(x_ref[:, cols], w_ref[a], preferred_element_type=jnp.float32)
+
+    def row_group(g, carry):
+        rows = pl.ds(pl.multiple_of(g * 8, 8), 8)
+        blocks = butterfly([y_ref[rows, a * HB:(a + 1) * HB] for a in range(HA)])
+        up = up_ref[rows, :]
+        dn = dn_ref[rows, :]
+        for a in range(HA):
+            coded = jnp.clip(blocks[a] * up, -127.0, 127.0).astype(jnp.bfloat16)
+            o_ref[rows, a * HB:(a + 1) * HB] = (coded.astype(jnp.float32) * dn).astype(o_ref.dtype)
+        return carry
+
+    lax.fori_loop(0, x_ref.shape[0] // 8, row_group, 0)
+
+
+def decoded_terms(grad_rows, signed_walsh, up_scale, down_scale):
+    rows, width = grad_rows.shape
+    return pl.pallas_call(
+        code_kernel,
+        grid=(rows // ROW_TILE,),
+        in_specs=[
+            pl.BlockSpec((ROW_TILE, width), lambda i: (i, 0)),
+            pl.BlockSpec((HA, HB, HB), lambda i: (0, 0, 0)),
+            pl.BlockSpec((ROW_TILE, 1), lambda i: (i, 0)),
+            pl.BlockSpec((ROW_TILE, 1), lambda i: (i, 0)),
+        ],
+        out_specs=pl.BlockSpec((ROW_TILE, width), lambda i: (i, 0)),
+        out_shape=jax.ShapeDtypeStruct((rows, width), jnp.bfloat16),
+        scratch_shapes=[pltpu.VMEM((ROW_TILE, width), jnp.float32)],
+        cost_estimate=pl.CostEstimate(
+            flops=2 * rows * width * HB + 8 * rows * width,
+            transcendentals=0,
+            bytes_accessed=rows * width * 4,
+        ),
+    )(grad_rows, signed_walsh, up_scale, down_scale)
+
+
 def select_pieces(slab_view, slot_lists, used_counts):
     gathered = jnp.take_along_axis(slab_view, slot_lists[:, :, None], axis=1)
     live_slots = lax.broadcasted_iota(jnp.int32, slot_lists.shape, 1) < used_counts[:, None]
@@ -61,13 +116,14 @@
     grad_rows = grads[0, 0]
     shift_rows = shifts[0, 0]
     blocks = first.shape[1]
-    rotated = rotate(grad_rows.astype(jnp.float32) * sign_vec[None, :])
+    signed_walsh = (sign_vec.reshape(HA, HB, 1) * walsh_table(HB)[None]).astype(jnp.bfloat16)
     unit_scale = half_power(shift_rows)[:, None]
-    coded = jnp.clip(rotated / unit_scale, -127.0, 127.0).astype(jnp.bfloat16)
-    summed = lax.psum_scatter(
-        coded.astype(jnp.float32) * unit_scale, "dp", scatter_dimension=0, tiled=True
-    )
-    mean_grad = summed / lax.axis_size("dp")
+    up_scale = (1.0 / unit_scale) / math.sqrt(HA * HB)
+    terms = decoded_terms(grad_rows, signed_walsh, up_scale, unit_scale)
+    workers = lax.axis_size("dp")
+    arrived_terms = lax.all_to_all(terms, "dp", split_axis=0, concat_axis=0, tiled=True)
+    summed = arrived_terms.reshape(workers, blocks, -1).astype(jnp.float32).sum(0)
+    mean_grad = summed / workers
     new_first = first_keep * first[0] + first_take * mean_grad
     new_second = second_keep * second[0] + second_take * mean_grad * mean_grad
     step_dir = new_first / first_fix / (jnp.sqrt(new_second / second_fix) + adam_eps)

time: 366 us -> 251 us (0.69)
  waiting for transfers between devices: 250 us -> 192 us
  matrix products: 38.6 us -> 1.19 us
  other arithmetic: 40.5 us -> 13.3 us
  Pallas kernels: 0 us -> 19 us
  between operations: 14.2 us -> 0.86 us
  local copies, waits for them, and re-layouts: 13 us -> 3.19 us
  starting transfers between devices: 9.36 us -> 18 us
    reduce_scatter x1 -> x0, waiting for transfers between devices: 246 us -> none  [per_device(): lax.psum_scatter(coded.astype(jnp.float32) * unit_scale, 'dp', scatter_di...]
    all_to_all x0 -> x1, waiting for transfers between devices: none -> 188 us  [per_device(): lax.all_to_all(terms, 'dp', split_axis=0, concat_axis=0, tiled=True)]
    mul x2 -> x0, other arithmetic: 24.4 us -> none  [the longest x1 22.2 us: per_device(): coded.astype(jnp.float32) * unit_scale]
    dot_general x2 -> x1, matrix products: 21.9 us -> 0.58 us  [rotate(): jnp.einsum('ka,rac->rkc', walsh_table(HA), cube_rows, precision=lax.Preci...]
    pallas_call x0 -> x1, Pallas kernels: none -> 19 us  [decoded_terms(): pl.pallas_call(code_kernel, grid=(rows // ROW_TILE,), in_specs=[pl.BlockS...]
    dot_general x2 -> x1, matrix products: 16.7 us -> 0.61 us  [rotate(): jnp.einsum('rab,bc->rac', cube_rows, walsh_table(HB), precision=lax.Preci...]
    unnamed x2, other arithmetic: 13.7 us -> 1.27 us
    all_to_all x0 -> x1, starting transfers between devices: none -> 12.1 us  [per_device(): lax.all_to_all(terms, 'dp', split_axis=0, concat_axis=0, tiled=True)]
  transfers between devices with their start and end apart: 2 -> 2, of which waited for: 2 -> 2; matrix products, arithmetic and copies ran while one was open for 0% -> 1% of each run, Pallas kernels for 0% -> 0%
where the time goes in v1:
time: 251 us; the launch traced here: 247 us
  waiting for transfers between devices  192 us (76%)
  Pallas kernels  19 us (8%)
  starting transfers between devices  18 us (7%)
  other arithmetic  13.3 us (5%)
  local copies, waits for them, and re-layouts  3.19 us (1%)
    all_to_all x1, waiting for transfers between devices, per_device(): lax.all_to_all(terms, 'dp', split_axis=0, concat_axis=0, tiled=True)  188 us
    pallas_call x1, Pallas kernels, decoded_terms(): pl.pallas_call(code_kernel, grid=(rows // ROW_TILE,), in_specs=[pl.BlockS...  19 us
    all_to_all x1, starting transfers between devices, per_device(): lax.all_to_all(terms, 'dp', split_axis=0, concat_axis=0, tiled=True)  12.1 us
    all_to_all x1, starting transfers between devices, per_device(): lax.all_to_all(chosen_pieces, 'tensor', split_axis=0, concat_axis=0, tile...  5.85 us
    reduce_sum x1, other arithmetic, per_device(): arrived_terms.reshape(workers, blocks, -1).astype(jnp.float32).sum(0)  5.23 us
  transfers between devices with their start and end apart: 2, of which 2 were waited for; matrix products, arithmetic and copies ran while one was open for 1% of the time, Pallas kernels for 0%

profile of v1, /device:TPU:1, one launch (start us, length us, event | category | flops | bytes accessed | tf_op | source)
XLA Modules:
  0.0 247.4 jit_solution(134374807406971529)
XLA Ops:
  0.6 0.1 subtract_convert_fusion
  0.7 0.7 fusion.45
  1.4 0.2 copy.18.dn_ref
  1.6 0.0 copy-start
  1.7 0.9 divide_multiply_fusion.up_ref
  2.6 0.7 add_convert_fusion
  3.3 1.7 multiply_convert_fusion.w_ref
  5.0 0.0 copy-done
  5.0 19.0 %shard_map.111 = bf16[1024,4096]{1,0:T(8,128)(2,1)} custom-call(bf16[1024,4096]{1,0:T(8,128)(2,1)} %bitcast.67, bf16[32,128,128]{2,1,0:T(8,128)(2,1)} %multiply_convert_fusion.w_ref, f32[1024,1]{1,0:T(8,128)} %divide_multiply_fusion.up_ref, f32[1024,1]{1,0:T(8,128)} %copy-done), custom_call_target="tpu_custom_call" | custom-call | flops 1107296256 | bytes 16777216 | tf_op jit(solution)/shard_map/pallas_call | solution.py:88
  24.0 0.0 copy-start.4
  24.0 0.0 copy-start.1
  24.0 0.0 copy-start.5
  24.1 0.0 copy-start.6
  24.1 12.1 %all-to-all-start = ((bf16[32,32,4096]{2,1,0:T(8,128)(2,1)}), bf16[32,32,4096]{2,1,0:T(8,128)(2,1)}, u32[]{:S(2)}, u32[]{:S(2)}) async-start(bf16[32,32,4096]{2,1,0:T(8,128)(2,1)} %bitcast.66), calls=%async_computation | async-start | bytes 16777216 | tf_op jit(solution)/shard_map/all_to_all | solution.py:124
  36.2 0.0 copy-done.4
  36.2 0.0 copy-start.2
  36.2 0.0 copy-start.3
  36.2 0.1 fusion.58
  36.3 0.0 copy-done.1
  36.3 0.3 copy.26
  36.6 0.0 copy-done.5
  36.7 0.1 reshape.399
  36.7 0.0 copy-done.6
  36.7 0.1 iota_compare_fusion
  36.8 187.5 %all-to-all-done = bf16[32,32,4096]{2,1,0:T(8,128)(2,1)} async-done(((bf16[32,32,4096]{2,1,0:T(8,128)(2,1)}), bf16[32,32,4096]{2,1,0:T(8,128)(2,1)}, u32[]{:S(2)}, u32[]{:S(2)}) %all-to-all-start) | async-done | bytes 8388640 | tf_op jit(solution)/shard_map/all_to_all | solution.py:124
  224.4 5.2 %convert_reduce_fusion = f32[32,4096]{1,0:T(8,128)S(1)} fusion(bf16[32,32,4096]{2,1,0:T(8,128)(2,1)} %all-to-all-done), kind=kLoop, calls=%fused_computation.1 | loop fusion | flops 8257536 | bytes 8912896 | tf_op jit(solution)/shard_map/reduce_sum | solution.py:125
  229.6 0.1 multiply_bitcast_fusion.1
  229.7 0.0 copy-done.2
  229.7 0.0 copy-done.3
  229.7 1.2 multiply_bitcast_fusion.2
  230.9 0.1 copy.22
  231.0 0.1 copy.24
  231.1 0.1 copy.23
  231.2 0.1 copy.25
  231.3 0.3 fusion.3
  231.6 0.6 fusion.9
  232.2 0.6 convolution_bitcast_fusion
  232.8 0.1 reshape.394
  232.9 0.1 reshape.393
  233.0 0.6 fusion.8
  233.6 1.3 gather_fusion
  234.9 0.8 select_select_fusion
  235.7 5.9 %all-to-all-start.1 = ((bf16[8,16,512]{2,1,0:T(8,128)(2,1)}), bf16[8,16,512]{2,1,0:T(8,128)(2,1)S(1)}, u32[]{:S(2)}, u32[]{:S(2)}) async-start(bf16[8,16,512]{2,1,0:T(8,128)(2,1)} %select_select_fusion), calls=%async_computation.1 | async-start | bytes 262144 | tf_op jit(solution)/shard_map/all_to_all | solution.py:139
  241.5 0.9 multiply_subtract_fusion
  242.4 4.4 %all-to-all-done.1 = bf16[8,16,512]{2,1,0:T(8,128)(2,1)S(1)} async-done(((bf16[8,16,512]{2,1,0:T(8,128)(2,1)}), bf16[8,16,512]{2,1,0:T(8,128)(2,1)S(1)}, u32[]{:S(2)}, u32[]{:S(2)}) %all-to-all-start.1) | async-done | bytes 131104 | tf_op jit(solution)/shard_map/all_to_all | solution.py:139
  246.8 0.7 copy.40
  (2 shorter events, 0.0 us)
Async XLA Ops:
  1.6 3.4 %copy-start = (f32[1024,1]{1,0:T(8,128)}, f32[1024,1]{1,0:T(8,128)S(1)}, u32[]{:S(2)}) copy-start(f32[1024,1]{1,0:T(8,128)S(1)} %copy.18.dn_ref) | copy-start | bytes 12292
  24.0 12.2 %copy-start.4 = (s32[1,4096]{1,0:T(1,128)S(1)}, s32[1,4096]{1,0:T(1,128)}, u32[]{:S(2)}) copy-start(s32[1,4096]{1,0:T(1,128)} %param.9) | copy-start | bytes 49156
  24.0 12.3 %copy-start.1 = (f32[1,32,4096]{2,1,0:T(8,128)S(1)}, f32[1,32,4096]{2,1,0:T(8,128)}, u32[]{:S(2)}) copy-start(f32[1,32,4096]{2,1,0:T(8,128)} %param.13) | copy-start | bytes 1572868
  24.0 12.6 %copy-start.5 = (s32[1,1,8,16]{3,2,1,0:T(8,128)S(1)}, s32[1,1,8,16]{3,2,1,0:T(8,128)}, u32[]{:S(2)}) copy-start(s32[1,1,8,16]{3,2,1,0:T(8,128)} %param.14) | copy-start | bytes 1540
  24.1 12.7 %copy-start.6 = (s32[1,1,8]{2,1,0:T(1,128)S(1)}, s32[1,1,8]{2,1,0:T(1,128)}, u32[]{:S(2)}) copy-start(s32[1,1,8]{2,1,0:T(1,128)} %param.15) | copy-start | bytes 100
  24.1 200.3 %all-to-all-start = ((bf16[32,32,4096]{2,1,0:T(8,128)(2,1)}), bf16[32,32,4096]{2,1,0:T(8,128)(2,1)}, u32[]{:S(2)}, u32[]{:S(2)}) async-start(bf16[32,32,4096]{2,1,0:T(8,128)(2,1)} %bitcast.66), calls=%async_computation | async-start | bytes 16777216 | tf_op jit(solution)/shard_map/all_to_all | solution.py:124
  36.2 193.5 %copy-start.2 = (f32[1,32,4096]{2,1,0:T(8,128)S(1)}, f32[1,32,4096]{2,1,0:T(8,128)}, u32[]{:S(2)}) copy-start(f32[1,32,4096]{2,1,0:T(8,128)} %param.11) | copy-start | bytes 1572868
  36.2 193.5 %copy-start.3 = (f32[1,32,4096]{2,1,0:T(8,128)S(1)}, f32[1,32,4096]{2,1,0:T(8,128)}, u32[]{:S(2)}) copy-start(f32[1,32,4096]{2,1,0:T(8,128)} %param.12) | copy-start | bytes 1572868
  235.7 11.1 %all-to-all-start.1 = ((bf16[8,16,512]{2,1,0:T(8,128)(2,1)}), bf16[8,16,512]{2,1,0:T(8,128)(2,1)S(1)}, u32[]{:S(2)}, u32[]{:S(2)}) async-start(bf16[8,16,512]{2,1,0:T(8,128)(2,1)} %select_select_fusion), calls=%async_computation.1 | async-start | bytes 262144 | tf_op jit(solution)/shard_map/all_to_all | solution.py:139

commit v2 on v1

--- a/solution.py
+++ b/solution.py
@@ -5,11 +5,14 @@
 from jax import lax
 from jax.experimental import pallas as pl
 from jax.experimental.pallas import tpu as pltpu
+from jax.sharding import Mesh
 from jax.sharding import PartitionSpec as P
 
 HA = 32
 HB = 128
 ROW_TILE = 256
+X_CHIPS = 4
+WORKERS = ("wx", "wz")
 
 
 first_keep = 0.9
@@ -120,9 +123,11 @@
     unit_scale = half_power(shift_rows)[:, None]
     up_scale = (1.0 / unit_scale) / math.sqrt(HA * HB)
     terms = decoded_terms(grad_rows, signed_walsh, up_scale, unit_scale)
-    workers = lax.axis_size("dp")
-    arrived_terms = lax.all_to_all(terms, "dp", split_axis=0, concat_axis=0, tiled=True)
-    summed = arrived_terms.reshape(workers, blocks, -1).astype(jnp.float32).sum(0)
+    x_size = lax.axis_size("wx")
+    workers = x_size * lax.axis_size("wz")
+    arrived_terms = lax.all_to_all(terms, "wx", split_axis=0, concat_axis=0, tiled=True)
+    partial = arrived_terms.reshape(x_size, grad_rows.shape[0] // x_size, -1).astype(jnp.float32).sum(0)
+    summed = lax.psum_scatter(partial, "wz", scatter_dimension=0, tiled=True)
     mean_grad = summed / workers
     new_first = first_keep * first[0] + first_take * mean_grad
     new_second = second_keep * second[0] + second_take * mean_grad * mean_grad
@@ -141,24 +146,28 @@
 
 
 def solution(mesh):
+    dp_size, tensor_size = mesh.devices.shape
+    split_mesh = Mesh(
+        mesh.devices.reshape(X_CHIPS, dp_size // X_CHIPS, tensor_size), WORKERS + ("tensor",)
+    )
     return jax.shard_map(
         per_device,
-        mesh=mesh,
+        mesh=split_mesh,
         in_specs=(
-            P("dp", "tensor", None, None),
+            P(WORKERS, "tensor", None, None),
             P("tensor", None),
-            P("dp", "tensor", None),
-            P("tensor", "dp", None),
-            P("tensor", "dp", None),
-            P("tensor", "dp", None),
-            P("dp", "tensor", None, None),
-            P("dp", "tensor", None),
+            P(WORKERS, "tensor", None),
+            P("tensor", WORKERS, None),
+            P("tensor", WORKERS, None),
+            P("tensor", WORKERS, None),
+            P(WORKERS, "tensor", None, None),
+            P(WORKERS, "tensor", None),
         ),
         out_specs=(
-            P("tensor", "dp", None),
-            P("tensor", "dp", None),
-            P("tensor", "dp", None),
-            P("dp", "tensor", None, None, None),
+            P("tensor", WORKERS, None),
+            P("tensor", WORKERS, None),
+            P("tensor", WORKERS, None),
+            P(WORKERS, "tensor", None, None, None),
         ),
         check_vma=False,
     )

time: 251 us -> 214 us (0.85); the launches traced: 247 us -> 214 us
  waiting for transfers between devices: 192 us -> 63.1 us
  blocking collectives: 0 us -> 96.2 us
  between operations: 0.86 us -> 14.2 us
  starting transfers between devices: 18 us -> 5.06 us
    all_to_all x1 -> x0, waiting for transfers between devices: 188 us -> none  [per_device(): lax.all_to_all(terms, 'dp', split_axis=0, concat_axis=0, tiled=True)]
    all_to_all x0 -> x1, blocking collectives: none -> 96.2 us  [per_device(): lax.all_to_all(terms, 'wx', split_axis=0, concat_axis=0, tiled=True)]
    reduce_scatter x0 -> x1, waiting for transfers between devices: none -> 58.7 us  [per_device(): summed = lax.psum_scatter(partial, 'wz', scatter_dimension=0, tiled=True)]
    all_to_all x1 -> x0, starting transfers between devices: 12.1 us -> none  [per_device(): lax.all_to_all(terms, 'dp', split_axis=0, concat_axis=0, tiled=True)]
where the time goes in v2:
time: 214 us
  blocking collectives  96.2 us (45%)
  waiting for transfers between devices  63.1 us (29%)
  Pallas kernels  19 us (9%)
  between operations  14.2 us (7%)
  other arithmetic  12.4 us (6%)
  starting transfers between devices  5.06 us (2%)
  local copies, waits for them, and re-layouts  2.9 us (1%)
    all_to_all x1, blocking collectives, per_device(): lax.all_to_all(terms, 'wx', split_axis=0, concat_axis=0, tiled=True)  96.2 us
    reduce_scatter x1, waiting for transfers between devices, per_device(): summed = lax.psum_scatter(partial, 'wz', scatter_dimension=0, tiled=True)  58.7 us
    pallas_call x1, Pallas kernels, decoded_terms(): pl.pallas_call(code_kernel, grid=(rows // ROW_TILE,), in_specs=[pl.BlockS...  19 us
    all_to_all x1, starting transfers between devices, per_device(): lax.all_to_all(chosen_pieces, 'tensor', split_axis=0, concat_axis=0, tile...  5.02 us
    all_to_all x1, waiting for transfers between devices, per_device(): lax.all_to_all(chosen_pieces, 'tensor', split_axis=0, concat_axis=0, tile...  4.37 us
  transfers between devices with their start and end apart: 2, of which 2 were waited for; matrix products, arithmetic and copies ran while one was open for 1% of the time, Pallas kernels for 0%

profile of v2, /device:TPU:1, one launch (start us, length us, event | category | flops | bytes accessed | tf_op | source)
XLA Modules:
  0.0 214.1 jit_solution(10907870483367299616)
XLA Ops:
  7.2 0.0 reduce-scatter.2.cloned.1.call-start
  7.2 0.1 subtract_convert_fusion
  7.3 0.7 fusion.41
  8.0 0.2 copy.18.dn_ref
  8.2 0.0 copy-start
  8.2 1.0 divide_multiply_fusion.up_ref
  9.2 0.7 add_convert_fusion
  10.0 1.7 multiply_convert_fusion.w_ref
  11.6 0.0 copy-done
  11.6 19.0 %shard_map.111 = bf16[1024,4096]{1,0:T(8,128)(2,1)} custom-call(bf16[1024,4096]{1,0:T(8,128)(2,1)} %bitcast.52, bf16[32,128,128]{2,1,0:T(8,128)(2,1)} %multiply_convert_fusion.w_ref, f32[1024,1]{1,0:T(8,128)} %divide_multiply_fusion.up_ref, f32[1024,1]{1,0:T(8,128)} %copy-done), custom_call_target="tpu_custom_call" | custom-call | flops 1107296256 | bytes 16777216 | tf_op jit(solution)/shard_map/pallas_call | solution.py:91
  30.7 96.2 %all_to_all.14 = bf16[4,256,4096]{2,1,0:T(8,128)(2,1)S(1)} all-to-all(bf16[4,256,4096]{2,1,0:T(8,128)(2,1)} %bitcast.51), channel_id=1, replica_groups=mesh['wx'=4,'wz'=8,'tensor'=8] {'wx'}, dimensions={0} | all-to-all | bytes 16777216 | tf_op jit(solution)/shard_map/all_to_all | solution.py:128
  126.8 0.0 copy-start.4
  126.8 0.0 copy-start.1
  126.8 0.0 copy-start.5
  126.8 0.0 copy-start.6
  126.8 0.0 copy-start.2
  126.8 0.0 copy-start.3
  126.9 3.5 %convert_reduce_fusion = f32[256,4096]{1,0:T(8,128)} fusion(bf16[4,256,4096]{2,1,0:T(8,128)(2,1)S(1)} %all_to_all.14), kind=kLoop, calls=%fused_computation.1 | loop fusion | flops 7340032 | bytes 12582912 | tf_op jit(solution)/shard_map/reduce_sum | solution.py:129
  130.4 0.0 reduce-scatter.2.cloned.1.call-update
  130.4 0.0 copy-done.4
  130.4 0.1 fusion.54
  130.5 0.0 copy-done.1
  130.5 0.3 copy.23
  130.8 0.0 copy-done.5
  130.9 0.1 reshape.365
  130.9 0.0 copy-done.6
  130.9 0.1 iota_compare_fusion
  131.0 58.7 %reduce-scatter.2.cloned.1.call-done = f32[32,4096]{1,0:T(8,128)} async-done(((f32[256,4096]{1,0:T(8,128)}), f32[32,4096]{1,0:T(8,128)}) %reduce-scatter.2.cloned.1.call-update) | async-done | bytes 524304 | tf_op jit(solution)/shard_map/reduce_scatter | solution.py:130
  189.7 0.0 copy-done.2
  189.8 0.0 copy-done.3
  189.8 2.3 %divide_bitcast_fusion = (f32[4,8,32,128]{3,1,2,0:T(8,128)S(1)}, f32[1,32,4096]{2,1,0:T(8,128)}, f32[1,32,4096]{2,1,0:T(8,128)}) fusion(f32[32,4096]{1,0:T(8,128)} %reduce-scatter.2.cloned.1.call-done, f32[1,32,4096]{2,1,0:T(8,128)S(1)} %copy-done.2, f32[1,32,4096]{2,1,0:T(8,128)S(1)} %copy-done.3), kind=kLoop, calls=%fused_computation.11 | loop fusion | flops 1572864 | bytes 3145728
  192.1 0.1 copy.22
  192.2 0.6 fusion.5
  192.8 0.6 convolution_bitcast_fusion
  193.4 0.1 reshape.360
  193.5 0.1 reshape.359
  193.6 0.6 fusion.2
  194.2 1.3 gather_fusion
  195.5 0.8 select_select_fusion
  196.3 5.0 %all-to-all-start.1 = ((bf16[8,16,512]{2,1,0:T(8,128)(2,1)}), bf16[8,16,512]{2,1,0:T(8,128)(2,1)S(1)}, u32[]{:S(2)}, u32[]{:S(2)}) async-start(bf16[8,16,512]{2,1,0:T(8,128)(2,1)} %select_select_fusion), calls=%async_computation.2 | async-start | bytes 262144 | tf_op jit(solution)/shard_map/all_to_all | solution.py:144
  201.3 0.9 multiply_subtract_fusion
  202.2 4.4 %all-to-all-done.1 = bf16[8,16,512]{2,1,0:T(8,128)(2,1)S(1)} async-done(((bf16[8,16,512]{2,1,0:T(8,128)(2,1)}), bf16[8,16,512]{2,1,0:T(8,128)(2,1)S(1)}, u32[]{:S(2)}, u32[]{:S(2)}) %all-to-all-start.1) | async-done | bytes 131104 | tf_op jit(solution)/shard_map/all_to_all | solution.py:144
  206.6 0.7 copy.37
  (2 shorter events, 0.0 us)
Async XLA Ops:
  7.2 182.6 %reduce-scatter.2.cloned.1.call-start = ((), (), s32[]{:S(2)}) async-start(), calls=%async_computation.3 | async-start | bytes 4718592 | tf_op jit(solution)/shard_map/reduce_scatter | solution.py:130
  8.2 3.4 %copy-start = (f32[1024,1]{1,0:T(8,128)}, f32[1024,1]{1,0:T(8,128)S(1)}, u32[]{:S(2)}) copy-start(f32[1024,1]{1,0:T(8,128)S(1)} %copy.18.dn_ref) | copy-start | bytes 12292
  126.8 3.6 %copy-start.4 = (s32[1,4096]{1,0:T(1,128)S(1)}, s32[1,4096]{1,0:T(1,128)}, u32[]{:S(2)}) copy-start(s32[1,4096]{1,0:T(1,128)} %param.9) | copy-start | bytes 49156
  126.8 3.7 %copy-start.1 = (f32[1,32,4096]{2,1,0:T(8,128)S(1)}, f32[1,32,4096]{2,1,0:T(8,128)}, u32[]{:S(2)}) copy-start(f32[1,32,4096]{2,1,0:T(8,128)} %param.13) | copy-start | bytes 1572868
  126.8 4.0 %copy-start.5 = (s32[1,1,8,16]{3,2,1,0:T(8,128)S(1)}, s32[1,1,8,16]{3,2,1,0:T(8,128)}, u32[]{:S(2)}) copy-start(s32[1,1,8,16]{3,2,1,0:T(8,128)} %param.14) | copy-start | bytes 1540
  126.8 4.1 %copy-start.6 = (s32[1,1,8]{2,1,0:T(1,128)S(1)}, s32[1,1,8]{2,1,0:T(1,128)}, u32[]{:S(2)}) copy-start(s32[1,1,8]{2,1,0:T(1,128)} %param.15) | copy-start | bytes 100
  126.8 62.9 %copy-start.2 = (f32[1,32,4096]{2,1,0:T(8,128)S(1)}, f32[1,32,4096]{2,1,0:T(8,128)}, u32[]{:S(2)}) copy-start(f32[1,32,4096]{2,1,0:T(8,128)} %param.11) | copy-start | bytes 1572868
  126.8 62.9 %copy-start.3 = (f32[1,32,4096]{2,1,0:T(8,128)S(1)}, f32[1,32,4096]{2,1,0:T(8,128)}, u32[]{:S(2)}) copy-start(f32[1,32,4096]{2,1,0:T(8,128)} %param.12) | copy-start | bytes 1572868
  196.3 10.3 %all-to-all-start.1 = ((bf16[8,16,512]{2,1,0:T(8,128)(2,1)}), bf16[8,16,512]{2,1,0:T(8,128)(2,1)S(1)}, u32[]{:S(2)}, u32[]{:S(2)}) async-start(bf16[8,16,512]{2,1,0:T(8,128)(2,1)} %select_select_fusion), calls=%async_computation.2 | async-start | bytes 262144 | tf_op jit(solution)/shard_map/all_to_all | solution.py:144
Sparse Core Ops, SparseCore 0:
  130.5 59.1 reduce-scatter.1

commit v3 on v2

--- a/solution.py
+++ b/solution.py
@@ -12,6 +12,7 @@
 HB = 128
 ROW_TILE = 256
 X_CHIPS = 4
+PARTS = 2
 WORKERS = ("wx", "wz")
 
 
@@ -69,43 +70,49 @@
 
 
 def code_kernel(x_ref, w_ref, up_ref, dn_ref, o_ref, y_ref):
+    groups, group_rows, _ = x_ref.shape
     for a in range(HA):
         cols = slice(a * HB, (a + 1) * HB)
-        y_ref[:, cols] = jnp.dot(x_ref[:, cols], w_ref[a], preferred_element_type=jnp.float32)
+        lhs = x_ref[:, :, cols].reshape(groups * group_rows, HB)
+        y_ref[:, cols] = jnp.dot(lhs, w_ref[a], preferred_element_type=jnp.float32)
 
     def row_group(g, carry):
         rows = pl.ds(pl.multiple_of(g * 8, 8), 8)
+        dest = g // (group_rows // 8)
+        within = pl.ds(pl.multiple_of((g % (group_rows // 8)) * 8, 8), 8)
         blocks = butterfly([y_ref[rows, a * HB:(a + 1) * HB] for a in range(HA)])
-        up = up_ref[rows, :]
-        dn = dn_ref[rows, :]
+        up = up_ref[dest, within, :]
+        dn = dn_ref[dest, within, :]
         for a in range(HA):
             coded = jnp.clip(blocks[a] * up, -127.0, 127.0).astype(jnp.bfloat16)
             o_ref[rows, a * HB:(a + 1) * HB] = (coded.astype(jnp.float32) * dn).astype(o_ref.dtype)
         return carry
 
-    lax.fori_loop(0, x_ref.shape[0] // 8, row_group, 0)
+    lax.fori_loop(0, groups * group_rows // 8, row_group, 0)
 
 
-def decoded_terms(grad_rows, signed_walsh, up_scale, down_scale):
-    rows, width = grad_rows.shape
+def decoded_terms(grad_groups, signed_walsh, up_scale, down_scale, part, x_size):
+    dests, _, part_rows, width = grad_groups.shape
+    per_x = dests // x_size
+    tile = lambda i: (i, part, 0, 0)
     return pl.pallas_call(
         code_kernel,
-        grid=(rows // ROW_TILE,),
+        grid=(x_size,),
         in_specs=[
-            pl.BlockSpec((ROW_TILE, width), lambda i: (i, 0)),
+            pl.BlockSpec((per_x, None, part_rows, width), tile),
             pl.BlockSpec((HA, HB, HB), lambda i: (0, 0, 0)),
-            pl.BlockSpec((ROW_TILE, 1), lambda i: (i, 0)),
-            pl.BlockSpec((ROW_TILE, 1), lambda i: (i, 0)),
+            pl.BlockSpec((per_x, None, part_rows, 1), tile),
+            pl.BlockSpec((per_x, None, part_rows, 1), tile),
         ],
-        out_specs=pl.BlockSpec((ROW_TILE, width), lambda i: (i, 0)),
-        out_shape=jax.ShapeDtypeStruct((rows, width), jnp.bfloat16),
-        scratch_shapes=[pltpu.VMEM((ROW_TILE, width), jnp.float32)],
+        out_specs=pl.BlockSpec((None, per_x * part_rows, width), lambda i: (i, 0, 0)),
+        out_shape=jax.ShapeDtypeStruct((x_size, per_x * part_rows, width), jnp.bfloat16),
+        scratch_shapes=[pltpu.VMEM((per_x * part_rows, width), jnp.float32)],
         cost_estimate=pl.CostEstimate(
-            flops=2 * rows * width * HB + 8 * rows * width,
+            flops=2 * dests * part_rows * width * HB + 8 * dests * part_rows * width,
             transcendentals=0,
-            bytes_accessed=rows * width * 4,
+            bytes_accessed=dests * part_rows * width * 4,
         ),
-    )(grad_rows, signed_walsh, up_scale, down_scale)
+    )(grad_groups, signed_walsh, up_scale, down_scale)
 
 
 def select_pieces(slab_view, slot_lists, used_counts):
@@ -122,12 +129,20 @@
     signed_walsh = (sign_vec.reshape(HA, HB, 1) * walsh_table(HB)[None]).astype(jnp.bfloat16)
     unit_scale = half_power(shift_rows)[:, None]
     up_scale = (1.0 / unit_scale) / math.sqrt(HA * HB)
-    terms = decoded_terms(grad_rows, signed_walsh, up_scale, unit_scale)
     x_size = lax.axis_size("wx")
-    workers = x_size * lax.axis_size("wz")
-    arrived_terms = lax.all_to_all(terms, "wx", split_axis=0, concat_axis=0, tiled=True)
-    partial = arrived_terms.reshape(x_size, grad_rows.shape[0] // x_size, -1).astype(jnp.float32).sum(0)
-    summed = lax.psum_scatter(partial, "wz", scatter_dimension=0, tiled=True)
+    dests = x_size * lax.axis_size("wz")
+    workers = dests
+    part_rows = blocks // PARTS
+    as_groups = lambda rows: rows.reshape(dests, PARTS, part_rows, rows.shape[-1])
+    grad_groups = as_groups(grad_rows)
+    up_groups, down_groups = as_groups(up_scale), as_groups(unit_scale)
+    pieces = []
+    for part in range(PARTS):
+        terms = decoded_terms(grad_groups, signed_walsh, up_groups, down_groups, part, x_size)
+        arrived_terms = lax.all_to_all(terms, "wx", split_axis=0, concat_axis=0, tiled=True)
+        partial = arrived_terms.astype(jnp.float32).sum(0)
+        pieces.append(lax.psum_scatter(partial, "wz", scatter_dimension=0, tiled=True))
+    summed = jnp.concatenate(pieces, 0)
     mean_grad = summed / workers
     new_first = first_keep * first[0] + first_take * mean_grad
     new_second = second_keep * second[0] + second_take * mean_grad * mean_grad

time: 214 us -> 213 us (level)
  waiting for transfers between devices: 63.1 us -> 48.5 us
  blocking collectives: 96.2 us -> 101 us
  starting transfers between devices: 5.06 us -> 9.35 us
  Pallas kernels: 19 us -> 22 us
    reduce_scatter x1 -> x2, waiting for transfers between devices: 58.7 us -> 44.1 us  [per_device(): lax.psum_scatter(partial, 'wz', scatter_dimension=0, tiled=True)]
    all_to_all x1 -> x2, blocking collectives: 96.2 us -> 101 us  [per_device(): lax.all_to_all(terms, 'wx', split_axis=0, concat_axis=0, tiled=True)]
    all_to_all x1, starting transfers between devices: 5.02 us -> 9.27 us  [per_device(): lax.all_to_all(chosen_pieces, 'tensor', split_axis=0, concat_axis=0, tile...]
    pallas_call x1 -> x2, Pallas kernels: 19 us -> 22 us  [decoded_terms(): pl.pallas_call(code_kernel, grid=(x_size,), in_specs=[pl.BlockSpec((per_x...]
  transfers between devices with their start and end apart: 2 -> 3, of which waited for: 2 -> 2; matrix products, arithmetic and copies ran while one was open for 1% -> 2% of each run, Pallas kernels for 0% -> 5%
where the time goes in v3:
time: 213 us; the launch traced here: 212 us
  blocking collectives  101 us (47%)
  waiting for transfers between devices  48.5 us (23%)
  Pallas kernels  22 us (10%)
  between operations  14.2 us (7%)
  other arithmetic  13.2 us (6%)
  starting transfers between devices  9.35 us (4%)
  local copies, waits for them, and re-layouts  3.26 us (2%)
    all_to_all x2, blocking collectives, per_device(): lax.all_to_all(terms, 'wx', split_axis=0, concat_axis=0, tiled=True)  101 us
    reduce_scatter x2, waiting for transfers between devices, per_device(): lax.psum_scatter(partial, 'wz', scatter_dimension=0, tiled=True)  44.1 us
    pallas_call x2, Pallas kernels, decoded_terms(): pl.pallas_call(code_kernel, grid=(x_size,), in_specs=[pl.BlockSpec((per_x...  22 us
    all_to_all x1, starting transfers between devices, per_device(): lax.all_to_all(chosen_pieces, 'tensor', split_axis=0, concat_axis=0, tile...  9.27 us
    all_to_all x1, waiting for transfers between devices, per_device(): lax.all_to_all(chosen_pieces, 'tensor', split_axis=0, concat_axis=0, tile...  4.38 us
  transfers between devices with their start and end apart: 3, of which 2 were waited for; matrix products, arithmetic and copies ran while one was open for 2% of the time, Pallas kernels for 5%

profile of v3, /device:TPU:1, one launch (start us, length us, event | category | flops | bytes accessed | tf_op | source)
XLA Modules:
  0.0 212.4 jit_solution(1866879554887224449)
XLA Ops:
  7.2 0.0 reduce-scatter.3.cloned.1.call-start
  7.2 0.1 subtract_convert_fusion
  7.3 0.7 fusion.44
  8.0 0.3 reshape.460.dn_ref
  8.4 0.0 copy-start
  8.4 0.9 divide_multiply_fusion.up_ref
  9.3 0.7 add_convert_fusion
  10.0 1.6 multiply_convert_fusion.w_ref
  11.7 0.0 copy-done
  11.7 11.0 %shard_map.111 = bf16[4,128,4096]{2,1,0:T(8,128)(2,1)} custom-call(bf16[32,2,16,4096]{3,2,1,0:T(8,128)(2,1)} %bitcast.57, bf16[32,128,128]{2,1,0:T(8,128)(2,1)} %multiply_convert_fusion.w_ref, f32[32,2,16,1]{3,2,1,0:T(8,128)} %divide_multiply_fusion.up_ref, f32[32,2,16,1]{3,2,1,0:T(8,128)} %copy-done), custom_call_target="tpu_custom_call" | custom-call | flops 553648128 | bytes 8388608 | tf_op jit(solution)/shard_map/pallas_call | solution.py:98
  22.6 51.3 %all_to_all.15 = bf16[4,128,4096]{2,1,0:T(8,128)(2,1)S(1)} all-to-all(bf16[4,128,4096]{2,1,0:T(8,128)(2,1)} %shard_map.111), channel_id=1, replica_groups=mesh['wx'=4,'wz'=8,'tensor'=8] {'wx'}, dimensions={0} | all-to-all | bytes 8388608 | tf_op jit(solution)/shard_map/all_to_all | solution.py:142
  73.9 2.1 convert_reduce_fusion.1
  76.0 0.0 reduce-scatter.3.cloned.1.call-update
  76.1 0.0 reduce-scatter.5.cloned.1.call-start
  76.1 11.0 %shard_map.112 = bf16[4,128,4096]{2,1,0:T(8,128)(2,1)} custom-call(bf16[32,2,16,4096]{3,2,1,0:T(8,128)(2,1)} %bitcast.58, bf16[32,128,128]{2,1,0:T(8,128)(2,1)} %multiply_convert_fusion.w_ref, f32[32,2,16,1]{3,2,1,0:T(8,128)} %divide_multiply_fusion.up_ref, f32[32,2,16,1]{3,2,1,0:T(8,128)} %copy-done), custom_call_target="tpu_custom_call" | custom-call | flops 553648128 | bytes 8388608 | tf_op jit(solution)/shard_map/pallas_call | solution.py:98
  87.1 49.4 %all_to_all.16 = bf16[4,128,4096]{2,1,0:T(8,128)(2,1)S(1)} all-to-all(bf16[4,128,4096]{2,1,0:T(8,128)(2,1)} %shard_map.112), channel_id=1, replica_groups=mesh['wx'=4,'wz'=8,'tensor'=8] {'wx'}, dimensions={0} | all-to-all | bytes 8388608 | tf_op jit(solution)/shard_map/all_to_all | solution.py:142
  136.5 0.0 copy-start.4
  136.5 0.0 copy-start.5
  136.5 2.1 convert_reduce_fusion
  138.6 0.0 reduce-scatter.5.cloned.1.call-update
  138.7 0.0 copy-done.6
  138.7 0.1 fusion.57
  138.8 0.0 copy-done.1
  138.8 0.3 copy.28
  139.1 0.0 copy-done.7
  139.1 0.1 reshape.452
  139.2 0.0 copy-done.8
  139.2 0.1 iota_compare_fusion
  139.3 44.1 %reduce-scatter.5.cloned.1.call-done = f32[16,4096]{1,0:T(8,128)} async-done(((f32[128,4096]{1,0:T(8,128)}), f32[16,4096]{1,0:T(8,128)}) %reduce-scatter.5.cloned.1.call-update) | async-done | bytes 262160 | tf_op jit(solution)/shard_map/reduce_scatter | solution.py:144
  183.4 0.0 copy-done.4
  183.4 2.2 %multiply_bitcast_fusion.1 = (f32[4,8,32,128]{3,1,2,0:T(8,128)S(1)}, f32[1,32,4096]{2,1,0:T(8,128)}, f32[1,32,4096]{2,1,0:T(8,128)}, f32[4,8,32,128]{3,1,2,0:T(8,128)S(1)}) fusion(f32[1,32,4096]{2,1,0:T(8,128)S(1)} %copy-done.4, f32[1,16,4096]{2,1,0:T(8,128)} %bitcast.63, f32[1,16,4096]{2,1,0:T(8,128)} %bitcast.61, f32[1,32,4096]{2,1,0:T(8,128)S(1)} %copy-done.5), kind=kLoop, calls=%fused_computation.22 | loop fusion | flops 1179648 | bytes 3670016
  185.6 0.1 copy.24
  185.7 0.1 copy.27
  185.8 0.0 copy-done.2
  185.8 0.1 copy.25
  185.9 0.1 copy.26
  186.0 0.3 fusion.3
  186.3 0.6 fusion.8
  186.9 0.6 convolution_bitcast_fusion
  187.5 0.1 reshape.447
  187.6 0.1 reshape.446
  187.7 0.6 fusion.7
  188.3 1.3 gather_fusion
  189.7 0.8 select_select_fusion
  190.4 9.3 %all-to-all-start.2 = ((bf16[8,16,512]{2,1,0:T(8,128)(2,1)}), bf16[8,16,512]{2,1,0:T(8,128)(2,1)S(1)}, u32[]{:S(2)}, u32[]{:S(2)}) async-start(bf16[8,16,512]{2,1,0:T(8,128)(2,1)} %select_select_fusion), calls=%async_computation.4 | async-start | bytes 262144 | tf_op jit(solution)/shard_map/all_to_all | solution.py:159
  199.7 0.9 multiply_subtract_fusion
  200.6 4.4 %all-to-all-done.2 = bf16[8,16,512]{2,1,0:T(8,128)(2,1)S(1)} async-done(((bf16[8,16,512]{2,1,0:T(8,128)(2,1)}), bf16[8,16,512]{2,1,0:T(8,128)(2,1)S(1)}, u32[]{:S(2)}, u32[]{:S(2)}) %all-to-all-start.2) | async-done | bytes 131104 | tf_op jit(solution)/shard_map/all_to_all | solution.py:159
  204.9 0.7 copy.43
  (13 shorter events, 0.1 us)
Async XLA Ops:
  7.2 132.1 %reduce-scatter.3.cloned.1.call-start = ((), (), s32[]{:S(2)}) async-start(), calls=%async_computation.5 | async-start | bytes 2359296 | tf_op jit(solution)/shard_map/reduce_scatter | solution.py:144
  8.4 3.3 %copy-start = (f32[32,2,16,1]{3,2,1,0:T(8,128)}, f32[32,2,16,1]{3,2,1,0:T(8,128)S(1)}, u32[]{:S(2)}) copy-start(f32[32,2,16,1]{3,2,1,0:T(8,128)S(1)} %reshape.460.dn_ref) | copy-start | bytes 12292
  76.1 107.3 %reduce-scatter.5.cloned.1.call-start = ((), (), s32[]{:S(2)}) async-start(), calls=%async_computation.6 | async-start | bytes 2359296 | tf_op jit(solution)/shard_map/reduce_scatter | solution.py:144
  136.5 2.2 %copy-start.6 = (s32[1,4096]{1,0:T(1,128)S(1)}, s32[1,4096]{1,0:T(1,128)}, u32[]{:S(2)}) copy-start(s32[1,4096]{1,0:T(1,128)} %param.9) | copy-start | bytes 49156
  136.5 2.3 %copy-start.1 = (f32[1,32,4096]{2,1,0:T(8,128)S(1)}, f32[1,32,4096]{2,1,0:T(8,128)}, u32[]{:S(2)}) copy-start(f32[1,32,4096]{2,1,0:T(8,128)} %param.13) | copy-start | bytes 1572868
  136.5 2.6 %copy-start.7 = (s32[1,1,8,16]{3,2,1,0:T(8,128)S(1)}, s32[1,1,8,16]{3,2,1,0:T(8,128)}, u32[]{:S(2)}) copy-start(s32[1,1,8,16]{3,2,1,0:T(8,128)} %param.14) | copy-start | bytes 1540
  136.5 2.7 %copy-start.8 = (s32[1,1,8]{2,1,0:T(1,128)S(1)}, s32[1,1,8]{2,1,0:T(1,128)}, u32[]{:S(2)}) copy-start(s32[1,1,8]{2,1,0:T(1,128)} %param.15) | copy-start | bytes 100
  136.5 46.9 %copy-start.4 = (f32[1,32,4096]{2,1,0:T(8,128)S(1)}, f32[1,32,4096]{2,1,0:T(8,128)}, u32[]{:S(2)}) copy-start(f32[1,32,4096]{2,1,0:T(8,128)} %param.11) | copy-start | bytes 1572868
  136.5 46.9 %copy-start.5 = (f32[1,32,4096]{2,1,0:T(8,128)S(1)}, f32[1,32,4096]{2,1,0:T(8,128)}, u32[]{:S(2)}) copy-start(f32[1,32,4096]{2,1,0:T(8,128)} %param.12) | copy-start | bytes 1572868
  139.3 46.5 %copy-start.2 = (f32[16,4096]{1,0:T(8,128)S(1)}, f32[16,4096]{1,0:T(8,128)}, u32[]{:S(2)}) copy-start(f32[16,4096]{1,0:T(8,128)} %reduce-scatter.3.cloned.1.call-done) | copy-start | bytes 786436
  183.4 2.5 %copy-start.3 = (f32[16,4096]{1,0:T(8,128)S(1)}, f32[16,4096]{1,0:T(8,128)}, u32[]{:S(2)}) copy-start(f32[16,4096]{1,0:T(8,128)} %reduce-scatter.5.cloned.1.call-done) | copy-start | bytes 786436
  190.4 14.5 %all-to-all-start.2 = ((bf16[8,16,512]{2,1,0:T(8,128)(2,1)}), bf16[8,16,512]{2,1,0:T(8,128)(2,1)S(1)}, u32[]{:S(2)}, u32[]{:S(2)}) async-start(bf16[8,16,512]{2,1,0:T(8,128)(2,1)} %select_select_fusion), calls=%async_computation.4 | async-start | bytes 262144 | tf_op jit(solution)/shard_map/all_to_all | solution.py:159
Sparse Core Ops, SparseCore 0:
  76.2 42.2 reduce-scatter.2
  138.8 44.5 reduce-scatter.4

commit v4 on v3

--- a/solution.py
+++ b/solution.py
@@ -115,6 +115,23 @@
     )(grad_groups, signed_walsh, up_scale, down_scale)
 
 
+def send_along_x(terms, x_size):
+    my_x = lax.axis_index("wx")
+    arrived = [lax.dynamic_index_in_dim(terms, my_x, 0, keepdims=False)]
+    for step in range(1, x_size):
+        outgoing = lax.dynamic_index_in_dim(terms, (my_x + step) % x_size, 0, keepdims=False)
+        pairs = [(i, (i + step) % x_size) for i in range(x_size)]
+        arrived.append(lax.ppermute(outgoing, "wx", pairs))
+    return arrived
+
+
+def sum_arrived(arrived):
+    partial = arrived[0].astype(jnp.float32)
+    for piece in arrived[1:]:
+        partial = partial + piece.astype(jnp.float32)
+    return partial
+
+
 def select_pieces(slab_view, slot_lists, used_counts):
     gathered = jnp.take_along_axis(slab_view, slot_lists[:, :, None], axis=1)
     live_slots = lax.broadcasted_iota(jnp.int32, slot_lists.shape, 1) < used_counts[:, None]
@@ -137,11 +154,16 @@
     grad_groups = as_groups(grad_rows)
     up_groups, down_groups = as_groups(up_scale), as_groups(unit_scale)
     pieces = []
-    for part in range(PARTS):
-        terms = decoded_terms(grad_groups, signed_walsh, up_groups, down_groups, part, x_size)
-        arrived_terms = lax.all_to_all(terms, "wx", split_axis=0, concat_axis=0, tiled=True)
-        partial = arrived_terms.astype(jnp.float32).sum(0)
+    terms = decoded_terms(grad_groups, signed_walsh, up_groups, down_groups, 0, x_size)
+    arrived = send_along_x(terms, x_size)
+    for part in range(1, PARTS + 1):
+        if part < PARTS:
+            terms = decoded_terms(grad_groups, signed_walsh, up_groups, down_groups, part, x_size)
+            arrived, terms = lax.optimization_barrier((arrived, terms))
+        partial = sum_arrived(arrived)
         pieces.append(lax.psum_scatter(partial, "wz", scatter_dimension=0, tiled=True))
+        if part < PARTS:
+            arrived = send_along_x(terms, x_size)
     summed = jnp.concatenate(pieces, 0)
     mean_grad = summed / workers
     new_first = first_keep * first[0] + first_take * mean_grad

time: 213 us -> 206 us (0.967)
  blocking collectives: 101 us -> 0 us
  waiting for transfers between devices: 48.5 us -> 121 us
  starting transfers between devices: 9.35 us -> 19.3 us
  local copies, waits for them, and re-layouts: 3.26 us -> 11.8 us
  other arithmetic: 13.2 us -> 15.9 us
    all_to_all x2 -> x0, blocking collectives: 101 us -> none  [per_device(): lax.all_to_all(terms, 'wx', split_axis=0, concat_axis=0, tiled=True)]
    ppermute x0 -> x6, waiting for transfers between devices: none -> 78.2 us  [send_along_x(): arrived.append(lax.ppermute(outgoing, 'wx', pairs))]
    ppermute x0 -> x6, starting transfers between devices: none -> 9.73 us  [send_along_x(): arrived.append(lax.ppermute(outgoing, 'wx', pairs))]
    add x0 -> x2, other arithmetic: none -> 7.01 us  [sum_arrived(): partial = partial + piece.astype(jnp.float32)]
    squeeze x0 -> x2, local copies, waits for them, and re-layouts: none -> 5.75 us  [send_along_x(): lax.dynamic_index_in_dim(terms, (my_x + step) % x_size, 0, keepdims=False)]
    reduce_scatter x2, waiting for transfers between devices: 44.1 us -> 38.6 us  [per_device(): lax.psum_scatter(partial, 'wz', scatter_dimension=0, tiled=True)]
    reduce_sum x2 -> x0, other arithmetic: 4.2 us -> none  [per_device(): partial = arrived_terms.astype(jnp.float32).sum(0)]
    unnamed x25 -> x21, local copies, waits for them, and re-layouts: 1.32 us -> 4.13 us
  transfers between devices with their start and end apart: 3 -> 9, of which waited for: 2 -> 6; matrix products, arithmetic and copies ran while one was open for 2% -> 4% of each run, Pallas kernels for 5% -> 5%
where the time goes in v4:
time: 206 us
  waiting for transfers between devices  121 us (59%)
  Pallas kernels  22 us (11%)
  starting transfers between devices  19.3 us (9%)
  other arithmetic  15.9 us (8%)
  between operations  14.3 us (7%)
  local copies, waits for them, and re-layouts  11.8 us (6%)
    ppermute x6, waiting for transfers between devices, send_along_x(): arrived.append(lax.ppermute(outgoing, 'wx', pairs))  78.2 us
    reduce_scatter x2, waiting for transfers between devices, per_device(): lax.psum_scatter(partial, 'wz', scatter_dimension=0, tiled=True)  38.6 us
    pallas_call x2, Pallas kernels, decoded_terms(): pl.pallas_call(code_kernel, grid=(x_size,), in_specs=[pl.BlockSpec((per_x...  22 us
    ppermute x6, starting transfers between devices, send_along_x(): arrived.append(lax.ppermute(outgoing, 'wx', pairs))  9.73 us
    all_to_all x1, starting transfers between devices, per_device(): lax.all_to_all(chosen_pieces, 'tensor', split_axis=0, concat_axis=0, tile...  9.5 us
    add x2, other arithmetic, sum_arrived(): partial = partial + piece.astype(jnp.float32)  7.01 us
    squeeze x2, local copies, waits for them, and re-layouts, send_along_x(): lax.dynamic_index_in_dim(terms, (my_x + step) % x_size, 0, keepdims=False)  5.75 us
    all_to_all x1, waiting for transfers between devices, per_device(): lax.all_to_all(chosen_pieces, 'tensor', split_axis=0, concat_axis=0, tile...  4.38 us
  transfers between devices with their start and end apart: 9, of which 6 were waited for; matrix products, arithmetic and copies ran while one was open for 4% of the time, Pallas kernels for 5%

profile of v4, /device:TPU:1, one launch (start us, length us, event | category | flops | bytes accessed | tf_op | source)
XLA Modules:
  0.0 205.8 jit_solution(13713408355124073461)
XLA Ops:
  7.2 0.0 reduce-scatter.3.cloned.1.call-start
  7.3 0.1 subtract_convert_fusion
  7.3 0.7 fusion.46
  8.1 0.3 reshape.463.dn_ref
  8.4 0.9 divide_multiply_fusion.up_ref
  9.3 0.7 add_convert_fusion
  10.1 1.6 multiply_convert_fusion.w_ref
  11.7 11.0 %shard_map.111 = bf16[4,128,4096]{2,1,0:T(8,128)(2,1)} custom-call(bf16[32,2,16,4096]{3,2,1,0:T(8,128)(2,1)} %bitcast.74, bf16[32,128,128]{2,1,0:T(8,128)(2,1)} %multiply_convert_fusion.w_ref, f32[32,2,16,1]{3,2,1,0:T(8,128)} %divide_multiply_fusion.up_ref, f32[32,2,16,1]{3,2,1,0:T(8,128)} %copy-done), custom_call_target="tpu_custom_call" | custom-call | flops 553648128 | bytes 8388608 | tf_op jit(solution)/shard_map/pallas_call | solution.py:98
  22.7 3.5 %dynamic-slice_bitcast_fusion.3 = (bf16[128,4096]{1,0:T(8,128)(2,1)S(1)}, bf16[128,4096]{1,0:T(8,128)(2,1)S(1)}, bf16[128,4096]{1,0:T(8,128)(2,1)}, bf16[128,4096]{1,0:T(8,128)(2,1)S(1)}) fusion(bf16[4,128,4096]{2,1,0:T(8,128)(2,1)} %shard_map.111, s32[]{:T(128)S(6)} %select_n.169, s32[]{:T(128)S(6)} %select_n.167, s32[]{:T(128)S(6)} %select_n.165, ...), kind=kLoop, calls=%fused_computation.10 | loop fusion | bytes 8388624 | tf_op jit(solution)/shard_map/jit(dynamic_index_in_dim)/squeeze | solution.py:122
  26.2 2.0 collective-permute-start
  28.2 2.5 %collective-permute-start.1 = (bf16[128,4096]{1,0:T(8,128)(2,1)S(1)}, bf16[128,4096]{1,0:T(8,128)(2,1)}, u32[]{:S(2)}, u32[]{:S(2)}) collective-permute-start(bf16[128,4096]{1,0:T(8,128)(2,1)S(1)} %get-tuple-element.18), channel_id=1, source_target_pairs={{0,128},{64,192},{128,0},{192,64},{1,129},{65,193},{129,1},{193,65... | collective-permute-start | bytes 3145736 | tf_op jit(solution)/shard_map/ppermute | solution.py:124
  30.7 1.2 collective-permute-start.2
  31.9 11.0 %shard_map.112 = bf16[4,128,4096]{2,1,0:T(8,128)(2,1)} custom-call(bf16[32,2,16,4096]{3,2,1,0:T(8,128)(2,1)} %bitcast.75, bf16[32,128,128]{2,1,0:T(8,128)(2,1)} %multiply_convert_fusion.w_ref, f32[32,2,16,1]{3,2,1,0:T(8,128)} %divide_multiply_fusion.up_ref, f32[32,2,16,1]{3,2,1,0:T(8,128)} %copy-done), custom_call_target="tpu_custom_call" | custom-call | flops 553648128 | bytes 8388608 | tf_op jit(solution)/shard_map/pallas_call | solution.py:98
  42.9 7.7 %collective-permute-done = bf16[128,4096]{1,0:T(8,128)(2,1)} collective-permute-done((bf16[128,4096]{1,0:T(8,128)(2,1)}, bf16[128,4096]{1,0:T(8,128)(2,1)}, u32[]{:S(2)}, u32[]{:S(2)}) %collective-permute-start) | collective-permute-done | bytes 1048608 | tf_op jit(solution)/shard_map/ppermute | solution.py:124
  50.5 25.5 %collective-permute-done.1 = bf16[128,4096]{1,0:T(8,128)(2,1)} collective-permute-done((bf16[128,4096]{1,0:T(8,128)(2,1)S(1)}, bf16[128,4096]{1,0:T(8,128)(2,1)}, u32[]{:S(2)}, u32[]{:S(2)}) %collective-permute-start.1) | collective-permute-done | bytes 1048608 | tf_op jit(solution)/shard_map/ppermute | solution.py:124
  76.1 3.8 %convert_add_fusion.1 = f32[128,4096]{1,0:T(8,128)} fusion(bf16[128,4096]{1,0:T(8,128)(2,1)} %collective-permute-done.2, bf16[128,4096]{1,0:T(8,128)(2,1)} %collective-permute-done.1, bf16[128,4096]{1,0:T(8,128)(2,1)} %collective-permute-done, bf16[128,4096]{1,0:T(8,128)(2,1)S(1)} %get-tuple-element.9), kind=kLoop, calls=%fused_computation.4 | loop fusion | flops 3670016 | bytes 6291456 | tf_op jit(solution)/shard_map/add | solution.py:131
  79.9 0.0 reduce-scatter.5.cloned.1.call-start
  80.0 2.2 %dynamic-slice_bitcast_fusion.2 = (bf16[128,4096]{1,0:T(8,128)(2,1)S(1)}, bf16[128,4096]{1,0:T(8,128)(2,1)S(1)}, bf16[128,4096]{1,0:T(8,128)(2,1)S(1)}) fusion(bf16[4,128,4096]{2,1,0:T(8,128)(2,1)} %shard_map.112, s32[]{:T(128)S(6)} %select_n.165, s32[]{:T(128)S(6)} %select_n.169, s32[]{:T(128)S(6)} %select_n.167), kind=kLoop, calls=%fused_computation.9 | loop fusion | bytes 6291468 | tf_op jit(solution)/shard_map/jit(dynamic_index_in_dim)/squeeze | solution.py:122
  82.2 0.9 collective-permute-start.3
  83.1 3.0 %collective-permute-start.4 = (bf16[128,4096]{1,0:T(8,128)(2,1)S(1)}, bf16[128,4096]{1,0:T(8,128)(2,1)S(1)}, u32[]{:S(2)}, u32[]{:S(2)}) collective-permute-start(bf16[128,4096]{1,0:T(8,128)(2,1)S(1)} %get-tuple-element.16), channel_id=1, source_target_pairs={{0,128},{64,192},{128,0},{192,64},{1,129},{65,193},{129,1},{193,65... | collective-permute-start | bytes 3145736 | tf_op jit(solution)/shard_map/ppermute | solution.py:124
  86.1 0.2 collective-permute-start.5
  86.3 20.4 %collective-permute-done.3 = bf16[128,4096]{1,0:T(8,128)(2,1)S(1)} collective-permute-done((bf16[128,4096]{1,0:T(8,128)(2,1)S(1)}, bf16[128,4096]{1,0:T(8,128)(2,1)S(1)}, u32[]{:S(2)}, u32[]{:S(2)}) %collective-permute-start.3) | collective-permute-done | bytes 1048608 | tf_op jit(solution)/shard_map/ppermute | solution.py:124
  106.6 24.6 %collective-permute-done.4 = bf16[128,4096]{1,0:T(8,128)(2,1)S(1)} collective-permute-done((bf16[128,4096]{1,0:T(8,128)(2,1)S(1)}, bf16[128,4096]{1,0:T(8,128)(2,1)S(1)}, u32[]{:S(2)}, u32[]{:S(2)}) %collective-permute-start.4) | collective-permute-done | bytes 1048608 | tf_op jit(solution)/shard_map/ppermute | solution.py:124
  131.3 3.2 %fusion.1 = f32[128,4096]{1,0:T(8,128)} fusion(bf16[128,4096]{1,0:T(8,128)(2,1)S(1)} %collective-permute-done.5, bf16[128,4096]{1,0:T(8,128)(2,1)S(1)} %collective-permute-done.4, bf16[128,4096]{1,0:T(8,128)(2,1)S(1)} %collective-permute-done.3, bf16[4,128,4096]{2,1,0:T(8,128)(2,1)} %shard_map.112, s32[]{:T(128)S(6)} %select_n.163), kind=kLoop, calls=%fused_computation.3 | loop fusion | flops 3670016 | bytes 6291460 | tf_op jit(solution)/shard_map/add | solution.py:131
  134.5 0.7 copy-done.4
  135.2 0.1 fusion.59
  135.3 0.3 copy-done.1
  135.5 0.3 copy.28
  135.9 0.1 reshape.455
  136.0 0.1 iota_compare_fusion
  136.0 1.0 copy.25
  137.1 38.6 %reduce-scatter.5.cloned.1.call-done = f32[16,4096]{1,0:T(8,128)} async-done(((f32[128,4096]{1,0:T(8,128)}), f32[16,4096]{1,0:T(8,128)}) %reduce-scatter.5.cloned.1.call-update) | async-done | bytes 262160 | tf_op jit(solution)/shard_map/reduce_scatter | solution.py:164
  175.7 1.0 copy.26
  176.7 2.2 %multiply_bitcast_fusion.1 = (f32[4,8,32,128]{3,1,2,0:T(8,128)S(1)}, f32[1,32,4096]{2,1,0:T(8,128)}, f32[1,32,4096]{2,1,0:T(8,128)}, f32[4,8,32,128]{3,1,2,0:T(8,128)S(1)}) fusion(f32[1,32,4096]{2,1,0:T(8,128)S(1)} %copy-done.2, f32[1,16,4096]{2,1,0:T(8,128)} %bitcast.81, f32[1,16,4096]{2,1,0:T(8,128)} %bitcast.79, f32[1,32,4096]{2,1,0:T(8,128)S(1)} %copy-done.3), kind=kLoop, calls=%fused_computation.31 | loop fusion | flops 1179648 | bytes 3670016
  178.9 0.1 copy.24
  179.0 0.1 copy.27
  179.1 0.3 fusion.5
  179.4 0.6 fusion.10
  180.0 0.6 convolution_bitcast_fusion
  180.6 0.1 reshape.449
  180.7 0.1 reshape.448
  180.8 0.6 fusion.9
  181.4 1.3 gather_fusion
  182.8 0.8 select_select_fusion
  183.5 9.5 %all-to-all-start = ((bf16[8,16,512]{2,1,0:T(8,128)(2,1)}), bf16[8,16,512]{2,1,0:T(8,128)(2,1)S(1)}, u32[]{:S(2)}, u32[]{:S(2)}) async-start(bf16[8,16,512]{2,1,0:T(8,128)(2,1)} %select_select_fusion), calls=%async_computation.2 | async-start | bytes 262144 | tf_op jit(solution)/shard_map/all_to_all | solution.py:181
  193.0 0.9 multiply_subtract_fusion
  193.9 4.4 %all-to-all-done = bf16[8,16,512]{2,1,0:T(8,128)(2,1)S(1)} async-done(((bf16[8,16,512]{2,1,0:T(8,128)(2,1)}), bf16[8,16,512]{2,1,0:T(8,128)(2,1)S(1)}, u32[]{:S(2)}, u32[]{:S(2)}) %all-to-all-start) | async-done | bytes 131104 | tf_op jit(solution)/shard_map/all_to_all | solution.py:181
  198.3 0.7 copy.43
  (21 shorter events, 0.1 us)
Async XLA Ops:
  7.2 128.9 %reduce-scatter.3.cloned.1.call-start = ((), (), s32[]{:S(2)}) async-start(), calls=%async_computation.3 | async-start | bytes 2359296 | tf_op jit(solution)/shard_map/reduce_scatter | solution.py:164
  8.4 3.3 %copy-start = (f32[32,2,16,1]{3,2,1,0:T(8,128)}, f32[32,2,16,1]{3,2,1,0:T(8,128)S(1)}, u32[]{:S(2)}) copy-start(f32[32,2,16,1]{3,2,1,0:T(8,128)S(1)} %reshape.463.dn_ref) | copy-start | bytes 12292
  26.2 24.3 %collective-permute-start = (bf16[128,4096]{1,0:T(8,128)(2,1)}, bf16[128,4096]{1,0:T(8,128)(2,1)}, u32[]{:S(2)}, u32[]{:S(2)}) collective-permute-start(bf16[128,4096]{1,0:T(8,128)(2,1)} %get-tuple-element.19), channel_id=1, source_target_pairs={{0,64},{64,128},{128,192},{192,0},{1,65},{65,129},{129,193},{193,1... | collective-permute-start | bytes 3145736 | tf_op jit(solution)/shard_map/ppermute | solution.py:124
  28.2 47.8 %collective-permute-start.1 = (bf16[128,4096]{1,0:T(8,128)(2,1)S(1)}, bf16[128,4096]{1,0:T(8,128)(2,1)}, u32[]{:S(2)}, u32[]{:S(2)}) collective-permute-start(bf16[128,4096]{1,0:T(8,128)(2,1)S(1)} %get-tuple-element.18), channel_id=1, source_target_pairs={{0,128},{64,192},{128,0},{192,64},{1,129},{65,193},{129,1},{193,65... | collective-permute-start | bytes 3145736 | tf_op jit(solution)/shard_map/ppermute | solution.py:124
  30.7 45.4 %collective-permute-start.2 = (bf16[128,4096]{1,0:T(8,128)(2,1)S(1)}, bf16[128,4096]{1,0:T(8,128)(2,1)}, u32[]{:S(2)}, u32[]{:S(2)}) collective-permute-start(bf16[128,4096]{1,0:T(8,128)(2,1)S(1)} %get-tuple-element.17), channel_id=1, source_target_pairs={{0,192},{64,0},{128,64},{192,128},{1,193},{65,1},{129,65},{193,129... | collective-permute-start | bytes 3145736 | tf_op jit(solution)/shard_map/ppermute | solution.py:124
  79.9 95.7 %reduce-scatter.5.cloned.1.call-start = ((), (), s32[]{:S(2)}) async-start(), calls=%async_computation.4 | async-start | bytes 2359296 | tf_op jit(solution)/shard_map/reduce_scatter | solution.py:164
  82.2 24.5 %collective-permute-start.3 = (bf16[128,4096]{1,0:T(8,128)(2,1)S(1)}, bf16[128,4096]{1,0:T(8,128)(2,1)S(1)}, u32[]{:S(2)}, u32[]{:S(2)}) collective-permute-start(bf16[128,4096]{1,0:T(8,128)(2,1)S(1)} %get-tuple-element.14), channel_id=1, source_target_pairs={{0,64},{64,128},{128,192},{192,0},{1,65},{65,129},{129,193},{193,1... | collective-permute-start | bytes 3145736 | tf_op jit(solution)/shard_map/ppermute | solution.py:124
  83.1 48.2 %collective-permute-start.4 = (bf16[128,4096]{1,0:T(8,128)(2,1)S(1)}, bf16[128,4096]{1,0:T(8,128)(2,1)S(1)}, u32[]{:S(2)}, u32[]{:S(2)}) collective-permute-start(bf16[128,4096]{1,0:T(8,128)(2,1)S(1)} %get-tuple-element.16), channel_id=1, source_target_pairs={{0,128},{64,192},{128,0},{192,64},{1,129},{65,193},{129,1},{193,65... | collective-permute-start | bytes 3145736 | tf_op jit(solution)/shard_map/ppermute | solution.py:124
  86.1 45.2 %collective-permute-start.5 = (bf16[128,4096]{1,0:T(8,128)(2,1)S(1)}, bf16[128,4096]{1,0:T(8,128)(2,1)S(1)}, u32[]{:S(2)}, u32[]{:S(2)}) collective-permute-start(bf16[128,4096]{1,0:T(8,128)(2,1)S(1)} %get-tuple-element.15), channel_id=1, source_target_pairs={{0,192},{64,0},{128,64},{192,128},{1,193},{65,1},{129,65},{193,129... | collective-permute-start | bytes 3145736 | tf_op jit(solution)/shard_map/ppermute | solution.py:124
  134.5 0.7 copy-start.4
  134.5 1.1 copy-start.1
  134.5 1.4 copy-start.5
  134.5 1.5 copy-start.6
  134.5 42.2 %copy-start.2 = (f32[1,32,4096]{2,1,0:T(8,128)S(1)}, f32[1,32,4096]{2,1,0:T(8,128)}, u32[]{:S(2)}) copy-start(f32[1,32,4096]{2,1,0:T(8,128)} %param.11) | copy-start | bytes 1572868
  134.5 42.2 %copy-start.3 = (f32[1,32,4096]{2,1,0:T(8,128)S(1)}, f32[1,32,4096]{2,1,0:T(8,128)}, u32[]{:S(2)}) copy-start(f32[1,32,4096]{2,1,0:T(8,128)} %param.12) | copy-start | bytes 1572868
  183.5 14.7 %all-to-all-start = ((bf16[8,16,512]{2,1,0:T(8,128)(2,1)}), bf16[8,16,512]{2,1,0:T(8,128)(2,1)S(1)}, u32[]{:S(2)}, u32[]{:S(2)}) async-start(bf16[8,16,512]{2,1,0:T(8,128)(2,1)} %select_select_fusion), calls=%async_computation.2 | async-start | bytes 262144 | tf_op jit(solution)/shard_map/all_to_all | solution.py:181
Sparse Core Ops, SparseCore 0:
  80.0 41.6 reduce-scatter.2
  134.7 40.9 reduce-scatter.4

commit v5 on v2

--- a/solution.py
+++ b/solution.py
@@ -12,6 +12,7 @@
 HB = 128
 ROW_TILE = 256
 X_CHIPS = 4
+Z_FIRST_ROWS = 8
 WORKERS = ("wx", "wz")
 
 
@@ -108,6 +109,23 @@
     )(grad_rows, signed_walsh, up_scale, down_scale)
 
 
+def send_along(axis, pieces, size, dim):
+    mine = lax.axis_index(axis)
+    arrived = [lax.dynamic_index_in_dim(pieces, mine, dim, keepdims=False)]
+    for step in range(1, size):
+        outgoing = lax.dynamic_index_in_dim(pieces, (mine + step) % size, dim, keepdims=False)
+        pairs = [(i, (i + step) % size) for i in range(size)]
+        arrived.append(lax.ppermute(outgoing, axis, pairs))
+    return arrived
+
+
+def sum_arrived(arrived):
+    partial = arrived[0].astype(jnp.float32)
+    for piece in arrived[1:]:
+        partial = partial + piece.astype(jnp.float32)
+    return partial
+
+
 def select_pieces(slab_view, slot_lists, used_counts):
     gathered = jnp.take_along_axis(slab_view, slot_lists[:, :, None], axis=1)
     live_slots = lax.broadcasted_iota(jnp.int32, slot_lists.shape, 1) < used_counts[:, None]
@@ -124,10 +142,17 @@
     up_scale = (1.0 / unit_scale) / math.sqrt(HA * HB)
     terms = decoded_terms(grad_rows, signed_walsh, up_scale, unit_scale)
     x_size = lax.axis_size("wx")
-    workers = x_size * lax.axis_size("wz")
-    arrived_terms = lax.all_to_all(terms, "wx", split_axis=0, concat_axis=0, tiled=True)
-    partial = arrived_terms.reshape(x_size, grad_rows.shape[0] // x_size, -1).astype(jnp.float32).sum(0)
-    summed = lax.psum_scatter(partial, "wz", scatter_dimension=0, tiled=True)
+    z_size = lax.axis_size("wz")
+    workers = x_size * z_size
+    by_dest = terms.reshape(x_size, z_size, blocks, -1)
+    x_rows = blocks - Z_FIRST_ROWS
+    x_arrived = send_along("wx", by_dest[:, :, :x_rows], x_size, 0)
+    z_arrived = send_along("wz", by_dest[:, :, x_rows:], z_size, 1)
+    x_arrived, z_arrived = lax.optimization_barrier((x_arrived, z_arrived))
+    x_first = sum_arrived(x_arrived)
+    x_first = lax.psum_scatter(x_first.reshape(z_size * x_rows, -1), "wz", scatter_dimension=0, tiled=True)
+    z_first = sum_arrived(send_along("wx", sum_arrived(z_arrived), x_size, 0))
+    summed = jnp.concatenate([x_first, z_first], 0)
     mean_grad = summed / workers
     new_first = first_keep * first[0] + first_take * mean_grad
     new_second = second_keep * second[0] + second_take * mean_grad * mean_grad

time: 214 us -> 210 us (0.981)
  blocking collectives: 96.2 us -> 0 us
  waiting for transfers between devices: 63.1 us -> 110 us
  starting transfers between devices: 5.06 us -> 30.6 us
  local copies, waits for them, and re-layouts: 2.9 us -> 19 us
  other arithmetic: 12.4 us -> 15.3 us
    all_to_all x1 -> x0, blocking collectives: 96.2 us -> none  [per_device(): lax.all_to_all(terms, 'wx', split_axis=0, concat_axis=0, tiled=True)]
    ppermute x0 -> x13, waiting for transfers between devices: none -> 72.5 us  [send_along(): arrived.append(lax.ppermute(outgoing, axis, pairs))]
    reduce_scatter x1, waiting for transfers between devices: 58.7 us -> 33.2 us  [per_device(): lax.psum_scatter(x_first.reshape(z_size * x_rows, -1), 'wz', scatter_dime...]
    ppermute x0 -> x13, starting transfers between devices: none -> 22.3 us  [send_along(): arrived.append(lax.ppermute(outgoing, axis, pairs))]
    slice x0 -> x2, local copies, waits for them, and re-layouts: none -> 8.01 us  [the longest x1 6.29 us: per_device(): x_arrived = send_along('wx', by_dest[:, :, :x_rows], x_size, 0)]
    add x0 -> x3, other arithmetic: none -> 6.35 us  [sum_arrived(): partial = partial + piece.astype(jnp.float32)]
    squeeze x0 -> x3, local copies, waits for them, and re-layouts: none -> 6.01 us  [send_along(): lax.dynamic_index_in_dim(pieces, (mine + step) % size, dim, keepdims=False)]
    reduce_sum x1 -> x0, other arithmetic: 3.54 us -> none  [per_device(): arrived_terms.reshape(x_size, grad_rows.shape[0] // x_size, -1)]
  transfers between devices with their start and end apart: 2 -> 15, of which waited for: 2 -> 11; matrix products, arithmetic and copies ran while one was open for 1% -> 2% of each run, Pallas kernels for 0% -> 0%
where the time goes in v5:
time: 210 us
  waiting for transfers between devices  110 us (52%)
  starting transfers between devices  30.6 us (15%)
  Pallas kernels  19.1 us (9%)
  local copies, waits for them, and re-layouts  19 us (9%)
  other arithmetic  15.3 us (7%)
  between operations  14.3 us (7%)
    ppermute x13, waiting for transfers between devices, send_along(): arrived.append(lax.ppermute(outgoing, axis, pairs))  72.5 us
    reduce_scatter x1, waiting for transfers between devices, per_device(): lax.psum_scatter(x_first.reshape(z_size * x_rows, -1), 'wz', scatter_dime...  33.2 us
    ppermute x13, starting transfers between devices, send_along(): arrived.append(lax.ppermute(outgoing, axis, pairs))  22.3 us
    pallas_call x1, Pallas kernels, decoded_terms(): pl.pallas_call(code_kernel, grid=(rows // ROW_TILE,), in_specs=[pl.BlockS...  19.1 us
    all_to_all x1, starting transfers between devices, per_device(): lax.all_to_all(chosen_pieces, 'tensor', split_axis=0, concat_axis=0, tile...  8.25 us
    add x3, other arithmetic, sum_arrived(): partial = partial + piece.astype(jnp.float32)  6.35 us
    slice x1, local copies, waits for them, and re-layouts, per_device(): x_arrived = send_along('wx', by_dest[:, :, :x_rows], x_size, 0)  6.29 us
    squeeze x3, local copies, waits for them, and re-layouts, send_along(): lax.dynamic_index_in_dim(pieces, (mine + step) % size, dim, keepdims=False)  6.01 us
  transfers between devices with their start and end apart: 15, of which 11 were waited for; matrix products, arithmetic and copies ran while one was open for 2% of the time, Pallas kernels for 0%

profile of v5, /device:TPU:1, one launch (start us, length us, event | category | flops | bytes accessed | tf_op | source)
XLA Modules:
  0.0 209.6 jit_solution(17220495575263324181)
XLA Ops:
  7.3 0.7 fusion.46
  8.0 0.7 add_convert_fusion
  8.8 0.2 copy.20.dn_ref
  9.0 0.9 divide_multiply_fusion.up_ref
  10.0 1.7 multiply_convert_fusion.w_ref
  11.7 19.1 %shard_map.111 = bf16[1024,4096]{1,0:T(8,128)(2,1)} custom-call(bf16[1024,4096]{1,0:T(8,128)(2,1)} %bitcast.99, bf16[32,128,128]{2,1,0:T(8,128)(2,1)} %multiply_convert_fusion.w_ref, f32[1024,1]{1,0:T(8,128)} %divide_multiply_fusion.up_ref, f32[1024,1]{1,0:T(8,128)} %copy-done.1), custom_call_target="tpu_custom_call" | custom-call | flops 1107296256 | bytes 16777216 | tf_op jit(solution)/shard_map/pallas_call | solution.py:92
  30.7 6.3 %slice.10 = bf16[4,8,24,4096]{3,2,1,0:T(8,128)(2,1)} slice(bf16[4,8,32,4096]{3,2,1,0:T(8,128)(2,1)} %bitcast.96), slice={[0:4], [0:8], [0:24], [0:4096]} | slice | bytes 12582912 | tf_op jit(solution)/shard_map/slice | solution.py:149
  37.0 5.8 %dynamic-slice_bitcast_fusion = (bf16[8,24,4096]{2,1,0:T(8,128)(2,1)}, bf16[8,24,4096]{2,1,0:T(8,128)(2,1)}, bf16[8,24,4096]{2,1,0:T(8,128)(2,1)}, bf16[8,24,4096]{2,1,0:T(8,128)(2,1)}) fusion(bf16[4,8,24,4096]{3,2,1,0:T(8,128)(2,1)} %slice.10, s32[]{:T(128)S(6)} %select_n.218, s32[]{:T(128)S(6)} %select_n.216, s32[]{:T(128)S(6)} %select_n.214, s32[]{:T(128)S(6)} %select_n.212), kind=kLoop, calls=%fused_computation.3 | loop fusion | bytes 12582928 | tf_op jit(solution)/shard_map/jit(dynamic_index_in_dim)/squeeze | solution.py:116
  42.8 3.3 %collective-permute-start.2 = (bf16[8,24,4096]{2,1,0:T(8,128)(2,1)}, bf16[8,24,4096]{2,1,0:T(8,128)(2,1)}, u32[]{:S(2)}, u32[]{:S(2)}) collective-permute-start(bf16[8,24,4096]{2,1,0:T(8,128)(2,1)} %get-tuple-element.28), channel_id=1, source_target_pairs={{0,192},{64,0},{128,64},{192,128},{1,193},{65,1},{129,65},{193,129... | collective-permute-start | bytes 4718600 | tf_op jit(solution)/shard_map/ppermute | solution.py:118
  46.1 0.5 collective-permute-start.1
  46.6 0.6 collective-permute-start
  47.2 1.7 slice.11
  49.0 0.2 dynamic-slice_bitcast_fusion.4
  49.2 5.7 %collective-permute-start.9 = (bf16[4,8,4096]{2,1,0:T(8,128)(2,1)S(1)}, bf16[4,8,4096]{2,1,0:T(8,128)(2,1)S(1)}, u32[]{:S(2)}, u32[]{:S(2)}) collective-permute-start(bf16[4,8,4096]{2,1,0:T(8,128)(2,1)S(1)} %get-tuple-element.32), channel_id=1, source_target_pairs={{0,56},{8,0},{16,8},{24,16},{32,24},{40,32},{48,40},{56,48},{1,57}... | collective-permute-start | bytes 786440 | tf_op jit(solution)/shard_map/ppermute | solution.py:118
  54.9 1.2 collective-permute-start.8
  56.0 5.9 %collective-permute-done.9 = bf16[4,8,4096]{2,1,0:T(8,128)(2,1)S(1)} collective-permute-done((bf16[4,8,4096]{2,1,0:T(8,128)(2,1)S(1)}, bf16[4,8,4096]{2,1,0:T(8,128)(2,1)S(1)}, u32[]{:S(2)}, u32[]{:S(2)}) %collective-permute-start.9) | collective-permute-done | bytes 262176 | tf_op jit(solution)/shard_map/ppermute | solution.py:118
  61.9 0.3 collective-permute-start.7
  62.2 12.5 %collective-permute-done.8 = bf16[4,8,4096]{2,1,0:T(8,128)(2,1)S(1)} collective-permute-done((bf16[4,8,4096]{2,1,0:T(8,128)(2,1)S(1)}, bf16[4,8,4096]{2,1,0:T(8,128)(2,1)S(1)}, u32[]{:S(2)}, u32[]{:S(2)}) %collective-permute-start.8) | collective-permute-done | bytes 262176 | tf_op jit(solution)/shard_map/ppermute | solution.py:118
  74.7 0.9 collective-permute-start.6
  75.5 23.1 %collective-permute-done.7 = bf16[4,8,4096]{2,1,0:T(8,128)(2,1)S(1)} collective-permute-done((bf16[4,8,4096]{2,1,0:T(8,128)(2,1)S(1)}, bf16[4,8,4096]{2,1,0:T(8,128)(2,1)S(1)}, u32[]{:S(2)}, u32[]{:S(2)}) %collective-permute-start.7) | collective-permute-done | bytes 262176 | tf_op jit(solution)/shard_map/ppermute | solution.py:118
  98.6 6.4 %collective-permute-start.4 = (bf16[4,8,4096]{2,1,0:T(8,128)(2,1)S(1)}, bf16[4,8,4096]{2,1,0:T(8,128)(2,1)S(1)}, u32[]{:S(2)}, u32[]{:S(2)}) collective-permute-start(bf16[4,8,4096]{2,1,0:T(8,128)(2,1)S(1)} %get-tuple-element.37), channel_id=1, source_target_pairs={{0,16},{8,24},{16,32},{24,40},{32,48},{40,56},{48,0},{56,8},{1,17}... | collective-permute-start | bytes 786440 | tf_op jit(solution)/shard_map/ppermute | solution.py:118
  105.0 9.6 %collective-permute-done.5 = bf16[4,8,4096]{2,1,0:T(8,128)(2,1)S(1)} collective-permute-done((bf16[4,8,4096]{2,1,0:T(8,128)(2,1)S(1)}, bf16[4,8,4096]{2,1,0:T(8,128)(2,1)S(1)}, u32[]{:S(2)}, u32[]{:S(2)}) %collective-permute-start.5) | collective-permute-done | bytes 262176 | tf_op jit(solution)/shard_map/ppermute | solution.py:118
  114.6 0.4 collective-permute-done.4
  114.9 16.6 %collective-permute-done.3 = bf16[4,8,4096]{2,1,0:T(8,128)(2,1)S(1)} collective-permute-done((bf16[4,8,4096]{2,1,0:T(8,128)(2,1)S(1)}, bf16[4,8,4096]{2,1,0:T(8,128)(2,1)S(1)}, u32[]{:S(2)}, u32[]{:S(2)}) %collective-permute-start.3) | collective-permute-done | bytes 262176 | tf_op jit(solution)/shard_map/ppermute | solution.py:118
  131.6 5.1 %convert_add_fusion = f32[8,24,4096]{2,1,0:T(8,128)} fusion(bf16[8,24,4096]{2,1,0:T(8,128)(2,1)} %collective-permute-done.2, bf16[8,24,4096]{2,1,0:T(8,128)(2,1)} %collective-permute-done.1, bf16[8,24,4096]{2,1,0:T(8,128)(2,1)} %collective-permute-done, bf16[8,24,4096]{2,1,0:T(8,128)(2,1)S(1)} %copy-done), kind=kLoop, calls=%fused_computation.1 | loop fusion | flops 5505024 | bytes 9437184 | tf_op jit(solution)/shard_map/add | solution.py:125
  136.7 0.6 copy-done.7
  137.5 0.2 copy-done.2
  137.8 0.3 copy.28
  138.1 1.2 convert_add_fusion.1
  139.4 1.6 collective-permute-start.10
  141.0 1.1 collective-permute-start.12
  142.1 0.8 collective-permute-start.11
  143.0 1.5 collective-permute-done.10
  144.5 0.4 collective-permute-done.12
  144.8 2.6 %collective-permute-done.11 = f32[8,4096]{1,0:T(8,128)S(1)} collective-permute-done((f32[8,4096]{1,0:T(8,128)S(1)}, f32[8,4096]{1,0:T(8,128)S(1)}, u32[]{:S(2)}, u32[]{:S(2)}) %collective-permute-start.11) | collective-permute-done | bytes 131104 | tf_op jit(solution)/shard_map/ppermute | solution.py:118
  147.5 33.2 %reduce-scatter.2.cloned.1.call-done = f32[24,4096]{1,0:T(8,128)} async-done(((f32[192,4096]{1,0:T(8,128)}), f32[24,4096]{1,0:T(8,128)}) %reduce-scatter.2.cloned.1.call-update) | async-done | bytes 393232 | tf_op jit(solution)/shard_map/reduce_scatter | solution.py:153
  180.7 1.1 copy.26
  181.8 2.2 %multiply_bitcast_fusion.1 = (f32[4,8,32,128]{3,1,2,0:T(8,128)S(1)}, f32[1,32,4096]{2,1,0:T(8,128)}, f32[1,32,4096]{2,1,0:T(8,128)}, f32[4,8,32,128]{3,1,2,0:T(8,128)S(1)}) fusion(f32[1,32,4096]{2,1,0:T(8,128)S(1)} %copy-done.3, f32[1,8,4096]{2,1,0:T(8,128)S(1)} %bitcast.105, f32[1,24,4096]{2,1,0:T(8,128)} %bitcast.103, f32[1,32,4096]{2,1,0:T(8,128)S(1)} %copy-done.4), kind=kLoop, calls=%fused_computation.26 | loop fusion | flops 1179648 | bytes 3670016
  184.2 0.3 fusion.3
  184.5 0.6 fusion.10
  185.1 0.6 convolution_bitcast_fusion
  185.9 0.6 fusion.7
  186.5 1.3 gather_fusion
  187.9 0.8 select_select_fusion
  188.6 8.2 %all-to-all-start = ((bf16[8,16,512]{2,1,0:T(8,128)(2,1)}), bf16[8,16,512]{2,1,0:T(8,128)(2,1)S(1)}, u32[]{:S(2)}, u32[]{:S(2)}) async-start(bf16[8,16,512]{2,1,0:T(8,128)(2,1)} %select_select_fusion), calls=%async_computation.1 | async-start | bytes 262144 | tf_op jit(solution)/shard_map/all_to_all | solution.py:169
  196.9 0.9 multiply_subtract_fusion
  197.7 4.4 %all-to-all-done = bf16[8,16,512]{2,1,0:T(8,128)(2,1)S(1)} async-done(((bf16[8,16,512]{2,1,0:T(8,128)(2,1)}), bf16[8,16,512]{2,1,0:T(8,128)(2,1)S(1)}, u32[]{:S(2)}, u32[]{:S(2)}) %all-to-all-start) | async-done | bytes 131104 | tf_op jit(solution)/shard_map/all_to_all | solution.py:169
  202.1 0.7 copy.44
  (38 shorter events, 0.9 us)
Async XLA Ops:
  7.2 173.5 %reduce-scatter.2.cloned.1.call-start = ((), (), s32[]{:S(2)}) async-start(), calls=%async_computation.2 | async-start | bytes 3538944 | tf_op jit(solution)/shard_map/reduce_scatter | solution.py:153
  9.0 2.6 %copy-start.1 = (f32[1024,1]{1,0:T(8,128)}, f32[1024,1]{1,0:T(8,128)S(1)}, u32[]{:S(2)}) copy-start(f32[1024,1]{1,0:T(8,128)S(1)} %copy.20.dn_ref) | copy-start | bytes 12292
  42.8 88.8 %collective-permute-start.2 = (bf16[8,24,4096]{2,1,0:T(8,128)(2,1)}, bf16[8,24,4096]{2,1,0:T(8,128)(2,1)}, u32[]{:S(2)}, u32[]{:S(2)}) collective-permute-start(bf16[8,24,4096]{2,1,0:T(8,128)(2,1)} %get-tuple-element.28), channel_id=1, source_target_pairs={{0,192},{64,0},{128,64},{192,128},{1,193},{65,1},{129,65},{193,129... | collective-permute-start | bytes 4718600 | tf_op jit(solution)/shard_map/ppermute | solution.py:118
  46.1 85.5 %collective-permute-start.1 = (bf16[8,24,4096]{2,1,0:T(8,128)(2,1)}, bf16[8,24,4096]{2,1,0:T(8,128)(2,1)}, u32[]{:S(2)}, u32[]{:S(2)}) collective-permute-start(bf16[8,24,4096]{2,1,0:T(8,128)(2,1)} %get-tuple-element.29), channel_id=1, source_target_pairs={{0,128},{64,192},{128,0},{192,64},{1,129},{65,193},{129,1},{193,65... | collective-permute-start | bytes 4718600 | tf_op jit(solution)/shard_map/ppermute | solution.py:118
  46.6 85.0 %collective-permute-start = (bf16[8,24,4096]{2,1,0:T(8,128)(2,1)}, bf16[8,24,4096]{2,1,0:T(8,128)(2,1)}, u32[]{:S(2)}, u32[]{:S(2)}) collective-permute-start(bf16[8,24,4096]{2,1,0:T(8,128)(2,1)} %get-tuple-element.30), channel_id=1, source_target_pairs={{0,64},{64,128},{128,192},{192,0},{1,65},{65,129},{129,193},{193,1... | collective-permute-start | bytes 4718600 | tf_op jit(solution)/shard_map/ppermute | solution.py:118
  49.0 82.6 %copy-start = (bf16[8,24,4096]{2,1,0:T(8,128)(2,1)S(1)}, bf16[8,24,4096]{2,1,0:T(8,128)(2,1)}, u32[]{:S(2)}) copy-start(bf16[8,24,4096]{2,1,0:T(8,128)(2,1)} %get-tuple-element.16) | copy-start | bytes 4718596
  49.2 12.7 %collective-permute-start.9 = (bf16[4,8,4096]{2,1,0:T(8,128)(2,1)S(1)}, bf16[4,8,4096]{2,1,0:T(8,128)(2,1)S(1)}, u32[]{:S(2)}, u32[]{:S(2)}) collective-permute-start(bf16[4,8,4096]{2,1,0:T(8,128)(2,1)S(1)} %get-tuple-element.32), channel_id=1, source_target_pairs={{0,56},{8,0},{16,8},{24,16},{32,24},{40,32},{48,40},{56,48},{1,57}... | collective-permute-start | bytes 786440 | tf_op jit(solution)/shard_map/ppermute | solution.py:118
  54.9 19.8 %collective-permute-start.8 = (bf16[4,8,4096]{2,1,0:T(8,128)(2,1)S(1)}, bf16[4,8,4096]{2,1,0:T(8,128)(2,1)S(1)}, u32[]{:S(2)}, u32[]{:S(2)}) collective-permute-start(bf16[4,8,4096]{2,1,0:T(8,128)(2,1)S(1)} %get-tuple-element.33), channel_id=1, source_target_pairs={{0,48},{8,56},{16,0},{24,8},{32,16},{40,24},{48,32},{56,40},{1,49}... | collective-permute-start | bytes 786440 | tf_op jit(solution)/shard_map/ppermute | solution.py:118
  61.9 36.6 %collective-permute-start.7 = (bf16[4,8,4096]{2,1,0:T(8,128)(2,1)S(1)}, bf16[4,8,4096]{2,1,0:T(8,128)(2,1)S(1)}, u32[]{:S(2)}, u32[]{:S(2)}) collective-permute-start(bf16[4,8,4096]{2,1,0:T(8,128)(2,1)S(1)} %get-tuple-element.34), channel_id=1, source_target_pairs={{0,40},{8,48},{16,56},{24,0},{32,8},{40,16},{48,24},{56,32},{1,41}... | collective-permute-start | bytes 786440 | tf_op jit(solution)/shard_map/ppermute | solution.py:118
  74.7 23.9 %collective-permute-start.6 = (bf16[4,8,4096]{2,1,0:T(8,128)(2,1)S(1)}, bf16[4,8,4096]{2,1,0:T(8,128)(2,1)S(1)}, u32[]{:S(2)}, u32[]{:S(2)}) collective-permute-start(bf16[4,8,4096]{2,1,0:T(8,128)(2,1)S(1)} %get-tuple-element.35), channel_id=1, source_target_pairs={{0,32},{8,40},{16,48},{24,56},{32,0},{40,8},{48,16},{56,24},{1,33}... | collective-permute-start | bytes 786440 | tf_op jit(solution)/shard_map/ppermute | solution.py:118
  98.6 16.0 %collective-permute-start.5 = (bf16[4,8,4096]{2,1,0:T(8,128)(2,1)S(1)}, bf16[4,8,4096]{2,1,0:T(8,128)(2,1)S(1)}, u32[]{:S(2)}, u32[]{:S(2)}) collective-permute-start(bf16[4,8,4096]{2,1,0:T(8,128)(2,1)S(1)} %get-tuple-element.36), channel_id=1, source_target_pairs={{0,24},{8,32},{16,40},{24,48},{32,56},{40,0},{48,8},{56,16},{1,25}... | collective-permute-start | bytes 786440 | tf_op jit(solution)/shard_map/ppermute | solution.py:118
  98.6 16.4 %collective-permute-start.4 = (bf16[4,8,4096]{2,1,0:T(8,128)(2,1)S(1)}, bf16[4,8,4096]{2,1,0:T(8,128)(2,1)S(1)}, u32[]{:S(2)}, u32[]{:S(2)}) collective-permute-start(bf16[4,8,4096]{2,1,0:T(8,128)(2,1)S(1)} %get-tuple-element.37), channel_id=1, source_target_pairs={{0,16},{8,24},{16,32},{24,40},{32,48},{40,56},{48,0},{56,8},{1,17}... | collective-permute-start | bytes 786440 | tf_op jit(solution)/shard_map/ppermute | solution.py:118
  114.6 17.0 %collective-permute-start.3 = (bf16[4,8,4096]{2,1,0:T(8,128)(2,1)S(1)}, bf16[4,8,4096]{2,1,0:T(8,128)(2,1)S(1)}, u32[]{:S(2)}, u32[]{:S(2)}) collective-permute-start(bf16[4,8,4096]{2,1,0:T(8,128)(2,1)S(1)} %get-tuple-element.38), channel_id=1, source_target_pairs={{0,8},{8,16},{16,24},{24,32},{32,40},{40,48},{48,56},{56,0},{1,9},... | collective-permute-start | bytes 786440 | tf_op jit(solution)/shard_map/ppermute | solution.py:118
  131.6 5.2 %copy-start.5 = (bf16[4,8,4096]{2,1,0:T(8,128)(2,1)}, bf16[4,8,4096]{2,1,0:T(8,128)(2,1)S(1)}, u32[]{:S(2)}) copy-start(bf16[4,8,4096]{2,1,0:T(8,128)(2,1)S(1)} %collective-permute-done.3) | copy-start | bytes 786436
  136.7 0.7 copy-start.7
  136.7 0.8 copy-start.6
  136.7 1.1 copy-start.2
  137.8 5.1 %copy-start.8 = (s32[1,1,8]{2,1,0:T(1,128)S(1)}, s32[1,1,8]{2,1,0:T(1,128)}, u32[]{:S(2)}) copy-start(s32[1,1,8]{2,1,0:T(1,128)} %param.15) | copy-start | bytes 100
  139.3 42.5 %copy-start.3 = (f32[1,32,4096]{2,1,0:T(8,128)S(1)}, f32[1,32,4096]{2,1,0:T(8,128)}, u32[]{:S(2)}) copy-start(f32[1,32,4096]{2,1,0:T(8,128)} %param.11) | copy-start | bytes 1572868
  139.3 42.5 %copy-start.4 = (f32[1,32,4096]{2,1,0:T(8,128)S(1)}, f32[1,32,4096]{2,1,0:T(8,128)}, u32[]{:S(2)}) copy-start(f32[1,32,4096]{2,1,0:T(8,128)} %param.12) | copy-start | bytes 1572868
  139.4 5.1 %collective-permute-start.10 = (f32[8,4096]{1,0:T(8,128)S(1)}, f32[8,4096]{1,0:T(8,128)S(1)}, u32[]{:S(2)}, u32[]{:S(2)}) collective-permute-start(f32[8,4096]{1,0:T(8,128)S(1)} %get-tuple-element.44), channel_id=1, source_target_pairs={{0,64},{64,128},{128,192},{192,0},{1,65},{65,129},{129,193},{193,1... | collective-permute-start | bytes 393224 | tf_op jit(solution)/shard_map/ppermute | solution.py:118
  141.0 3.8 %collective-permute-start.12 = (f32[8,4096]{1,0:T(8,128)S(1)}, f32[8,4096]{1,0:T(8,128)S(1)}, u32[]{:S(2)}, u32[]{:S(2)}) collective-permute-start(f32[8,4096]{1,0:T(8,128)S(1)} %get-tuple-element.45), channel_id=1, source_target_pairs={{0,192},{64,0},{128,64},{192,128},{1,193},{65,1},{129,65},{193,129... | collective-permute-start | bytes 393224 | tf_op jit(solution)/shard_map/ppermute | solution.py:118
  142.1 5.3 %collective-permute-start.11 = (f32[8,4096]{1,0:T(8,128)S(1)}, f32[8,4096]{1,0:T(8,128)S(1)}, u32[]{:S(2)}, u32[]{:S(2)}) collective-permute-start(f32[8,4096]{1,0:T(8,128)S(1)} %get-tuple-element.46), channel_id=1, source_target_pairs={{0,128},{64,192},{128,0},{192,64},{1,129},{65,193},{129,1},{193,65... | collective-permute-start | bytes 393224 | tf_op jit(solution)/shard_map/ppermute | solution.py:118
  188.6 13.5 %all-to-all-start = ((bf16[8,16,512]{2,1,0:T(8,128)(2,1)}), bf16[8,16,512]{2,1,0:T(8,128)(2,1)S(1)}, u32[]{:S(2)}, u32[]{:S(2)}) async-start(bf16[8,16,512]{2,1,0:T(8,128)(2,1)} %select_select_fusion), calls=%async_computation.1 | async-start | bytes 262144 | tf_op jit(solution)/shard_map/all_to_all | solution.py:169
Sparse Core Ops, SparseCore 0:
  136.8 43.8 reduce-scatter.1

commit v6 on v4

--- a/solution.py
+++ b/solution.py
@@ -1,3 +1,4 @@
+import functools
 import math
 
 import jax
@@ -69,59 +70,82 @@
     return blocks
 
 
-def code_kernel(x_ref, w_ref, up_ref, dn_ref, o_ref, y_ref):
+def exact_powers(shift_vals):
+    up = jnp.ones(shift_vals.shape, jnp.float32)
+    down = jnp.ones(shift_vals.shape, jnp.float32)
+    factor = 2.0
+    for bit_level in range(5):
+        chosen = jnp.bitwise_and(jnp.right_shift(shift_vals, bit_level), 1) == 1
+        up = up * jnp.where(chosen, factor, 1.0)
+        down = down * jnp.where(chosen, 1.0 / factor, 1.0)
+        factor = factor * factor
+    return up, down
+
+
+def code_rows(y_ref, sh_ref, o_ref, group_rows, g, carry):
+    rows = pl.ds(pl.multiple_of(g * 8, 8), 8)
+    dest = g // (group_rows // 8)
+    within = pl.ds(pl.multiple_of((g % (group_rows // 8)) * 8, 8), 8)
+    blocks = butterfly([y_ref[rows, a * HB:(a + 1) * HB] for a in range(HA)])
+    up, dn = exact_powers(sh_ref[dest, within, :])
+    up = up * (1.0 / math.sqrt(HA * HB))
+    for a in range(HA):
+        coded = jnp.clip(blocks[a] * up, -127.0, 127.0).astype(jnp.bfloat16)
+        o_ref[rows, a * HB:(a + 1) * HB] = (coded.astype(jnp.float32) * dn).astype(o_ref.dtype)
+    return carry
+
+
+def code_kernel(mx_ref, x_ref, sg_ref, w_ref, sh_ref, *refs):
+    out_refs, y_ref = refs[:-1], refs[-1]
+    step = pl.program_id(0)
     groups, group_rows, _ = x_ref.shape
     for a in range(HA):
         cols = slice(a * HB, (a + 1) * HB)
-        lhs = x_ref[:, :, cols].reshape(groups * group_rows, HB)
-        y_ref[:, cols] = jnp.dot(lhs, w_ref[a], preferred_element_type=jnp.float32)
-
-    def row_group(g, carry):
-        rows = pl.ds(pl.multiple_of(g * 8, 8), 8)
-        dest = g // (group_rows // 8)
-        within = pl.ds(pl.multiple_of((g % (group_rows // 8)) * 8, 8), 8)
-        blocks = butterfly([y_ref[rows, a * HB:(a + 1) * HB] for a in range(HA)])
-        up = up_ref[dest, within, :]
-        dn = dn_ref[dest, within, :]
-        for a in range(HA):
-            coded = jnp.clip(blocks[a] * up, -127.0, 127.0).astype(jnp.bfloat16)
-            o_ref[rows, a * HB:(a + 1) * HB] = (coded.astype(jnp.float32) * dn).astype(o_ref.dtype)
-        return carry
-
-    lax.fori_loop(0, groups * group_rows // 8, row_group, 0)
-
-
-def decoded_terms(grad_groups, signed_walsh, up_scale, down_scale, part, x_size):
+        lhs = (x_ref[:, :, cols] * sg_ref[:, cols]).reshape(groups * group_rows, HB)
+        y_ref[:, cols] = jnp.dot(lhs, w_ref[...], preferred_element_type=jnp.float32)
+    for k, o_ref in enumerate(out_refs):
+
+        @pl.when(step == k)
+        def _(o_ref=o_ref):
+            coder = functools.partial(code_rows, y_ref, sh_ref, o_ref, group_rows)
+            lax.fori_loop(0, groups * group_rows // 8, coder, 0)
+
+
+def decoded_terms(grad_groups, sign_row, walsh, shift_groups, part, x_size):
     dests, _, part_rows, width = grad_groups.shape
     per_x = dests // x_size
-    tile = lambda i: (i, part, 0, 0)
+    my_x = jnp.reshape(lax.axis_index("wx"), (1,)).astype(jnp.int32)
+    tile = lambda i, mx: ((mx[0] + i) % x_size, part, 0, 0)
+    whole = lambda i, mx: (0, 0)
+    out_rows = per_x * part_rows
     return pl.pallas_call(
         code_kernel,
-        grid=(x_size,),
-        in_specs=[
-            pl.BlockSpec((per_x, None, part_rows, width), tile),
-            pl.BlockSpec((HA, HB, HB), lambda i: (0, 0, 0)),
-            pl.BlockSpec((per_x, None, part_rows, 1), tile),
-            pl.BlockSpec((per_x, None, part_rows, 1), tile),
-        ],
-        out_specs=pl.BlockSpec((None, per_x * part_rows, width), lambda i: (i, 0, 0)),
-        out_shape=jax.ShapeDtypeStruct((x_size, per_x * part_rows, width), jnp.bfloat16),
-        scratch_shapes=[pltpu.VMEM((per_x * part_rows, width), jnp.float32)],
+        grid_spec=pltpu.PrefetchScalarGridSpec(
+            num_scalar_prefetch=1,
+            grid=(x_size,),
+            in_specs=[
+                pl.BlockSpec((per_x, None, part_rows, width), tile),
+                pl.BlockSpec((1, width), whole),
+                pl.BlockSpec((HB, HB), whole),
+                pl.BlockSpec((per_x, None, part_rows, 1), tile),
+            ],
+            out_specs=[pl.BlockSpec((out_rows, width), whole) for _ in range(x_size)],
+            scratch_shapes=[pltpu.VMEM((out_rows, width), jnp.float32)],
+        ),
+        out_shape=[jax.ShapeDtypeStruct((out_rows, width), jnp.bfloat16) for _ in range(x_size)],
         cost_estimate=pl.CostEstimate(
             flops=2 * dests * part_rows * width * HB + 8 * dests * part_rows * width,
             transcendentals=0,
             bytes_accessed=dests * part_rows * width * 4,
         ),
-    )(grad_groups, signed_walsh, up_scale, down_scale)
+    )(my_x, grad_groups, sign_row, walsh, shift_groups)
 
 
 def send_along_x(terms, x_size):
-    my_x = lax.axis_index("wx")
-    arrived = [lax.dynamic_index_in_dim(terms, my_x, 0, keepdims=False)]
+    arrived = [terms[0]]
     for step in range(1, x_size):
-        outgoing = lax.dynamic_index_in_dim(terms, (my_x + step) % x_size, 0, keepdims=False)
         pairs = [(i, (i + step) % x_size) for i in range(x_size)]
-        arrived.append(lax.ppermute(outgoing, "wx", pairs))
+        arrived.append(lax.ppermute(terms[step], "wx", pairs))
     return arrived
 
 
@@ -143,22 +167,21 @@
     grad_rows = grads[0, 0]
     shift_rows = shifts[0, 0]
     blocks = first.shape[1]
-    signed_walsh = (sign_vec.reshape(HA, HB, 1) * walsh_table(HB)[None]).astype(jnp.bfloat16)
-    unit_scale = half_power(shift_rows)[:, None]
-    up_scale = (1.0 / unit_scale) / math.sqrt(HA * HB)
+    sign_row = sign_vec.astype(jnp.bfloat16)[None, :]
+    walsh = walsh_table(HB).astype(jnp.bfloat16)
     x_size = lax.axis_size("wx")
     dests = x_size * lax.axis_size("wz")
     workers = dests
     part_rows = blocks // PARTS
     as_groups = lambda rows: rows.reshape(dests, PARTS, part_rows, rows.shape[-1])
     grad_groups = as_groups(grad_rows)
-    up_groups, down_groups = as_groups(up_scale), as_groups(unit_scale)
+    shift_groups = as_groups(shift_rows[:, None])
     pieces = []
-    terms = decoded_terms(grad_groups, signed_walsh, up_groups, down_groups, 0, x_size)
+    terms = decoded_terms(grad_groups, sign_row, walsh, shift_groups, 0, x_size)
     arrived = send_along_x(terms, x_size)
     for part in range(1, PARTS + 1):
         if part < PARTS:
-            terms = decoded_terms(grad_groups, signed_walsh, up_groups, down_groups, part, x_size)
+            terms = decoded_terms(grad_groups, sign_row, walsh, shift_groups, part, x_size)
             arrived, terms = lax.optimization_barrier((arrived, terms))
         partial = sum_arrived(arrived)
         pieces.append(lax.psum_scatter(partial, "wz", scatter_dimension=0, tiled=True))

time: 206 us -> 201 us (0.976)
  local copies, waits for them, and re-layouts: 11.8 us -> 7.12 us
  Pallas kernels: 22 us -> 24.7 us
    squeeze x2 -> x0, local copies, waits for them, and re-layouts: 5.75 us -> none  [send_along_x(): lax.dynamic_index_in_dim(terms, (my_x + step) % x_size, 0, keepdims=False)]
    pallas_call x2, Pallas kernels: 22 us -> 24.7 us  [decoded_terms(): pl.pallas_call(code_kernel, grid_spec=pltpu.PrefetchScalarGridSpec(num_sc...]
    unnamed x21 -> x26, local copies, waits for them, and re-layouts: 4.13 us -> 3.87 us
  transfers between devices with their start and end apart: 9 -> 9, of which waited for: 6 -> 6; matrix products, arithmetic and copies ran while one was open for 4% -> 3% of each run, Pallas kernels for 5% -> 6%
where the time goes in v6:
time: 201 us
  waiting for transfers between devices  120 us (60%)
  Pallas kernels  24.7 us (12%)
  starting transfers between devices  19.4 us (10%)
  between operations  14.2 us (7%)
  other arithmetic  14.1 us (7%)
  local copies, waits for them, and re-layouts  7.12 us (4%)
    ppermute x6, waiting for transfers between devices, send_along_x(): arrived.append(lax.ppermute(terms[step], 'wx', pairs))  77 us
    reduce_scatter x2, waiting for transfers between devices, per_device(): lax.psum_scatter(partial, 'wz', scatter_dimension=0, tiled=True)  38.6 us
    pallas_call x2, Pallas kernels, decoded_terms(): pl.pallas_call(code_kernel, grid_spec=pltpu.PrefetchScalarGridSpec(num_sc...  24.7 us
    ppermute x6, starting transfers between devices, send_along_x(): arrived.append(lax.ppermute(terms[step], 'wx', pairs))  10 us
    all_to_all x1, starting transfers between devices, per_device(): lax.all_to_all(chosen_pieces, 'tensor', split_axis=0, concat_axis=0, tile...  9.37 us
    add x2, other arithmetic, sum_arrived(): partial = partial + piece.astype(jnp.float32)  5.14 us
    all_to_all x1, waiting for transfers between devices, per_device(): lax.all_to_all(chosen_pieces, 'tensor', split_axis=0, concat_axis=0, tile...  4.36 us
  transfers between devices with their start and end apart: 9, of which 6 were waited for; matrix products, arithmetic and copies ran while one was open for 3% of the time, Pallas kernels for 6%

profile of v6, /device:TPU:1, one launch (start us, length us, event | category | flops | bytes accessed | tf_op | source)
XLA Modules:
  0.0 200.7 jit_solution(8214666979610953385)
XLA Ops:
  7.2 0.0 reduce-scatter.3.cloned.1.call-start
  7.2 0.7 convert_convert_fusion.w_ref
  7.9 0.5 broadcast.242
  8.4 1.3 reduce.6
  9.7 1.1 reshape_broadcast_in_dim_squeeze.4.sh_ref
  10.9 1.3 convert_convert_fusion.1.sg_ref
  12.2 12.3 %shard_map.111 = (bf16[128,4096]{1,0:T(8,128)(2,1)}, bf16[128,4096]{1,0:T(8,128)(2,1)}, bf16[128,4096]{1,0:T(8,128)(2,1)}, bf16[128,4096]{1,0:T(8,128)(2,1)}) custom-call(s32[1]{0:T(128)} %bitcast.mx_ref, bf16[32,2,16,4096]{3,2,1,0:T(8,128)(2,1)} %bitcast.57, bf16[1,4096]{1,0:T(2,128)(2,1)} %convert_convert_fusion.1.sg_ref, ...), custom_call_target="tpu_custom_call" | custom-call | flops 553648128 | bytes 8388608 | tf_op jit(solution)/shard_map/pallas_call | solution.py:121
  24.6 2.0 %collective-permute-start = (bf16[128,4096]{1,0:T(8,128)(2,1)}, bf16[128,4096]{1,0:T(8,128)(2,1)S(1)}, u32[]{:S(2)}, u32[]{:S(2)}) collective-permute-start(bf16[128,4096]{1,0:T(8,128)(2,1)} %get-tuple-element.21), channel_id=1, source_target_pairs={{0,64},{64,128},{128,192},{192,0},{1,65},{65,129},{129,193},{193,1... | collective-permute-start | bytes 3145736 | tf_op jit(solution)/shard_map/ppermute | solution.py:148
  26.6 2.5 %collective-permute-start.1 = (bf16[128,4096]{1,0:T(8,128)(2,1)}, bf16[128,4096]{1,0:T(8,128)(2,1)S(1)}, u32[]{:S(2)}, u32[]{:S(2)}) collective-permute-start(bf16[128,4096]{1,0:T(8,128)(2,1)} %get-tuple-element.22), channel_id=1, source_target_pairs={{0,128},{64,192},{128,0},{192,64},{1,129},{65,193},{129,1},{193,65... | collective-permute-start | bytes 3145736 | tf_op jit(solution)/shard_map/ppermute | solution.py:148
  29.0 1.1 collective-permute-start.2
  30.2 12.3 %shard_map.112 = (bf16[128,4096]{1,0:T(8,128)(2,1)}, bf16[128,4096]{1,0:T(8,128)(2,1)}, bf16[128,4096]{1,0:T(8,128)(2,1)}, bf16[128,4096]{1,0:T(8,128)(2,1)}) custom-call(s32[1]{0:T(128)} %bitcast.mx_ref, bf16[32,2,16,4096]{3,2,1,0:T(8,128)(2,1)} %bitcast.58, bf16[1,4096]{1,0:T(2,128)(2,1)} %convert_convert_fusion.1.sg_ref, ...), custom_call_target="tpu_custom_call" | custom-call | flops 553648128 | bytes 8388608 | tf_op jit(solution)/shard_map/pallas_call | solution.py:121
  42.5 6.2 %collective-permute-done = bf16[128,4096]{1,0:T(8,128)(2,1)S(1)} collective-permute-done((bf16[128,4096]{1,0:T(8,128)(2,1)}, bf16[128,4096]{1,0:T(8,128)(2,1)S(1)}, u32[]{:S(2)}, u32[]{:S(2)}) %collective-permute-start) | collective-permute-done | bytes 1048608 | tf_op jit(solution)/shard_map/ppermute | solution.py:148
  48.7 25.6 %collective-permute-done.1 = bf16[128,4096]{1,0:T(8,128)(2,1)S(1)} collective-permute-done((bf16[128,4096]{1,0:T(8,128)(2,1)}, bf16[128,4096]{1,0:T(8,128)(2,1)S(1)}, u32[]{:S(2)}, u32[]{:S(2)}) %collective-permute-start.1) | collective-permute-done | bytes 1048608 | tf_op jit(solution)/shard_map/ppermute | solution.py:148
  74.3 3.2 %convert_add_fusion.1 = f32[128,4096]{1,0:T(8,128)} fusion(bf16[128,4096]{1,0:T(8,128)(2,1)} %collective-permute-done.2, bf16[128,4096]{1,0:T(8,128)(2,1)S(1)} %collective-permute-done.1, bf16[128,4096]{1,0:T(8,128)(2,1)S(1)} %collective-permute-done, bf16[128,4096]{1,0:T(8,128)(2,1)S(1)} %copy-done.2), kind=kLoop, calls=%fused_computation.2 | loop fusion | flops 3670016 | bytes 6291456 | tf_op jit(solution)/shard_map/add | solution.py:155
  77.5 0.0 reduce-scatter.3.cloned.1.call-update
  77.5 0.0 reduce-scatter.5.cloned.1.call-start
  77.6 1.2 collective-permute-start.3
  78.8 3.0 %collective-permute-start.4 = (bf16[128,4096]{1,0:T(8,128)(2,1)}, bf16[128,4096]{1,0:T(8,128)(2,1)S(1)}, u32[]{:S(2)}, u32[]{:S(2)}) collective-permute-start(bf16[128,4096]{1,0:T(8,128)(2,1)} %get-tuple-element.34), channel_id=1, source_target_pairs={{0,128},{64,192},{128,0},{192,64},{1,129},{65,193},{129,1},{193,65... | collective-permute-start | bytes 3145736 | tf_op jit(solution)/shard_map/ppermute | solution.py:148
  81.8 0.2 collective-permute-start.5
  82.0 20.9 %collective-permute-done.3 = bf16[128,4096]{1,0:T(8,128)(2,1)S(1)} collective-permute-done((bf16[128,4096]{1,0:T(8,128)(2,1)}, bf16[128,4096]{1,0:T(8,128)(2,1)S(1)}, u32[]{:S(2)}, u32[]{:S(2)}) %collective-permute-start.3) | collective-permute-done | bytes 1048608 | tf_op jit(solution)/shard_map/ppermute | solution.py:148
  102.9 24.3 %collective-permute-done.4 = bf16[128,4096]{1,0:T(8,128)(2,1)S(1)} collective-permute-done((bf16[128,4096]{1,0:T(8,128)(2,1)}, bf16[128,4096]{1,0:T(8,128)(2,1)S(1)}, u32[]{:S(2)}, u32[]{:S(2)}) %collective-permute-start.4) | collective-permute-done | bytes 1048608 | tf_op jit(solution)/shard_map/ppermute | solution.py:148
  127.2 2.0 convert_add_fusion
  129.2 0.0 copy-start.3
  129.2 0.0 reduce-scatter.5.cloned.1.call-update
  129.2 0.5 broadcast.243
  129.7 0.1 copy-done.5
  129.9 0.7 fusion.53
  130.6 0.3 copy.21
  130.9 0.1 reshape.230
  131.0 0.1 iota_compare_fusion
  131.1 1.0 copy.18
  132.1 38.6 %reduce-scatter.5.cloned.1.call-done = f32[16,4096]{1,0:T(8,128)} async-done(((f32[128,4096]{1,0:T(8,128)}), f32[16,4096]{1,0:T(8,128)}) %reduce-scatter.5.cloned.1.call-update) | async-done | bytes 262160 | tf_op jit(solution)/shard_map/reduce_scatter | solution.py:187
  170.7 1.0 copy.19
  171.7 2.2 %multiply_bitcast_fusion.1 = (f32[4,8,32,128]{3,1,2,0:T(8,128)S(1)}, f32[1,32,4096]{2,1,0:T(8,128)}, f32[1,32,4096]{2,1,0:T(8,128)}, f32[4,8,32,128]{3,1,2,0:T(8,128)S(1)}) fusion(f32[1,32,4096]{2,1,0:T(8,128)S(1)} %copy-done.3, f32[1,16,4096]{2,1,0:T(8,128)} %bitcast.64, f32[1,16,4096]{2,1,0:T(8,128)} %bitcast.62, f32[1,32,4096]{2,1,0:T(8,128)S(1)} %copy-done.4), kind=kLoop, calls=%fused_computation.20 | loop fusion | flops 1179648 | bytes 3670016
  173.9 0.1 copy.17
  174.0 0.1 copy.20
  174.2 0.3 fusion.3
  174.5 0.6 fusion.8
  175.1 0.6 convolution_bitcast_fusion
  175.7 0.1 reshape.229
  175.8 0.1 reshape.228
  175.9 0.6 fusion.7
  176.5 1.3 gather_fusion
  177.8 0.8 select_select_fusion
  178.6 9.4 %all-to-all-start = ((bf16[8,16,512]{2,1,0:T(8,128)(2,1)}), bf16[8,16,512]{2,1,0:T(8,128)(2,1)S(1)}, u32[]{:S(2)}, u32[]{:S(2)}) async-start(bf16[8,16,512]{2,1,0:T(8,128)(2,1)} %select_select_fusion), calls=%async_computation.2 | async-start | bytes 262144 | tf_op jit(solution)/shard_map/all_to_all | solution.py:204
  188.0 0.9 multiply_subtract_fusion
  188.8 4.4 %all-to-all-done = bf16[8,16,512]{2,1,0:T(8,128)(2,1)S(1)} async-done(((bf16[8,16,512]{2,1,0:T(8,128)(2,1)}), bf16[8,16,512]{2,1,0:T(8,128)(2,1)S(1)}, u32[]{:S(2)}, u32[]{:S(2)}) %all-to-all-start) | async-done | bytes 131104 | tf_op jit(solution)/shard_map/all_to_all | solution.py:204
  193.2 0.7 copy.36
  (23 shorter events, 0.1 us)
Async XLA Ops:
  7.2 123.9 %reduce-scatter.3.cloned.1.call-start = ((), (), s32[]{:S(2)}) async-start(), calls=%async_computation.3 | async-start | bytes 2359296 | tf_op jit(solution)/shard_map/reduce_scatter | solution.py:187
  24.6 24.2 %collective-permute-start = (bf16[128,4096]{1,0:T(8,128)(2,1)}, bf16[128,4096]{1,0:T(8,128)(2,1)S(1)}, u32[]{:S(2)}, u32[]{:S(2)}) collective-permute-start(bf16[128,4096]{1,0:T(8,128)(2,1)} %get-tuple-element.21), channel_id=1, source_target_pairs={{0,64},{64,128},{128,192},{192,0},{1,65},{65,129},{129,193},{193,1... | collective-permute-start | bytes 3145736 | tf_op jit(solution)/shard_map/ppermute | solution.py:148
  26.6 47.7 %collective-permute-start.1 = (bf16[128,4096]{1,0:T(8,128)(2,1)}, bf16[128,4096]{1,0:T(8,128)(2,1)S(1)}, u32[]{:S(2)}, u32[]{:S(2)}) collective-permute-start(bf16[128,4096]{1,0:T(8,128)(2,1)} %get-tuple-element.22), channel_id=1, source_target_pairs={{0,128},{64,192},{128,0},{192,64},{1,129},{65,193},{129,1},{193,65... | collective-permute-start | bytes 3145736 | tf_op jit(solution)/shard_map/ppermute | solution.py:148
  29.0 45.3 %copy-start.2 = (bf16[128,4096]{1,0:T(8,128)(2,1)S(1)}, bf16[128,4096]{1,0:T(8,128)(2,1)}, u32[]{:S(2)}) copy-start(bf16[128,4096]{1,0:T(8,128)(2,1)} %get-tuple-element.28) | copy-start | bytes 3145732
  29.0 45.3 %collective-permute-start.2 = (bf16[128,4096]{1,0:T(8,128)(2,1)}, bf16[128,4096]{1,0:T(8,128)(2,1)}, u32[]{:S(2)}, u32[]{:S(2)}) collective-permute-start(bf16[128,4096]{1,0:T(8,128)(2,1)} %get-tuple-element.23), channel_id=1, source_target_pairs={{0,192},{64,0},{128,64},{192,128},{1,193},{65,1},{129,65},{193,129... | collective-permute-start | bytes 3145736 | tf_op jit(solution)/shard_map/ppermute | solution.py:148
  77.5 4.3 %copy-start.8 = (bf16[128,4096]{1,0:T(8,128)(2,1)S(1)}, bf16[128,4096]{1,0:T(8,128)(2,1)}, u32[]{:S(2)}) copy-start(bf16[128,4096]{1,0:T(8,128)(2,1)} %get-tuple-element.35) | copy-start | bytes 3145732
  77.5 49.7 %copy-start.1 = (bf16[128,4096]{1,0:T(8,128)(2,1)S(1)}, bf16[128,4096]{1,0:T(8,128)(2,1)}, u32[]{:S(2)}) copy-start(bf16[128,4096]{1,0:T(8,128)(2,1)} %get-tuple-element.32) | copy-start | bytes 3145732
  77.5 93.2 %reduce-scatter.5.cloned.1.call-start = ((), (), s32[]{:S(2)}) async-start(), calls=%async_computation.4 | async-start | bytes 2359296 | tf_op jit(solution)/shard_map/reduce_scatter | solution.py:187
  77.6 25.3 %collective-permute-start.3 = (bf16[128,4096]{1,0:T(8,128)(2,1)}, bf16[128,4096]{1,0:T(8,128)(2,1)S(1)}, u32[]{:S(2)}, u32[]{:S(2)}) collective-permute-start(bf16[128,4096]{1,0:T(8,128)(2,1)} %get-tuple-element.33), channel_id=1, source_target_pairs={{0,64},{64,128},{128,192},{192,0},{1,65},{65,129},{129,193},{193,1... | collective-permute-start | bytes 3145736 | tf_op jit(solution)/shard_map/ppermute | solution.py:148
  78.8 48.4 %collective-permute-start.4 = (bf16[128,4096]{1,0:T(8,128)(2,1)}, bf16[128,4096]{1,0:T(8,128)(2,1)S(1)}, u32[]{:S(2)}, u32[]{:S(2)}) collective-permute-start(bf16[128,4096]{1,0:T(8,128)(2,1)} %get-tuple-element.34), channel_id=1, source_target_pairs={{0,128},{64,192},{128,0},{192,64},{1,129},{65,193},{129,1},{193,65... | collective-permute-start | bytes 3145736 | tf_op jit(solution)/shard_map/ppermute | solution.py:148
  81.8 45.4 %collective-permute-start.5 = (bf16[128,4096]{1,0:T(8,128)(2,1)S(1)}, bf16[128,4096]{1,0:T(8,128)(2,1)S(1)}, u32[]{:S(2)}, u32[]{:S(2)}) collective-permute-start(bf16[128,4096]{1,0:T(8,128)(2,1)S(1)} %copy-done.8), channel_id=1, source_target_pairs={{0,192},{64,0},{128,64},{192,128},{1,193},{65,1},{129,65},{193,129... | collective-permute-start | bytes 3145736 | tf_op jit(solution)/shard_map/ppermute | solution.py:148
  129.2 0.7 copy-start.5
  129.2 1.4 copy-start
  129.2 1.8 copy-start.6
  129.2 1.9 copy-start.7
  129.2 42.5 %copy-start.3 = (f32[1,32,4096]{2,1,0:T(8,128)S(1)}, f32[1,32,4096]{2,1,0:T(8,128)}, u32[]{:S(2)}) copy-start(f32[1,32,4096]{2,1,0:T(8,128)} %param.11) | copy-start | bytes 1572868
  129.2 42.5 %copy-start.4 = (f32[1,32,4096]{2,1,0:T(8,128)S(1)}, f32[1,32,4096]{2,1,0:T(8,128)}, u32[]{:S(2)}) copy-start(f32[1,32,4096]{2,1,0:T(8,128)} %param.12) | copy-start | bytes 1572868
  178.6 14.6 %all-to-all-start = ((bf16[8,16,512]{2,1,0:T(8,128)(2,1)}), bf16[8,16,512]{2,1,0:T(8,128)(2,1)S(1)}, u32[]{:S(2)}, u32[]{:S(2)}) async-start(bf16[8,16,512]{2,1,0:T(8,128)(2,1)} %select_select_fusion), calls=%async_computation.2 | async-start | bytes 262144 | tf_op jit(solution)/shard_map/all_to_all | solution.py:204
Sparse Core Ops, SparseCore 0:
  77.6 42.0 reduce-scatter.2
  129.3 41.3 reduce-scatter.4

commit v7 on v6

--- a/solution.py
+++ b/solution.py
@@ -2,6 +2,7 @@
 import math
 
 import jax
+import numpy as np
 import jax.numpy as jnp
 from jax import lax
 from jax.experimental import pallas as pl
@@ -82,12 +83,26 @@
     return up, down
 
 
-def code_rows(y_ref, sh_ref, o_ref, group_rows, g, carry):
+def walsh_constant(table_order):
+    positions = np.arange(table_order)
+    common_bits = np.bitwise_and(positions[:, None], positions[None, :])
+    parity = np.zeros((table_order, table_order), np.int64)
+    for bit_level in range(max(table_order.bit_length() - 1, 1)):
+        parity = parity + np.right_shift(common_bits, bit_level) % 2
+    return jnp.asarray((1 - 2 * (parity % 2)).astype(np.float32), dtype=jnp.bfloat16)
+
+
+def code_rows(y_ref, sh_ref, o_ref, group_rows, first_row, g, carry):
     rows = pl.ds(pl.multiple_of(g * 8, 8), 8)
     dest = g // (group_rows // 8)
-    within = pl.ds(pl.multiple_of((g % (group_rows // 8)) * 8, 8), 8)
+    within = (g % (group_rows // 8)) * 8
     blocks = butterfly([y_ref[rows, a * HB:(a + 1) * HB] for a in range(HA)])
-    up, dn = exact_powers(sh_ref[dest, within, :])
+    base = first_row(dest) + within
+    row_ids = lax.broadcasted_iota(jnp.int32, (8, 1), 0)
+    shift_col = jnp.zeros((8, 1), jnp.int32)
+    for j in range(8):
+        shift_col = jnp.where(row_ids == j, sh_ref[0, 0, base + j], shift_col)
+    up, dn = exact_powers(shift_col)
     up = up * (1.0 / math.sqrt(HA * HB))
     for a in range(HA):
         coded = jnp.clip(blocks[a] * up, -127.0, 127.0).astype(jnp.bfloat16)
@@ -95,39 +110,42 @@
     return carry
 
 
-def code_kernel(mx_ref, x_ref, sg_ref, w_ref, sh_ref, *refs):
+def code_kernel(part, x_size, mx_ref, sh_ref, x_ref, sg_ref, w_ref, *refs):
     out_refs, y_ref = refs[:-1], refs[-1]
     step = pl.program_id(0)
     groups, group_rows, _ = x_ref.shape
+    dest_rows = group_rows * PARTS
+    first_dest = ((mx_ref[0] + step) % x_size) * groups
+    first_row = lambda dest: (first_dest + dest) * dest_rows + part * group_rows
     for a in range(HA):
         cols = slice(a * HB, (a + 1) * HB)
-        lhs = (x_ref[:, :, cols] * sg_ref[:, cols]).reshape(groups * group_rows, HB)
+        sign = (2 * sg_ref[:, cols] - 1).astype(jnp.float32).astype(jnp.bfloat16)
+        lhs = (x_ref[:, :, cols] * sign).reshape(groups * group_rows, HB)
         y_ref[:, cols] = jnp.dot(lhs, w_ref[...], preferred_element_type=jnp.float32)
     for k, o_ref in enumerate(out_refs):
 
         @pl.when(step == k)
         def _(o_ref=o_ref):
-            coder = functools.partial(code_rows, y_ref, sh_ref, o_ref, group_rows)
+            coder = functools.partial(code_rows, y_ref, sh_ref, o_ref, group_rows, first_row)
             lax.fori_loop(0, groups * group_rows // 8, coder, 0)
 
 
-def decoded_terms(grad_groups, sign_row, walsh, shift_groups, part, x_size):
+def decoded_terms(grad_groups, signs, walsh, shifts, part, x_size):
     dests, _, part_rows, width = grad_groups.shape
     per_x = dests // x_size
     my_x = jnp.reshape(lax.axis_index("wx"), (1,)).astype(jnp.int32)
-    tile = lambda i, mx: ((mx[0] + i) % x_size, part, 0, 0)
-    whole = lambda i, mx: (0, 0)
+    tile = lambda i, mx, sh: ((mx[0] + i) % x_size, part, 0, 0)
+    whole = lambda i, mx, sh: (0, 0)
     out_rows = per_x * part_rows
     return pl.pallas_call(
-        code_kernel,
+        functools.partial(code_kernel, part, x_size),
         grid_spec=pltpu.PrefetchScalarGridSpec(
-            num_scalar_prefetch=1,
+            num_scalar_prefetch=2,
             grid=(x_size,),
             in_specs=[
                 pl.BlockSpec((per_x, None, part_rows, width), tile),
                 pl.BlockSpec((1, width), whole),
                 pl.BlockSpec((HB, HB), whole),
-                pl.BlockSpec((per_x, None, part_rows, 1), tile),
             ],
             out_specs=[pl.BlockSpec((out_rows, width), whole) for _ in range(x_size)],
             scratch_shapes=[pltpu.VMEM((out_rows, width), jnp.float32)],
@@ -138,7 +156,7 @@
             transcendentals=0,
             bytes_accessed=dests * part_rows * width * 4,
         ),
-    )(my_x, grad_groups, sign_row, walsh, shift_groups)
+    )(my_x, shifts, grad_groups, signs, walsh)
 
 
 def send_along_x(terms, x_size):
@@ -165,23 +183,19 @@
 def per_device(grads, signs, shifts, first, second, weights, slots, counts):
     sign_vec = (2 * signs[0] - 1).astype(jnp.float32)
     grad_rows = grads[0, 0]
-    shift_rows = shifts[0, 0]
     blocks = first.shape[1]
-    sign_row = sign_vec.astype(jnp.bfloat16)[None, :]
-    walsh = walsh_table(HB).astype(jnp.bfloat16)
+    walsh = walsh_constant(HB)
     x_size = lax.axis_size("wx")
     dests = x_size * lax.axis_size("wz")
     workers = dests
     part_rows = blocks // PARTS
-    as_groups = lambda rows: rows.reshape(dests, PARTS, part_rows, rows.shape[-1])
-    grad_groups = as_groups(grad_rows)
-    shift_groups = as_groups(shift_rows[:, None])
+    grad_groups = grad_rows.reshape(dests, PARTS, part_rows, grad_rows.shape[-1])
     pieces = []
-    terms = decoded_terms(grad_groups, sign_row, walsh, shift_groups, 0, x_size)
+    terms = decoded_terms(grad_groups, signs, walsh, shifts, 0, x_size)
     arrived = send_along_x(terms, x_size)
     for part in range(1, PARTS + 1):
         if part < PARTS:
-            terms = decoded_terms(grad_groups, sign_row, walsh, shift_groups, part, x_size)
+            terms = decoded_terms(grad_groups, signs, walsh, shifts, part, x_size)
             arrived, terms = lax.optimization_barrier((arrived, terms))
         partial = sum_arrived(arrived)
         pieces.append(lax.psum_scatter(partial, "wz", scatter_dimension=0, tiled=True))

time: 201 us -> 194 us (0.965)
  Pallas kernels: 24.7 us -> 20.2 us
  other arithmetic: 14.1 us -> 10.7 us
    pallas_call x2, Pallas kernels: 24.7 us -> 20.2 us  [decoded_terms(): pl.pallas_call(functools.partial(code_kernel, part, x_size), grid_spec=pl...]
    ppermute x6, waiting for transfers between devices: 77 us -> 79.3 us  [send_along_x(): arrived.append(lax.ppermute(terms[step], 'wx', pairs))]
    convert_element_type x2 -> x0, other arithmetic: 2.02 us -> none  [the longest x1 1.34 us: per_device(): sign_row = sign_vec.astype(jnp.bfloat16)[None, :]]
  transfers between devices with their start and end apart: 9 -> 9, of which waited for: 6 -> 6; matrix products, arithmetic and copies ran while one was open for 3% -> 3% of each run, Pallas kernels for 6% -> 5%
where the time goes in v7:
time: 194 us; the launch traced here: 193 us
  waiting for transfers between devices  122 us (63%)
  Pallas kernels  20.2 us (10%)
  starting transfers between devices  19.4 us (10%)
  between operations  14.2 us (7%)
  other arithmetic  10.7 us (6%)
  local copies, waits for them, and re-layouts  5.48 us (3%)
    ppermute x6, waiting for transfers between devices, send_along_x(): arrived.append(lax.ppermute(terms[step], 'wx', pairs))  79.3 us
    reduce_scatter x2, waiting for transfers between devices, per_device(): lax.psum_scatter(partial, 'wz', scatter_dimension=0, tiled=True)  38.4 us
    pallas_call x2, Pallas kernels, decoded_terms(): pl.pallas_call(functools.partial(code_kernel, part, x_size), grid_spec=pl...  20.2 us
    ppermute x6, starting transfers between devices, send_along_x(): arrived.append(lax.ppermute(terms[step], 'wx', pairs))  10 us
    all_to_all x1, starting transfers between devices, per_device(): lax.all_to_all(chosen_pieces, 'tensor', split_axis=0, concat_axis=0, tile...  9.3 us
    add x2, other arithmetic, sum_arrived(): partial = partial + piece.astype(jnp.float32)  5.14 us
    all_to_all x1, waiting for transfers between devices, per_device(): lax.all_to_all(chosen_pieces, 'tensor', split_axis=0, concat_axis=0, tile...  4.36 us
  transfers between devices with their start and end apart: 9, of which 6 were waited for; matrix products, arithmetic and copies ran while one was open for 3% of the time, Pallas kernels for 5%

profile of v7, /device:TPU:1, one launch (start us, length us, event | category | flops | bytes accessed | tf_op | source)
XLA Modules:
  0.0 193.2 jit_solution(10794596731934215091)
XLA Ops:
  7.2 0.0 reduce-scatter.3.cloned.1.call-start
  7.2 10.1 %shard_map.120 = (bf16[128,4096]{1,0:T(8,128)(2,1)}, bf16[128,4096]{1,0:T(8,128)(2,1)}, bf16[128,4096]{1,0:T(8,128)(2,1)}, bf16[128,4096]{1,0:T(8,128)(2,1)}) custom-call(s32[1]{0:T(128)} %bitcast.mx_ref, s32[1,1,1024]{2,1,0:T(1,128)} %sh_ref.3, bf16[32,2,16,4096]{3,2,1,0:T(8,128)(2,1)} %bitcast.57, s32[1,4096]{1,0:T(1,128)} %sg_ref.3, ...), custom_call_target="tpu_custom_call" | custom-call | flops 553648128 | bytes 8388608 | tf_op jit(solution)/shard_map/pallas_call | solution.py:140
  17.3 2.0 %collective-permute-start = (bf16[128,4096]{1,0:T(8,128)(2,1)}, bf16[128,4096]{1,0:T(8,128)(2,1)S(1)}, u32[]{:S(2)}, u32[]{:S(2)}) collective-permute-start(bf16[128,4096]{1,0:T(8,128)(2,1)} %get-tuple-element.21), channel_id=1, source_target_pairs={{0,64},{64,128},{128,192},{192,0},{1,65},{65,129},{129,193},{193,1... | collective-permute-start | bytes 3145736 | tf_op jit(solution)/shard_map/ppermute | solution.py:166
  19.3 2.4 %collective-permute-start.1 = (bf16[128,4096]{1,0:T(8,128)(2,1)}, bf16[128,4096]{1,0:T(8,128)(2,1)S(1)}, u32[]{:S(2)}, u32[]{:S(2)}) collective-permute-start(bf16[128,4096]{1,0:T(8,128)(2,1)} %get-tuple-element.22), channel_id=1, source_target_pairs={{0,128},{64,192},{128,0},{192,64},{1,129},{65,193},{129,1},{193,65... | collective-permute-start | bytes 3145736 | tf_op jit(solution)/shard_map/ppermute | solution.py:166
  21.8 1.2 collective-permute-start.2
  22.9 10.1 %shard_map.121 = (bf16[128,4096]{1,0:T(8,128)(2,1)}, bf16[128,4096]{1,0:T(8,128)(2,1)}, bf16[128,4096]{1,0:T(8,128)(2,1)}, bf16[128,4096]{1,0:T(8,128)(2,1)}) custom-call(s32[1]{0:T(128)} %bitcast.mx_ref, s32[1,1,1024]{2,1,0:T(1,128)} %sh_ref.3, bf16[32,2,16,4096]{3,2,1,0:T(8,128)(2,1)} %bitcast.58, s32[1,4096]{1,0:T(1,128)} %sg_ref.3, ...), custom_call_target="tpu_custom_call" | custom-call | flops 553648128 | bytes 8388608 | tf_op jit(solution)/shard_map/pallas_call | solution.py:140
  33.0 8.5 %collective-permute-done = bf16[128,4096]{1,0:T(8,128)(2,1)S(1)} collective-permute-done((bf16[128,4096]{1,0:T(8,128)(2,1)}, bf16[128,4096]{1,0:T(8,128)(2,1)S(1)}, u32[]{:S(2)}, u32[]{:S(2)}) %collective-permute-start) | collective-permute-done | bytes 1048608 | tf_op jit(solution)/shard_map/ppermute | solution.py:166
  41.5 25.6 %collective-permute-done.1 = bf16[128,4096]{1,0:T(8,128)(2,1)S(1)} collective-permute-done((bf16[128,4096]{1,0:T(8,128)(2,1)}, bf16[128,4096]{1,0:T(8,128)(2,1)S(1)}, u32[]{:S(2)}, u32[]{:S(2)}) %collective-permute-start.1) | collective-permute-done | bytes 1048608 | tf_op jit(solution)/shard_map/ppermute | solution.py:166
  67.0 0.0 collective-permute-done.2
  67.0 3.2 %convert_add_fusion.1 = f32[128,4096]{1,0:T(8,128)} fusion(bf16[128,4096]{1,0:T(8,128)(2,1)} %collective-permute-done.2, bf16[128,4096]{1,0:T(8,128)(2,1)S(1)} %collective-permute-done.1, bf16[128,4096]{1,0:T(8,128)(2,1)S(1)} %collective-permute-done, bf16[128,4096]{1,0:T(8,128)(2,1)S(1)} %copy-done.2), kind=kLoop, calls=%fused_computation.2 | loop fusion | flops 3670016 | bytes 6291456 | tf_op jit(solution)/shard_map/add | solution.py:173
  70.2 0.0 reduce-scatter.3.cloned.1.call-update
  70.3 0.0 reduce-scatter.5.cloned.1.call-start
  70.3 1.2 collective-permute-start.3
  71.5 3.0 %collective-permute-start.4 = (bf16[128,4096]{1,0:T(8,128)(2,1)}, bf16[128,4096]{1,0:T(8,128)(2,1)S(1)}, u32[]{:S(2)}, u32[]{:S(2)}) collective-permute-start(bf16[128,4096]{1,0:T(8,128)(2,1)} %get-tuple-element.34), channel_id=1, source_target_pairs={{0,128},{64,192},{128,0},{192,64},{1,129},{65,193},{129,1},{193,65... | collective-permute-start | bytes 3145736 | tf_op jit(solution)/shard_map/ppermute | solution.py:166
  74.5 0.0 copy-done.8
  74.5 0.2 collective-permute-start.5
  74.7 20.9 %collective-permute-done.3 = bf16[128,4096]{1,0:T(8,128)(2,1)S(1)} collective-permute-done((bf16[128,4096]{1,0:T(8,128)(2,1)}, bf16[128,4096]{1,0:T(8,128)(2,1)S(1)}, u32[]{:S(2)}, u32[]{:S(2)}) %collective-permute-start.3) | collective-permute-done | bytes 1048608 | tf_op jit(solution)/shard_map/ppermute | solution.py:166
  95.6 24.3 %collective-permute-done.4 = bf16[128,4096]{1,0:T(8,128)(2,1)S(1)} collective-permute-done((bf16[128,4096]{1,0:T(8,128)(2,1)}, bf16[128,4096]{1,0:T(8,128)(2,1)S(1)}, u32[]{:S(2)}, u32[]{:S(2)}) %collective-permute-start.4) | collective-permute-done | bytes 1048608 | tf_op jit(solution)/shard_map/ppermute | solution.py:166
  119.9 0.0 collective-permute-done.5
  119.9 1.9 %convert_add_fusion = f32[128,4096]{1,0:T(8,128)} fusion(bf16[128,4096]{1,0:T(8,128)(2,1)S(1)} %collective-permute-done.5, bf16[128,4096]{1,0:T(8,128)(2,1)S(1)} %collective-permute-done.4, bf16[128,4096]{1,0:T(8,128)(2,1)S(1)} %collective-permute-done.3, bf16[128,4096]{1,0:T(8,128)(2,1)S(1)} %copy-done.1), kind=kLoop, calls=%fused_computation.1 | loop fusion | flops 3670016 | bytes 6291456 | tf_op jit(solution)/shard_map/add | solution.py:173
  121.9 0.0 copy-start.3
  121.9 0.0 copy-start.4
  121.9 0.0 reduce-scatter.5.cloned.1.call-update
  121.9 0.5 broadcast.179
  122.5 0.1 copy-done.5
  122.6 0.7 fusion.86
  123.3 0.0 copy-done
  123.3 0.3 copy.20
  123.7 0.1 reshape.230
  123.8 0.1 iota_compare_fusion
  123.8 1.0 copy.17
  124.9 38.4 %reduce-scatter.5.cloned.1.call-done = f32[16,4096]{1,0:T(8,128)} async-done(((f32[128,4096]{1,0:T(8,128)}), f32[16,4096]{1,0:T(8,128)}) %reduce-scatter.5.cloned.1.call-update) | async-done | bytes 262160 | tf_op jit(solution)/shard_map/reduce_scatter | solution.py:201
  163.2 1.0 copy.18
  164.3 2.2 %multiply_bitcast_fusion.1 = (f32[4,8,32,128]{3,1,2,0:T(8,128)S(1)}, f32[1,32,4096]{2,1,0:T(8,128)}, f32[1,32,4096]{2,1,0:T(8,128)}, f32[4,8,32,128]{3,1,2,0:T(8,128)S(1)}) fusion(f32[1,32,4096]{2,1,0:T(8,128)S(1)} %copy-done.3, f32[1,16,4096]{2,1,0:T(8,128)} %bitcast.64, f32[1,16,4096]{2,1,0:T(8,128)} %bitcast.62, f32[1,32,4096]{2,1,0:T(8,128)S(1)} %copy-done.4), kind=kLoop, calls=%fused_computation.20 | loop fusion | flops 1179648 | bytes 3670016
  166.5 0.1 copy.16
  166.6 0.1 copy.19
  166.7 0.3 fusion.3
  167.0 0.6 fusion.8
  167.6 0.6 convolution_bitcast_fusion
  168.2 0.1 reshape.229
  168.3 0.1 reshape.228
  168.4 0.6 fusion.7
  169.0 1.3 gather_fusion
  170.4 0.8 select_select_fusion
  171.1 9.3 %all-to-all-start = ((bf16[8,16,512]{2,1,0:T(8,128)(2,1)}), bf16[8,16,512]{2,1,0:T(8,128)(2,1)S(1)}, u32[]{:S(2)}, u32[]{:S(2)}) async-start(bf16[8,16,512]{2,1,0:T(8,128)(2,1)} %select_select_fusion), calls=%async_computation.2 | async-start | bytes 262144 | tf_op jit(solution)/shard_map/all_to_all | solution.py:218
  180.4 0.9 multiply_subtract_fusion
  181.3 4.4 %all-to-all-done = bf16[8,16,512]{2,1,0:T(8,128)(2,1)S(1)} async-done(((bf16[8,16,512]{2,1,0:T(8,128)(2,1)}), bf16[8,16,512]{2,1,0:T(8,128)(2,1)S(1)}, u32[]{:S(2)}, u32[]{:S(2)}) %all-to-all-start) | async-done | bytes 131104 | tf_op jit(solution)/shard_map/all_to_all | solution.py:218
  185.7 0.7 copy.35
  (18 shorter events, 0.1 us)
Async XLA Ops:
  7.2 116.7 %reduce-scatter.3.cloned.1.call-start = ((), (), s32[]{:S(2)}) async-start(), calls=%async_computation.3 | async-start | bytes 2359296 | tf_op jit(solution)/shard_map/reduce_scatter | solution.py:201
  17.3 24.2 %collective-permute-start = (bf16[128,4096]{1,0:T(8,128)(2,1)}, bf16[128,4096]{1,0:T(8,128)(2,1)S(1)}, u32[]{:S(2)}, u32[]{:S(2)}) collective-permute-start(bf16[128,4096]{1,0:T(8,128)(2,1)} %get-tuple-element.21), channel_id=1, source_target_pairs={{0,64},{64,128},{128,192},{192,0},{1,65},{65,129},{129,193},{193,1... | collective-permute-start | bytes 3145736 | tf_op jit(solution)/shard_map/ppermute | solution.py:166
  19.3 47.7 %collective-permute-start.1 = (bf16[128,4096]{1,0:T(8,128)(2,1)}, bf16[128,4096]{1,0:T(8,128)(2,1)S(1)}, u32[]{:S(2)}, u32[]{:S(2)}) collective-permute-start(bf16[128,4096]{1,0:T(8,128)(2,1)} %get-tuple-element.22), channel_id=1, source_target_pairs={{0,128},{64,192},{128,0},{192,64},{1,129},{65,193},{129,1},{193,65... | collective-permute-start | bytes 3145736 | tf_op jit(solution)/shard_map/ppermute | solution.py:166
  21.8 45.3 %copy-start.2 = (bf16[128,4096]{1,0:T(8,128)(2,1)S(1)}, bf16[128,4096]{1,0:T(8,128)(2,1)}, u32[]{:S(2)}) copy-start(bf16[128,4096]{1,0:T(8,128)(2,1)} %get-tuple-element.28) | copy-start | bytes 3145732
  21.8 45.3 %collective-permute-start.2 = (bf16[128,4096]{1,0:T(8,128)(2,1)}, bf16[128,4096]{1,0:T(8,128)(2,1)}, u32[]{:S(2)}, u32[]{:S(2)}) collective-permute-start(bf16[128,4096]{1,0:T(8,128)(2,1)} %get-tuple-element.23), channel_id=1, source_target_pairs={{0,192},{64,0},{128,64},{192,128},{1,193},{65,1},{129,65},{193,129... | collective-permute-start | bytes 3145736 | tf_op jit(solution)/shard_map/ppermute | solution.py:166
  70.2 4.3 %copy-start.8 = (bf16[128,4096]{1,0:T(8,128)(2,1)S(1)}, bf16[128,4096]{1,0:T(8,128)(2,1)}, u32[]{:S(2)}) copy-start(bf16[128,4096]{1,0:T(8,128)(2,1)} %get-tuple-element.35) | copy-start | bytes 3145732
  70.2 49.7 %copy-start.1 = (bf16[128,4096]{1,0:T(8,128)(2,1)S(1)}, bf16[128,4096]{1,0:T(8,128)(2,1)}, u32[]{:S(2)}) copy-start(bf16[128,4096]{1,0:T(8,128)(2,1)} %get-tuple-element.32) | copy-start | bytes 3145732
  70.3 93.0 %reduce-scatter.5.cloned.1.call-start = ((), (), s32[]{:S(2)}) async-start(), calls=%async_computation.4 | async-start | bytes 2359296 | tf_op jit(solution)/shard_map/reduce_scatter | solution.py:201
  70.3 25.3 %collective-permute-start.3 = (bf16[128,4096]{1,0:T(8,128)(2,1)}, bf16[128,4096]{1,0:T(8,128)(2,1)S(1)}, u32[]{:S(2)}, u32[]{:S(2)}) collective-permute-start(bf16[128,4096]{1,0:T(8,128)(2,1)} %get-tuple-element.33), channel_id=1, source_target_pairs={{0,64},{64,128},{128,192},{192,0},{1,65},{65,129},{129,193},{193,1... | collective-permute-start | bytes 3145736 | tf_op jit(solution)/shard_map/ppermute | solution.py:166
  71.5 48.4 %collective-permute-start.4 = (bf16[128,4096]{1,0:T(8,128)(2,1)}, bf16[128,4096]{1,0:T(8,128)(2,1)S(1)}, u32[]{:S(2)}, u32[]{:S(2)}) collective-permute-start(bf16[128,4096]{1,0:T(8,128)(2,1)} %get-tuple-element.34), channel_id=1, source_target_pairs={{0,128},{64,192},{128,0},{192,64},{1,129},{65,193},{129,1},{193,65... | collective-permute-start | bytes 3145736 | tf_op jit(solution)/shard_map/ppermute | solution.py:166
  74.5 45.4 %collective-permute-start.5 = (bf16[128,4096]{1,0:T(8,128)(2,1)S(1)}, bf16[128,4096]{1,0:T(8,128)(2,1)S(1)}, u32[]{:S(2)}, u32[]{:S(2)}) collective-permute-start(bf16[128,4096]{1,0:T(8,128)(2,1)S(1)} %copy-done.8), channel_id=1, source_target_pairs={{0,192},{64,0},{128,64},{192,128},{1,193},{65,1},{129,65},{193,129... | collective-permute-start | bytes 3145736 | tf_op jit(solution)/shard_map/ppermute | solution.py:166
  121.9 0.7 copy-start.5
  121.9 1.4 copy-start
  121.9 1.8 copy-start.6
  121.9 1.9 copy-start.7
  121.9 42.3 %copy-start.3 = (f32[1,32,4096]{2,1,0:T(8,128)S(1)}, f32[1,32,4096]{2,1,0:T(8,128)}, u32[]{:S(2)}) copy-start(f32[1,32,4096]{2,1,0:T(8,128)} %param.12) | copy-start | bytes 1572868
  121.9 42.3 %copy-start.4 = (f32[1,32,4096]{2,1,0:T(8,128)S(1)}, f32[1,32,4096]{2,1,0:T(8,128)}, u32[]{:S(2)}) copy-start(f32[1,32,4096]{2,1,0:T(8,128)} %param.13) | copy-start | bytes 1572868
  171.1 14.5 %all-to-all-start = ((bf16[8,16,512]{2,1,0:T(8,128)(2,1)}), bf16[8,16,512]{2,1,0:T(8,128)(2,1)S(1)}, u32[]{:S(2)}, u32[]{:S(2)}) async-start(bf16[8,16,512]{2,1,0:T(8,128)(2,1)} %select_select_fusion), calls=%async_computation.2 | async-start | bytes 262144 | tf_op jit(solution)/shard_map/all_to_all | solution.py:218
Sparse Core Ops, SparseCore 0:
  70.4 42.0 reduce-scatter.2
  122.1 41.1 reduce-scatter.4

commit v8 on v7

--- a/solution.py
+++ b/solution.py
@@ -104,9 +104,10 @@
         shift_col = jnp.where(row_ids == j, sh_ref[0, 0, base + j], shift_col)
     up, dn = exact_powers(shift_col)
     up = up * (1.0 / math.sqrt(HA * HB))
+    dn = dn.astype(jnp.bfloat16)
     for a in range(HA):
         coded = jnp.clip(blocks[a] * up, -127.0, 127.0).astype(jnp.bfloat16)
-        o_ref[rows, a * HB:(a + 1) * HB] = (coded.astype(jnp.float32) * dn).astype(o_ref.dtype)
+        o_ref[rows, a * HB:(a + 1) * HB] = (coded * dn).astype(o_ref.dtype)
     return carry
 
 

time: 194 us -> 193 us (level)
  no operation moved by 1% of the time
where the time goes in v8:
time: 193 us
  waiting for transfers between devices  123 us (64%)
  starting transfers between devices  19.4 us (10%)
  Pallas kernels  18.9 us (10%)
  between operations  14.2 us (7%)
  other arithmetic  10.7 us (6%)
  local copies, waits for them, and re-layouts  5.48 us (3%)
    ppermute x6, waiting for transfers between devices, send_along_x(): arrived.append(lax.ppermute(terms[step], 'wx', pairs))  79.9 us
    reduce_scatter x2, waiting for transfers between devices, per_device(): lax.psum_scatter(partial, 'wz', scatter_dimension=0, tiled=True)  38.4 us
    pallas_call x2, Pallas kernels, decoded_terms(): pl.pallas_call(functools.partial(code_kernel, part, x_size), grid_spec=pl...  18.9 us
    ppermute x6, starting transfers between devices, send_along_x(): arrived.append(lax.ppermute(terms[step], 'wx', pairs))  10 us
    all_to_all x1, starting transfers between devices, per_device(): lax.all_to_all(chosen_pieces, 'tensor', split_axis=0, concat_axis=0, tile...  9.3 us
    add x2, other arithmetic, sum_arrived(): partial = partial + piece.astype(jnp.float32)  5.14 us
    all_to_all x1, waiting for transfers between devices, per_device(): lax.all_to_all(chosen_pieces, 'tensor', split_axis=0, concat_axis=0, tile...  4.36 us
  transfers between devices with their start and end apart: 9, of which 6 were waited for; matrix products, arithmetic and copies ran while one was open for 3% of the time, Pallas kernels for 5%

profile of v8, /device:TPU:1, one launch (start us, length us, event | category | flops | bytes accessed | tf_op | source)
XLA Modules:
  0.0 192.5 jit_solution(16786410093262085277)
XLA Ops:
  7.2 0.0 reduce-scatter.3.cloned.1.call-start
  7.2 9.4 %shard_map.120 = (bf16[128,4096]{1,0:T(8,128)(2,1)}, bf16[128,4096]{1,0:T(8,128)(2,1)}, bf16[128,4096]{1,0:T(8,128)(2,1)}, bf16[128,4096]{1,0:T(8,128)(2,1)}) custom-call(s32[1]{0:T(128)} %bitcast.mx_ref, s32[1,1,1024]{2,1,0:T(1,128)} %sh_ref.3, bf16[32,2,16,4096]{3,2,1,0:T(8,128)(2,1)} %bitcast.57, s32[1,4096]{1,0:T(1,128)} %sg_ref.3, ...), custom_call_target="tpu_custom_call" | custom-call | flops 553648128 | bytes 8388608 | tf_op jit(solution)/shard_map/pallas_call | solution.py:141
  16.7 2.0 %collective-permute-start = (bf16[128,4096]{1,0:T(8,128)(2,1)}, bf16[128,4096]{1,0:T(8,128)(2,1)S(1)}, u32[]{:S(2)}, u32[]{:S(2)}) collective-permute-start(bf16[128,4096]{1,0:T(8,128)(2,1)} %get-tuple-element.21), channel_id=1, source_target_pairs={{0,64},{64,128},{128,192},{192,0},{1,65},{65,129},{129,193},{193,1... | collective-permute-start | bytes 3145736 | tf_op jit(solution)/shard_map/ppermute | solution.py:167
  18.7 2.4 %collective-permute-start.1 = (bf16[128,4096]{1,0:T(8,128)(2,1)}, bf16[128,4096]{1,0:T(8,128)(2,1)S(1)}, u32[]{:S(2)}, u32[]{:S(2)}) collective-permute-start(bf16[128,4096]{1,0:T(8,128)(2,1)} %get-tuple-element.22), channel_id=1, source_target_pairs={{0,128},{64,192},{128,0},{192,64},{1,129},{65,193},{129,1},{193,65... | collective-permute-start | bytes 3145736 | tf_op jit(solution)/shard_map/ppermute | solution.py:167
  21.1 1.2 collective-permute-start.2
  22.3 9.5 %shard_map.121 = (bf16[128,4096]{1,0:T(8,128)(2,1)}, bf16[128,4096]{1,0:T(8,128)(2,1)}, bf16[128,4096]{1,0:T(8,128)(2,1)}, bf16[128,4096]{1,0:T(8,128)(2,1)}) custom-call(s32[1]{0:T(128)} %bitcast.mx_ref, s32[1,1,1024]{2,1,0:T(1,128)} %sh_ref.3, bf16[32,2,16,4096]{3,2,1,0:T(8,128)(2,1)} %bitcast.58, s32[1,4096]{1,0:T(1,128)} %sg_ref.3, ...), custom_call_target="tpu_custom_call" | custom-call | flops 553648128 | bytes 8388608 | tf_op jit(solution)/shard_map/pallas_call | solution.py:141
  31.8 9.1 %collective-permute-done = bf16[128,4096]{1,0:T(8,128)(2,1)S(1)} collective-permute-done((bf16[128,4096]{1,0:T(8,128)(2,1)}, bf16[128,4096]{1,0:T(8,128)(2,1)S(1)}, u32[]{:S(2)}, u32[]{:S(2)}) %collective-permute-start) | collective-permute-done | bytes 1048608 | tf_op jit(solution)/shard_map/ppermute | solution.py:167
  40.8 25.6 %collective-permute-done.1 = bf16[128,4096]{1,0:T(8,128)(2,1)S(1)} collective-permute-done((bf16[128,4096]{1,0:T(8,128)(2,1)}, bf16[128,4096]{1,0:T(8,128)(2,1)S(1)}, u32[]{:S(2)}, u32[]{:S(2)}) %collective-permute-start.1) | collective-permute-done | bytes 1048608 | tf_op jit(solution)/shard_map/ppermute | solution.py:167
  66.4 0.0 collective-permute-done.2
  66.4 3.2 %convert_add_fusion.1 = f32[128,4096]{1,0:T(8,128)} fusion(bf16[128,4096]{1,0:T(8,128)(2,1)} %collective-permute-done.2, bf16[128,4096]{1,0:T(8,128)(2,1)S(1)} %collective-permute-done.1, bf16[128,4096]{1,0:T(8,128)(2,1)S(1)} %collective-permute-done, bf16[128,4096]{1,0:T(8,128)(2,1)S(1)} %copy-done.2), kind=kLoop, calls=%fused_computation.2 | loop fusion | flops 3670016 | bytes 6291456 | tf_op jit(solution)/shard_map/add | solution.py:174
  69.6 0.0 reduce-scatter.3.cloned.1.call-update
  69.6 0.0 reduce-scatter.5.cloned.1.call-start
  69.7 1.2 collective-permute-start.3
  70.9 3.0 %collective-permute-start.4 = (bf16[128,4096]{1,0:T(8,128)(2,1)}, bf16[128,4096]{1,0:T(8,128)(2,1)S(1)}, u32[]{:S(2)}, u32[]{:S(2)}) collective-permute-start(bf16[128,4096]{1,0:T(8,128)(2,1)} %get-tuple-element.34), channel_id=1, source_target_pairs={{0,128},{64,192},{128,0},{192,64},{1,129},{65,193},{129,1},{193,65... | collective-permute-start | bytes 3145736 | tf_op jit(solution)/shard_map/ppermute | solution.py:167
  73.9 0.0 copy-done.8
  73.9 0.2 collective-permute-start.5
  74.1 20.9 %collective-permute-done.3 = bf16[128,4096]{1,0:T(8,128)(2,1)S(1)} collective-permute-done((bf16[128,4096]{1,0:T(8,128)(2,1)}, bf16[128,4096]{1,0:T(8,128)(2,1)S(1)}, u32[]{:S(2)}, u32[]{:S(2)}) %collective-permute-start.3) | collective-permute-done | bytes 1048608 | tf_op jit(solution)/shard_map/ppermute | solution.py:167
  95.0 24.3 %collective-permute-done.4 = bf16[128,4096]{1,0:T(8,128)(2,1)S(1)} collective-permute-done((bf16[128,4096]{1,0:T(8,128)(2,1)}, bf16[128,4096]{1,0:T(8,128)(2,1)S(1)}, u32[]{:S(2)}, u32[]{:S(2)}) %collective-permute-start.4) | collective-permute-done | bytes 1048608 | tf_op jit(solution)/shard_map/ppermute | solution.py:167
  119.3 0.0 collective-permute-done.5
  119.3 1.9 %convert_add_fusion = f32[128,4096]{1,0:T(8,128)} fusion(bf16[128,4096]{1,0:T(8,128)(2,1)S(1)} %collective-permute-done.5, bf16[128,4096]{1,0:T(8,128)(2,1)S(1)} %collective-permute-done.4, bf16[128,4096]{1,0:T(8,128)(2,1)S(1)} %collective-permute-done.3, bf16[128,4096]{1,0:T(8,128)(2,1)S(1)} %copy-done.1), kind=kLoop, calls=%fused_computation.1 | loop fusion | flops 3670016 | bytes 6291456 | tf_op jit(solution)/shard_map/add | solution.py:174
  121.3 0.0 copy-start.3
  121.3 0.0 copy-start.4
  121.3 0.0 reduce-scatter.5.cloned.1.call-update
  121.3 0.5 broadcast.179
  121.8 0.1 copy-done.5
  122.0 0.7 fusion.86
  122.7 0.0 copy-done
  122.7 0.3 copy.20
  123.0 0.1 reshape.230
  123.1 0.1 iota_compare_fusion
  123.2 1.0 copy.17
  124.2 38.4 %reduce-scatter.5.cloned.1.call-done = f32[16,4096]{1,0:T(8,128)} async-done(((f32[128,4096]{1,0:T(8,128)}), f32[16,4096]{1,0:T(8,128)}) %reduce-scatter.5.cloned.1.call-update) | async-done | bytes 262160 | tf_op jit(solution)/shard_map/reduce_scatter | solution.py:202
  162.6 1.0 copy.18
  163.6 2.2 %multiply_bitcast_fusion.1 = (f32[4,8,32,128]{3,1,2,0:T(8,128)S(1)}, f32[1,32,4096]{2,1,0:T(8,128)}, f32[1,32,4096]{2,1,0:T(8,128)}, f32[4,8,32,128]{3,1,2,0:T(8,128)S(1)}) fusion(f32[1,32,4096]{2,1,0:T(8,128)S(1)} %copy-done.3, f32[1,16,4096]{2,1,0:T(8,128)} %bitcast.64, f32[1,16,4096]{2,1,0:T(8,128)} %bitcast.62, f32[1,32,4096]{2,1,0:T(8,128)S(1)} %copy-done.4), kind=kLoop, calls=%fused_computation.20 | loop fusion | flops 1179648 | bytes 3670016
  165.8 0.1 copy.16
  165.9 0.1 copy.19
  166.1 0.3 fusion.3
  166.4 0.6 fusion.8
  167.0 0.6 convolution_bitcast_fusion
  167.6 0.1 reshape.229
  167.7 0.1 reshape.228
  167.8 0.6 fusion.7
  168.4 1.3 gather_fusion
  169.7 0.8 select_select_fusion
  170.5 9.3 %all-to-all-start = ((bf16[8,16,512]{2,1,0:T(8,128)(2,1)}), bf16[8,16,512]{2,1,0:T(8,128)(2,1)S(1)}, u32[]{:S(2)}, u32[]{:S(2)}) async-start(bf16[8,16,512]{2,1,0:T(8,128)(2,1)} %select_select_fusion), calls=%async_computation.2 | async-start | bytes 262144 | tf_op jit(solution)/shard_map/all_to_all | solution.py:219
  179.8 0.9 multiply_subtract_fusion
  180.7 4.4 %all-to-all-done = bf16[8,16,512]{2,1,0:T(8,128)(2,1)S(1)} async-done(((bf16[8,16,512]{2,1,0:T(8,128)(2,1)}), bf16[8,16,512]{2,1,0:T(8,128)(2,1)S(1)}, u32[]{:S(2)}, u32[]{:S(2)}) %all-to-all-start) | async-done | bytes 131104 | tf_op jit(solution)/shard_map/all_to_all | solution.py:219
  185.0 0.7 copy.35
  (18 shorter events, 0.1 us)
Async XLA Ops:
  7.2 116.0 %reduce-scatter.3.cloned.1.call-start = ((), (), s32[]{:S(2)}) async-start(), calls=%async_computation.3 | async-start | bytes 2359296 | tf_op jit(solution)/shard_map/reduce_scatter | solution.py:202
  16.7 24.2 %collective-permute-start = (bf16[128,4096]{1,0:T(8,128)(2,1)}, bf16[128,4096]{1,0:T(8,128)(2,1)S(1)}, u32[]{:S(2)}, u32[]{:S(2)}) collective-permute-start(bf16[128,4096]{1,0:T(8,128)(2,1)} %get-tuple-element.21), channel_id=1, source_target_pairs={{0,64},{64,128},{128,192},{192,0},{1,65},{65,129},{129,193},{193,1... | collective-permute-start | bytes 3145736 | tf_op jit(solution)/shard_map/ppermute | solution.py:167
  18.7 47.7 %collective-permute-start.1 = (bf16[128,4096]{1,0:T(8,128)(2,1)}, bf16[128,4096]{1,0:T(8,128)(2,1)S(1)}, u32[]{:S(2)}, u32[]{:S(2)}) collective-permute-start(bf16[128,4096]{1,0:T(8,128)(2,1)} %get-tuple-element.22), channel_id=1, source_target_pairs={{0,128},{64,192},{128,0},{192,64},{1,129},{65,193},{129,1},{193,65... | collective-permute-start | bytes 3145736 | tf_op jit(solution)/shard_map/ppermute | solution.py:167
  21.1 45.3 %copy-start.2 = (bf16[128,4096]{1,0:T(8,128)(2,1)S(1)}, bf16[128,4096]{1,0:T(8,128)(2,1)}, u32[]{:S(2)}) copy-start(bf16[128,4096]{1,0:T(8,128)(2,1)} %get-tuple-element.28) | copy-start | bytes 3145732
  21.1 45.3 %collective-permute-start.2 = (bf16[128,4096]{1,0:T(8,128)(2,1)}, bf16[128,4096]{1,0:T(8,128)(2,1)}, u32[]{:S(2)}, u32[]{:S(2)}) collective-permute-start(bf16[128,4096]{1,0:T(8,128)(2,1)} %get-tuple-element.23), channel_id=1, source_target_pairs={{0,192},{64,0},{128,64},{192,128},{1,193},{65,1},{129,65},{193,129... | collective-permute-start | bytes 3145736 | tf_op jit(solution)/shard_map/ppermute | solution.py:167
  69.6 4.3 %copy-start.8 = (bf16[128,4096]{1,0:T(8,128)(2,1)S(1)}, bf16[128,4096]{1,0:T(8,128)(2,1)}, u32[]{:S(2)}) copy-start(bf16[128,4096]{1,0:T(8,128)(2,1)} %get-tuple-element.35) | copy-start | bytes 3145732
  69.6 49.7 %copy-start.1 = (bf16[128,4096]{1,0:T(8,128)(2,1)S(1)}, bf16[128,4096]{1,0:T(8,128)(2,1)}, u32[]{:S(2)}) copy-start(bf16[128,4096]{1,0:T(8,128)(2,1)} %get-tuple-element.32) | copy-start | bytes 3145732
  69.6 93.0 %reduce-scatter.5.cloned.1.call-start = ((), (), s32[]{:S(2)}) async-start(), calls=%async_computation.4 | async-start | bytes 2359296 | tf_op jit(solution)/shard_map/reduce_scatter | solution.py:202
  69.7 25.3 %collective-permute-start.3 = (bf16[128,4096]{1,0:T(8,128)(2,1)}, bf16[128,4096]{1,0:T(8,128)(2,1)S(1)}, u32[]{:S(2)}, u32[]{:S(2)}) collective-permute-start(bf16[128,4096]{1,0:T(8,128)(2,1)} %get-tuple-element.33), channel_id=1, source_target_pairs={{0,64},{64,128},{128,192},{192,0},{1,65},{65,129},{129,193},{193,1... | collective-permute-start | bytes 3145736 | tf_op jit(solution)/shard_map/ppermute | solution.py:167
  70.9 48.4 %collective-permute-start.4 = (bf16[128,4096]{1,0:T(8,128)(2,1)}, bf16[128,4096]{1,0:T(8,128)(2,1)S(1)}, u32[]{:S(2)}, u32[]{:S(2)}) collective-permute-start(bf16[128,4096]{1,0:T(8,128)(2,1)} %get-tuple-element.34), channel_id=1, source_target_pairs={{0,128},{64,192},{128,0},{192,64},{1,129},{65,193},{129,1},{193,65... | collective-permute-start | bytes 3145736 | tf_op jit(solution)/shard_map/ppermute | solution.py:167
  73.9 45.4 %collective-permute-start.5 = (bf16[128,4096]{1,0:T(8,128)(2,1)S(1)}, bf16[128,4096]{1,0:T(8,128)(2,1)S(1)}, u32[]{:S(2)}, u32[]{:S(2)}) collective-permute-start(bf16[128,4096]{1,0:T(8,128)(2,1)S(1)} %copy-done.8), channel_id=1, source_target_pairs={{0,192},{64,0},{128,64},{192,128},{1,193},{65,1},{129,65},{193,129... | collective-permute-start | bytes 3145736 | tf_op jit(solution)/shard_map/ppermute | solution.py:167
  121.2 0.7 copy-start.5
  121.3 1.4 copy-start
  121.3 1.8 copy-start.6
  121.3 1.9 copy-start.7
  121.3 42.3 %copy-start.3 = (f32[1,32,4096]{2,1,0:T(8,128)S(1)}, f32[1,32,4096]{2,1,0:T(8,128)}, u32[]{:S(2)}) copy-start(f32[1,32,4096]{2,1,0:T(8,128)} %param.12) | copy-start | bytes 1572868
  121.3 42.3 %copy-start.4 = (f32[1,32,4096]{2,1,0:T(8,128)S(1)}, f32[1,32,4096]{2,1,0:T(8,128)}, u32[]{:S(2)}) copy-start(f32[1,32,4096]{2,1,0:T(8,128)} %param.13) | copy-start | bytes 1572868
  170.5 14.5 %all-to-all-start = ((bf16[8,16,512]{2,1,0:T(8,128)(2,1)}), bf16[8,16,512]{2,1,0:T(8,128)(2,1)S(1)}, u32[]{:S(2)}, u32[]{:S(2)}) async-start(bf16[8,16,512]{2,1,0:T(8,128)(2,1)} %select_select_fusion), calls=%async_computation.2 | async-start | bytes 262144 | tf_op jit(solution)/shard_map/all_to_all | solution.py:219
Sparse Core Ops, SparseCore 0:
  69.7 42.0 reduce-scatter.2
  121.4 41.1 reduce-scatter.4

commit v9 on v8

--- a/solution.py
+++ b/solution.py
@@ -158,6 +158,54 @@
             bytes_accessed=dests * part_rows * width * 4,
         ),
     )(my_x, shifts, grad_groups, signs, walsh)
+
+
+def update_kernel(workers, p0_ref, p1_ref, f_ref, s_ref, w_ref, sg_ref, h_ref,
+                  nf_ref, ns_ref, nw_ref, nb_ref, y_ref):
+    half = p0_ref.shape[0]
+    rows_all = 2 * half
+    for part, p_ref in enumerate((p0_ref, p1_ref)):
+        rows = slice(part * half, (part + 1) * half)
+        mean_grad = p_ref[...] * (1.0 / workers)
+        new_first = first_keep * f_ref[rows, :] + first_take * mean_grad
+        new_second = second_keep * s_ref[rows, :] + second_take * mean_grad * mean_grad
+        nf_ref[rows, :] = new_first
+        ns_ref[rows, :] = new_second
+        nb_ref[rows, :] = new_first / first_fix / (jnp.sqrt(new_second / second_fix) + adam_eps)
+    stacked = jnp.concatenate([nb_ref[:, a * HB:(a + 1) * HB] for a in range(HA)], axis=0)
+    high = stacked.astype(jnp.bfloat16)
+    rest = stacked - high.astype(jnp.float32)
+    mid = rest.astype(jnp.bfloat16)
+    low = (rest - mid.astype(jnp.float32)).astype(jnp.bfloat16)
+    walsh = h_ref[...]
+    y_ref[...] = (
+        jnp.dot(high, walsh, preferred_element_type=jnp.float32)
+        + jnp.dot(mid, walsh, preferred_element_type=jnp.float32)
+        + jnp.dot(low, walsh, preferred_element_type=jnp.float32)
+    )
+    for g in range(rows_all // 8):
+        blocks = butterfly([y_ref[a * rows_all + g * 8:a * rows_all + g * 8 + 8, :] for a in range(HA)])
+        for a in range(HA):
+            cols = slice(a * HB, (a + 1) * HB)
+            sign = (2 * sg_ref[:, cols] - 1).astype(jnp.float32)
+            step = blocks[a] * (1.0 / math.sqrt(HA * HB)) * sign
+            updated = w_ref[g * 8:g * 8 + 8, cols] - learn_rate * step
+            nw_ref[g * 8:g * 8 + 8, cols] = updated
+            nb_ref[g * 8:g * 8 + 8, cols] = updated
+
+
+def adam_update(pieces, first_rows, second_rows, weight_rows, signs, walsh, workers):
+    rows, width = first_rows.shape
+    f32 = jax.ShapeDtypeStruct((rows, width), jnp.float32)
+    nf, ns, nw, nb = pl.pallas_call(
+        functools.partial(update_kernel, workers),
+        out_shape=[f32, f32, f32, f32],
+        scratch_shapes=[pltpu.VMEM((rows * HA, HB), jnp.float32)],
+        cost_estimate=pl.CostEstimate(
+            flops=6 * rows * width * HB, transcendentals=rows * width, bytes_accessed=rows * width * 32
+        ),
+    )(pieces[0], pieces[1], first_rows, second_rows, weight_rows, signs, walsh)
+    return nf, ns, nw, nb
 
 
 def send_along_x(terms, x_size):
@@ -202,13 +250,9 @@
         pieces.append(lax.psum_scatter(partial, "wz", scatter_dimension=0, tiled=True))
         if part < PARTS:
             arrived = send_along_x(terms, x_size)
-    summed = jnp.concatenate(pieces, 0)
-    mean_grad = summed / workers
-    new_first = first_keep * first[0] + first_take * mean_grad
-    new_second = second_keep * second[0] + second_take * mean_grad * mean_grad
-    step_dir = new_first / first_fix / (jnp.sqrt(new_second / second_fix) + adam_eps)
-    weight_step = rotate(step_dir) * sign_vec[None, :]
-    new_weights = weights[0] - learn_rate * weight_step
+    new_first, new_second, new_weights, _ = adam_update(
+        pieces, first[0], second[0], weights[0], signs, walsh, workers
+    )
     owners = lax.axis_size("tensor")
     piece_width = new_weights.shape[1] // owners
     narrow = new_weights.astype(jnp.bfloat16).reshape(blocks, owners, piece_width)

time: 193 us -> 191 us (0.990)
  blocking collectives: 0 us -> 14.3 us
  starting transfers between devices: 19.4 us -> 10.1 us
  other arithmetic: 10.7 us -> 6.38 us
  Pallas kernels: 18.9 us -> 22.2 us
  waiting for transfers between devices: 123 us -> 120 us
  local copies, waits for them, and re-layouts: 5.48 us -> 2.76 us
    all_to_all x0 -> x1, blocking collectives: none -> 14.3 us  [per_device(): lax.all_to_all(chosen_pieces, 'tensor', split_axis=0, concat_axis=0, tile...]
    all_to_all x1 -> x0, starting transfers between devices: 9.3 us -> none  [per_device(): lax.all_to_all(chosen_pieces, 'tensor', split_axis=0, concat_axis=0, tile...]
    all_to_all x1 -> x0, waiting for transfers between devices: 4.36 us -> none  [per_device(): lax.all_to_all(chosen_pieces, 'tensor', split_axis=0, concat_axis=0, tile...]
    pallas_call x0 -> x1, Pallas kernels: none -> 3.3 us  [adam_update(): pl.pallas_call(functools.partial(update_kernel, workers), out_shape=[f32,...]
    unnamed x1 -> x0, other arithmetic: 2.21 us -> none
    reduce_scatter x2, waiting for transfers between devices: 38.4 us -> 40.5 us  [per_device(): lax.psum_scatter(partial, 'wz', scatter_dimension=0, tiled=True)]
    unnamed x25 -> x11, local copies, waits for them, and re-layouts: 3.36 us -> 1.33 us
  transfers between devices with their start and end apart: 9 -> 8, of which waited for: 6 -> 5; matrix products, arithmetic and copies ran while one was open for 3% -> 1% of each run, Pallas kernels for 5% -> 5%
where the time goes in v9:
time: 191 us; the launch traced here: 190 us
  waiting for transfers between devices  120 us (63%)
  Pallas kernels  22.2 us (12%)
  blocking collectives  14.3 us (7%)
  between operations  14.1 us (7%)
  starting transfers between devices  10.1 us (5%)
  other arithmetic  6.38 us (3%)
  local copies, waits for them, and re-layouts  2.76 us (1%)
    ppermute x6, waiting for transfers between devices, send_along_x(): arrived.append(lax.ppermute(terms[step], 'wx', pairs))  79.9 us
    reduce_scatter x2, waiting for transfers between devices, per_device(): lax.psum_scatter(partial, 'wz', scatter_dimension=0, tiled=True)  40.5 us
    pallas_call x2, Pallas kernels, decoded_terms(): pl.pallas_call(functools.partial(code_kernel, part, x_size), grid_spec=pl...  18.9 us
    all_to_all x1, blocking collectives, per_device(): lax.all_to_all(chosen_pieces, 'tensor', split_axis=0, concat_axis=0, tile...  14.3 us
    ppermute x6, starting transfers between devices, send_along_x(): arrived.append(lax.ppermute(terms[step], 'wx', pairs))  10 us
    add x2, other arithmetic, sum_arrived(): partial = partial + piece.astype(jnp.float32)  5.13 us
  transfers between devices with their start and end apart: 8, of which 5 were waited for; matrix products, arithmetic and copies ran while one was open for 1% of the time, Pallas kernels for 5%

profile of v9, /device:TPU:1, one launch (start us, length us, event | category | flops | bytes accessed | tf_op | source)
XLA Modules:
  0.0 190.2 jit_solution(1041935312104416063)
XLA Ops:
  7.2 0.0 reduce-scatter.3.cloned.1.call-start
  7.2 9.4 %shard_map.120 = (bf16[128,4096]{1,0:T(8,128)(2,1)}, bf16[128,4096]{1,0:T(8,128)(2,1)}, bf16[128,4096]{1,0:T(8,128)(2,1)}, bf16[128,4096]{1,0:T(8,128)(2,1)}) custom-call(s32[1]{0:T(128)} %bitcast.mx_ref, s32[1,1,1024]{2,1,0:T(1,128)} %sh_ref.3, bf16[32,2,16,4096]{3,2,1,0:T(8,128)(2,1)} %bitcast.26, s32[1,4096]{1,0:T(1,128)} %sg_ref.5, ...), custom_call_target="tpu_custom_call" | custom-call | flops 553648128 | bytes 8388608 | tf_op jit(solution)/shard_map/pallas_call | solution.py:141
  16.7 2.0 %collective-permute-start = (bf16[128,4096]{1,0:T(8,128)(2,1)}, bf16[128,4096]{1,0:T(8,128)(2,1)S(1)}, u32[]{:S(2)}, u32[]{:S(2)}) collective-permute-start(bf16[128,4096]{1,0:T(8,128)(2,1)} %get-tuple-element.24), channel_id=1, source_target_pairs={{0,64},{64,128},{128,192},{192,0},{1,65},{65,129},{129,193},{193,1... | collective-permute-start | bytes 3145736 | tf_op jit(solution)/shard_map/ppermute | solution.py:215
  18.7 2.4 %collective-permute-start.1 = (bf16[128,4096]{1,0:T(8,128)(2,1)}, bf16[128,4096]{1,0:T(8,128)(2,1)S(1)}, u32[]{:S(2)}, u32[]{:S(2)}) collective-permute-start(bf16[128,4096]{1,0:T(8,128)(2,1)} %get-tuple-element.25), channel_id=1, source_target_pairs={{0,128},{64,192},{128,0},{192,64},{1,129},{65,193},{129,1},{193,65... | collective-permute-start | bytes 3145736 | tf_op jit(solution)/shard_map/ppermute | solution.py:215
  21.1 0.0 copy-start.1
  21.1 1.2 collective-permute-start.2
  22.3 9.4 %shard_map.121 = (bf16[128,4096]{1,0:T(8,128)(2,1)}, bf16[128,4096]{1,0:T(8,128)(2,1)}, bf16[128,4096]{1,0:T(8,128)(2,1)}, bf16[128,4096]{1,0:T(8,128)(2,1)}) custom-call(s32[1]{0:T(128)} %bitcast.mx_ref, s32[1,1,1024]{2,1,0:T(1,128)} %sh_ref.3, bf16[32,2,16,4096]{3,2,1,0:T(8,128)(2,1)} %bitcast.27, s32[1,4096]{1,0:T(1,128)} %sg_ref.5, ...), custom_call_target="tpu_custom_call" | custom-call | flops 553648128 | bytes 8388608 | tf_op jit(solution)/shard_map/pallas_call | solution.py:141
  31.7 9.1 %collective-permute-done = bf16[128,4096]{1,0:T(8,128)(2,1)S(1)} collective-permute-done((bf16[128,4096]{1,0:T(8,128)(2,1)}, bf16[128,4096]{1,0:T(8,128)(2,1)S(1)}, u32[]{:S(2)}, u32[]{:S(2)}) %collective-permute-start) | collective-permute-done | bytes 1048608 | tf_op jit(solution)/shard_map/ppermute | solution.py:215
  40.8 25.6 %collective-permute-done.1 = bf16[128,4096]{1,0:T(8,128)(2,1)S(1)} collective-permute-done((bf16[128,4096]{1,0:T(8,128)(2,1)}, bf16[128,4096]{1,0:T(8,128)(2,1)S(1)}, u32[]{:S(2)}, u32[]{:S(2)}) %collective-permute-start.1) | collective-permute-done | bytes 1048608 | tf_op jit(solution)/shard_map/ppermute | solution.py:215
  66.4 0.0 collective-permute-done.2
  66.4 0.0 copy-done.1
  66.4 3.2 %convert_add_fusion.1 = f32[128,4096]{1,0:T(8,128)} fusion(bf16[128,4096]{1,0:T(8,128)(2,1)} %collective-permute-done.2, bf16[128,4096]{1,0:T(8,128)(2,1)S(1)} %collective-permute-done.1, bf16[128,4096]{1,0:T(8,128)(2,1)S(1)} %collective-permute-done, bf16[128,4096]{1,0:T(8,128)(2,1)S(1)} %copy-done.1), kind=kLoop, calls=%fused_computation.2 | loop fusion | flops 3670016 | bytes 6291456 | tf_op jit(solution)/shard_map/add | solution.py:222
  69.6 0.0 copy-start.4
  69.6 0.0 copy-start
  69.6 0.0 reduce-scatter.3.cloned.1.call-update
  69.6 0.0 reduce-scatter.5.cloned.1.call-start
  69.7 1.2 collective-permute-start.3
  70.9 3.0 %collective-permute-start.4 = (bf16[128,4096]{1,0:T(8,128)(2,1)}, bf16[128,4096]{1,0:T(8,128)(2,1)S(1)}, u32[]{:S(2)}, u32[]{:S(2)}) collective-permute-start(bf16[128,4096]{1,0:T(8,128)(2,1)} %get-tuple-element.37), channel_id=1, source_target_pairs={{0,128},{64,192},{128,0},{192,64},{1,129},{65,193},{129,1},{193,65... | collective-permute-start | bytes 3145736 | tf_op jit(solution)/shard_map/ppermute | solution.py:215
  73.9 0.0 copy-done.4
  73.9 0.2 collective-permute-start.5
  74.1 20.9 %collective-permute-done.3 = bf16[128,4096]{1,0:T(8,128)(2,1)S(1)} collective-permute-done((bf16[128,4096]{1,0:T(8,128)(2,1)}, bf16[128,4096]{1,0:T(8,128)(2,1)S(1)}, u32[]{:S(2)}, u32[]{:S(2)}) %collective-permute-start.3) | collective-permute-done | bytes 1048608 | tf_op jit(solution)/shard_map/ppermute | solution.py:215
  95.0 24.3 %collective-permute-done.4 = bf16[128,4096]{1,0:T(8,128)(2,1)S(1)} collective-permute-done((bf16[128,4096]{1,0:T(8,128)(2,1)}, bf16[128,4096]{1,0:T(8,128)(2,1)S(1)}, u32[]{:S(2)}, u32[]{:S(2)}) %collective-permute-start.4) | collective-permute-done | bytes 1048608 | tf_op jit(solution)/shard_map/ppermute | solution.py:215
  119.3 0.0 collective-permute-done.5
  119.3 0.0 copy-done
  119.3 1.9 %convert_add_fusion = f32[128,4096]{1,0:T(8,128)} fusion(bf16[128,4096]{1,0:T(8,128)(2,1)S(1)} %collective-permute-done.5, bf16[128,4096]{1,0:T(8,128)(2,1)S(1)} %collective-permute-done.4, bf16[128,4096]{1,0:T(8,128)(2,1)S(1)} %collective-permute-done.3, bf16[128,4096]{1,0:T(8,128)(2,1)S(1)} %copy-done), kind=kLoop, calls=%fused_computation.1 | loop fusion | flops 3670016 | bytes 6291456 | tf_op jit(solution)/shard_map/add | solution.py:222
  121.2 0.0 copy-start.2
  121.2 0.0 copy-start.3
  121.2 0.0 reduce-scatter.5.cloned.1.call-update
  121.3 0.7 copy-done.2
  121.9 0.1 reshape.85
  122.0 0.0 copy-done.3
  122.0 0.1 iota_compare_fusion
  122.1 0.0 reduce-scatter.3.cloned.1.call-done.p0_ref
  122.1 40.5 %reduce-scatter.5.cloned.1.call-done.p1_ref = f32[16,4096]{1,0:T(8,128)} async-done(((f32[128,4096]{1,0:T(8,128)}), f32[16,4096]{1,0:T(8,128)}) %reduce-scatter.5.cloned.1.call-update) | async-done | bytes 262160 | tf_op jit(solution)/shard_map/reduce_scatter | solution.py:250
  162.6 3.3 %shard_map.122 = (f32[32,4096]{1,0:T(8,128)}, f32[32,4096]{1,0:T(8,128)}, f32[32,4096]{1,0:T(8,128)}, f32[32,4096]{1,0:T(8,128)}) custom-call(f32[16,4096]{1,0:T(8,128)} %reduce-scatter.3.cloned.1.call-done.p0_ref, f32[16,4096]{1,0:T(8,128)} %reduce-scatter.5.cloned.1.call-done.p1_ref, f32[32,4096]{1,0:T(8,128)} %bitcast.33, f32[32,4096]{1,0:T(8,128)} %bitcast.34, ...), custom_call_target="tpu_custom_call" | custom-call | flops 100663296 | bytes 4194304 | tf_op jit(solution)/shard_map/pallas_call | solution.py:200
  165.9 1.1 convert_element_type.35
  167.0 1.3 gather_fusion
  168.3 0.1 select_select_fusion
  168.4 14.3 %all_to_all.5 = bf16[8,16,512]{2,1,0:T(8,128)(2,1)S(1)} all-to-all(bf16[8,16,512]{2,1,0:T(8,128)(2,1)S(1)} %select_select_fusion), channel_id=1, replica_groups=mesh['wx'=4,'wz'=8,'tensor'=8] {'tensor'}, dimensions={0} | all-to-all | bytes 262144 | tf_op jit(solution)/shard_map/all_to_all | solution.py:263
  182.7 0.7 copy.18
  (2 shorter events, 0.0 us)
Async XLA Ops:
  7.2 114.9 %reduce-scatter.3.cloned.1.call-start = ((), (), s32[]{:S(2)}) async-start(), calls=%async_computation.3 | async-start | bytes 2359296 | tf_op jit(solution)/shard_map/reduce_scatter | solution.py:250
  16.7 24.2 %collective-permute-start = (bf16[128,4096]{1,0:T(8,128)(2,1)}, bf16[128,4096]{1,0:T(8,128)(2,1)S(1)}, u32[]{:S(2)}, u32[]{:S(2)}) collective-permute-start(bf16[128,4096]{1,0:T(8,128)(2,1)} %get-tuple-element.24), channel_id=1, source_target_pairs={{0,64},{64,128},{128,192},{192,0},{1,65},{65,129},{129,193},{193,1... | collective-permute-start | bytes 3145736 | tf_op jit(solution)/shard_map/ppermute | solution.py:215
  18.7 47.7 %collective-permute-start.1 = (bf16[128,4096]{1,0:T(8,128)(2,1)}, bf16[128,4096]{1,0:T(8,128)(2,1)S(1)}, u32[]{:S(2)}, u32[]{:S(2)}) collective-permute-start(bf16[128,4096]{1,0:T(8,128)(2,1)} %get-tuple-element.25), channel_id=1, source_target_pairs={{0,128},{64,192},{128,0},{192,64},{1,129},{65,193},{129,1},{193,65... | collective-permute-start | bytes 3145736 | tf_op jit(solution)/shard_map/ppermute | solution.py:215
  21.1 45.3 %copy-start.1 = (bf16[128,4096]{1,0:T(8,128)(2,1)S(1)}, bf16[128,4096]{1,0:T(8,128)(2,1)}, u32[]{:S(2)}) copy-start(bf16[128,4096]{1,0:T(8,128)(2,1)} %get-tuple-element.31) | copy-start | bytes 3145732
  21.1 45.3 %collective-permute-start.2 = (bf16[128,4096]{1,0:T(8,128)(2,1)}, bf16[128,4096]{1,0:T(8,128)(2,1)}, u32[]{:S(2)}, u32[]{:S(2)}) collective-permute-start(bf16[128,4096]{1,0:T(8,128)(2,1)} %get-tuple-element.26), channel_id=1, source_target_pairs={{0,192},{64,0},{128,64},{192,128},{1,193},{65,1},{129,65},{193,129... | collective-permute-start | bytes 3145736 | tf_op jit(solution)/shard_map/ppermute | solution.py:215
  69.6 4.3 %copy-start.4 = (bf16[128,4096]{1,0:T(8,128)(2,1)S(1)}, bf16[128,4096]{1,0:T(8,128)(2,1)}, u32[]{:S(2)}) copy-start(bf16[128,4096]{1,0:T(8,128)(2,1)} %get-tuple-element.38) | copy-start | bytes 3145732
  69.6 49.7 %copy-start = (bf16[128,4096]{1,0:T(8,128)(2,1)S(1)}, bf16[128,4096]{1,0:T(8,128)(2,1)}, u32[]{:S(2)}) copy-start(bf16[128,4096]{1,0:T(8,128)(2,1)} %get-tuple-element.35) | copy-start | bytes 3145732
  69.6 92.9 %reduce-scatter.5.cloned.1.call-start = ((), (), s32[]{:S(2)}) async-start(), calls=%async_computation.4 | async-start | bytes 2359296 | tf_op jit(solution)/shard_map/reduce_scatter | solution.py:250
  69.7 25.3 %collective-permute-start.3 = (bf16[128,4096]{1,0:T(8,128)(2,1)}, bf16[128,4096]{1,0:T(8,128)(2,1)S(1)}, u32[]{:S(2)}, u32[]{:S(2)}) collective-permute-start(bf16[128,4096]{1,0:T(8,128)(2,1)} %get-tuple-element.36), channel_id=1, source_target_pairs={{0,64},{64,128},{128,192},{192,0},{1,65},{65,129},{129,193},{193,1... | collective-permute-start | bytes 3145736 | tf_op jit(solution)/shard_map/ppermute | solution.py:215
  70.9 48.4 %collective-permute-start.4 = (bf16[128,4096]{1,0:T(8,128)(2,1)}, bf16[128,4096]{1,0:T(8,128)(2,1)S(1)}, u32[]{:S(2)}, u32[]{:S(2)}) collective-permute-start(bf16[128,4096]{1,0:T(8,128)(2,1)} %get-tuple-element.37), channel_id=1, source_target_pairs={{0,128},{64,192},{128,0},{192,64},{1,129},{65,193},{129,1},{193,65... | collective-permute-start | bytes 3145736 | tf_op jit(solution)/shard_map/ppermute | solution.py:215
  73.9 45.4 %collective-permute-start.5 = (bf16[128,4096]{1,0:T(8,128)(2,1)S(1)}, bf16[128,4096]{1,0:T(8,128)(2,1)S(1)}, u32[]{:S(2)}, u32[]{:S(2)}) collective-permute-start(bf16[128,4096]{1,0:T(8,128)(2,1)S(1)} %copy-done.4), channel_id=1, source_target_pairs={{0,192},{64,0},{128,64},{192,128},{1,193},{65,1},{129,65},{193,129... | collective-permute-start | bytes 3145736 | tf_op jit(solution)/shard_map/ppermute | solution.py:215
  121.2 0.7 copy-start.2
  121.2 0.8 copy-start.3
Sparse Core Ops, SparseCore 0:
  69.7 42.0 reduce-scatter.2
  121.4 41.1 reduce-scatter.4

commit v10 on v9

--- a/solution.py
+++ b/solution.py
@@ -161,7 +161,7 @@
 
 
 def update_kernel(workers, p0_ref, p1_ref, f_ref, s_ref, w_ref, sg_ref, h_ref,
-                  nf_ref, ns_ref, nw_ref, nb_ref, y_ref):
+                  nf_ref, ns_ref, nw_ref, nb_ref, sd_ref, y_ref):
     half = p0_ref.shape[0]
     rows_all = 2 * half
     for part, p_ref in enumerate((p0_ref, p1_ref)):
@@ -171,8 +171,8 @@
         new_second = second_keep * s_ref[rows, :] + second_take * mean_grad * mean_grad
         nf_ref[rows, :] = new_first
         ns_ref[rows, :] = new_second
-        nb_ref[rows, :] = new_first / first_fix / (jnp.sqrt(new_second / second_fix) + adam_eps)
-    stacked = jnp.concatenate([nb_ref[:, a * HB:(a + 1) * HB] for a in range(HA)], axis=0)
+        sd_ref[rows, :] = new_first / first_fix / (jnp.sqrt(new_second / second_fix) + adam_eps)
+    stacked = jnp.concatenate([sd_ref[:, a * HB:(a + 1) * HB] for a in range(HA)], axis=0)
     high = stacked.astype(jnp.bfloat16)
     rest = stacked - high.astype(jnp.float32)
     mid = rest.astype(jnp.bfloat16)
@@ -191,7 +191,7 @@
             step = blocks[a] * (1.0 / math.sqrt(HA * HB)) * sign
             updated = w_ref[g * 8:g * 8 + 8, cols] - learn_rate * step
             nw_ref[g * 8:g * 8 + 8, cols] = updated
-            nb_ref[g * 8:g * 8 + 8, cols] = updated
+            nb_ref[g * 8:g * 8 + 8, cols] = updated.astype(nb_ref.dtype)
 
 
 def adam_update(pieces, first_rows, second_rows, weight_rows, signs, walsh, workers):
@@ -199,8 +199,8 @@
     f32 = jax.ShapeDtypeStruct((rows, width), jnp.float32)
     nf, ns, nw, nb = pl.pallas_call(
         functools.partial(update_kernel, workers),
-        out_shape=[f32, f32, f32, f32],
-        scratch_shapes=[pltpu.VMEM((rows * HA, HB), jnp.float32)],
+        out_shape=[f32, f32, f32, jax.ShapeDtypeStruct((rows, width), jnp.bfloat16)],
+        scratch_shapes=[pltpu.VMEM((rows, width), jnp.float32), pltpu.VMEM((rows * HA, HB), jnp.float32)],
         cost_estimate=pl.CostEstimate(
             flops=6 * rows * width * HB, transcendentals=rows * width, bytes_accessed=rows * width * 32
         ),
@@ -250,12 +250,12 @@
         pieces.append(lax.psum_scatter(partial, "wz", scatter_dimension=0, tiled=True))
         if part < PARTS:
             arrived = send_along_x(terms, x_size)
-    new_first, new_second, new_weights, _ = adam_update(
+    new_first, new_second, new_weights, narrow_weights = adam_update(
         pieces, first[0], second[0], weights[0], signs, walsh, workers
     )
     owners = lax.axis_size("tensor")
     piece_width = new_weights.shape[1] // owners
-    narrow = new_weights.astype(jnp.bfloat16).reshape(blocks, owners, piece_width)
+    narrow = narrow_weights.reshape(blocks, owners, piece_width)
     slab_view = jnp.transpose(narrow, (1, 0, 2))
     slot_lists = slots[0, 0]
     used_counts = counts[0, 0]

time: 191 us -> 190 us (level)
  no operation moved by 1% of the time
where the time goes in v10:
time: 190 us
  waiting for transfers between devices  120 us (63%)
  Pallas kernels  22.1 us (12%)
  blocking collectives  14.3 us (8%)
  between operations  14.1 us (7%)
  starting transfers between devices  10.1 us (5%)
  other arithmetic  5.31 us (3%)
  local copies, waits for them, and re-layouts  3.7 us (2%)
    ppermute x6, waiting for transfers between devices, send_along_x(): arrived.append(lax.ppermute(terms[step], 'wx', pairs))  79.9 us
    reduce_scatter x2, waiting for transfers between devices, per_device(): lax.psum_scatter(partial, 'wz', scatter_dimension=0, tiled=True)  40.5 us
    pallas_call x2, Pallas kernels, decoded_terms(): pl.pallas_call(functools.partial(code_kernel, part, x_size), grid_spec=pl...  18.9 us
    all_to_all x1, blocking collectives, per_device(): lax.all_to_all(chosen_pieces, 'tensor', split_axis=0, concat_axis=0, tile...  14.3 us
    ppermute x6, starting transfers between devices, send_along_x(): arrived.append(lax.ppermute(terms[step], 'wx', pairs))  10 us
    add x2, other arithmetic, sum_arrived(): partial = partial + piece.astype(jnp.float32)  5.13 us
  transfers between devices with their start and end apart: 8, of which 5 were waited for; matrix products, arithmetic and copies ran while one was open for 1% of the time, Pallas kernels for 5%

profile of v10, /device:TPU:1, one launch (start us, length us, event | category | flops | bytes accessed | tf_op | source)
XLA Modules:
  0.0 190.0 jit_solution(12197244515845203690)
XLA Ops:
  7.2 0.0 reduce-scatter.3.cloned.1.call-start
  7.2 9.4 %shard_map.120 = (bf16[128,4096]{1,0:T(8,128)(2,1)}, bf16[128,4096]{1,0:T(8,128)(2,1)}, bf16[128,4096]{1,0:T(8,128)(2,1)}, bf16[128,4096]{1,0:T(8,128)(2,1)}) custom-call(s32[1]{0:T(128)} %bitcast.mx_ref, s32[1,1,1024]{2,1,0:T(1,128)} %sh_ref.3, bf16[32,2,16,4096]{3,2,1,0:T(8,128)(2,1)} %bitcast.26, s32[1,4096]{1,0:T(1,128)} %sg_ref.5, ...), custom_call_target="tpu_custom_call" | custom-call | flops 553648128 | bytes 8388608 | tf_op jit(solution)/shard_map/pallas_call | solution.py:141
  16.7 2.0 %collective-permute-start = (bf16[128,4096]{1,0:T(8,128)(2,1)}, bf16[128,4096]{1,0:T(8,128)(2,1)S(1)}, u32[]{:S(2)}, u32[]{:S(2)}) collective-permute-start(bf16[128,4096]{1,0:T(8,128)(2,1)} %get-tuple-element.25), channel_id=1, source_target_pairs={{0,64},{64,128},{128,192},{192,0},{1,65},{65,129},{129,193},{193,1... | collective-permute-start | bytes 3145736 | tf_op jit(solution)/shard_map/ppermute | solution.py:215
  18.7 2.4 %collective-permute-start.1 = (bf16[128,4096]{1,0:T(8,128)(2,1)}, bf16[128,4096]{1,0:T(8,128)(2,1)S(1)}, u32[]{:S(2)}, u32[]{:S(2)}) collective-permute-start(bf16[128,4096]{1,0:T(8,128)(2,1)} %get-tuple-element.26), channel_id=1, source_target_pairs={{0,128},{64,192},{128,0},{192,64},{1,129},{65,193},{129,1},{193,65... | collective-permute-start | bytes 3145736 | tf_op jit(solution)/shard_map/ppermute | solution.py:215
  21.1 0.0 copy-start.1
  21.1 1.2 collective-permute-start.2
  22.3 9.4 %shard_map.121 = (bf16[128,4096]{1,0:T(8,128)(2,1)}, bf16[128,4096]{1,0:T(8,128)(2,1)}, bf16[128,4096]{1,0:T(8,128)(2,1)}, bf16[128,4096]{1,0:T(8,128)(2,1)}) custom-call(s32[1]{0:T(128)} %bitcast.mx_ref, s32[1,1,1024]{2,1,0:T(1,128)} %sh_ref.3, bf16[32,2,16,4096]{3,2,1,0:T(8,128)(2,1)} %bitcast.27, s32[1,4096]{1,0:T(1,128)} %sg_ref.5, ...), custom_call_target="tpu_custom_call" | custom-call | flops 553648128 | bytes 8388608 | tf_op jit(solution)/shard_map/pallas_call | solution.py:141
  31.7 9.1 %collective-permute-done = bf16[128,4096]{1,0:T(8,128)(2,1)S(1)} collective-permute-done((bf16[128,4096]{1,0:T(8,128)(2,1)}, bf16[128,4096]{1,0:T(8,128)(2,1)S(1)}, u32[]{:S(2)}, u32[]{:S(2)}) %collective-permute-start) | collective-permute-done | bytes 1048608 | tf_op jit(solution)/shard_map/ppermute | solution.py:215
  40.8 25.6 %collective-permute-done.1 = bf16[128,4096]{1,0:T(8,128)(2,1)S(1)} collective-permute-done((bf16[128,4096]{1,0:T(8,128)(2,1)}, bf16[128,4096]{1,0:T(8,128)(2,1)S(1)}, u32[]{:S(2)}, u32[]{:S(2)}) %collective-permute-start.1) | collective-permute-done | bytes 1048608 | tf_op jit(solution)/shard_map/ppermute | solution.py:215
  66.4 0.0 collective-permute-done.2
  66.4 0.0 copy-done.1
  66.4 3.2 %convert_add_fusion.1 = f32[128,4096]{1,0:T(8,128)} fusion(bf16[128,4096]{1,0:T(8,128)(2,1)} %collective-permute-done.2, bf16[128,4096]{1,0:T(8,128)(2,1)S(1)} %collective-permute-done.1, bf16[128,4096]{1,0:T(8,128)(2,1)S(1)} %collective-permute-done, bf16[128,4096]{1,0:T(8,128)(2,1)S(1)} %copy-done.1), kind=kLoop, calls=%fused_computation.2 | loop fusion | flops 3670016 | bytes 6291456 | tf_op jit(solution)/shard_map/add | solution.py:222
  69.6 0.0 copy-start.4
  69.6 0.0 copy-start
  69.6 0.0 reduce-scatter.3.cloned.1.call-update
  69.6 0.0 reduce-scatter.5.cloned.1.call-start
  69.7 1.2 collective-permute-start.3
  70.9 3.0 %collective-permute-start.4 = (bf16[128,4096]{1,0:T(8,128)(2,1)}, bf16[128,4096]{1,0:T(8,128)(2,1)S(1)}, u32[]{:S(2)}, u32[]{:S(2)}) collective-permute-start(bf16[128,4096]{1,0:T(8,128)(2,1)} %get-tuple-element.38), channel_id=1, source_target_pairs={{0,128},{64,192},{128,0},{192,64},{1,129},{65,193},{129,1},{193,65... | collective-permute-start | bytes 3145736 | tf_op jit(solution)/shard_map/ppermute | solution.py:215
  73.9 0.0 copy-done.4
  73.9 0.2 collective-permute-start.5
  74.1 20.9 %collective-permute-done.3 = bf16[128,4096]{1,0:T(8,128)(2,1)S(1)} collective-permute-done((bf16[128,4096]{1,0:T(8,128)(2,1)}, bf16[128,4096]{1,0:T(8,128)(2,1)S(1)}, u32[]{:S(2)}, u32[]{:S(2)}) %collective-permute-start.3) | collective-permute-done | bytes 1048608 | tf_op jit(solution)/shard_map/ppermute | solution.py:215
  95.0 24.3 %collective-permute-done.4 = bf16[128,4096]{1,0:T(8,128)(2,1)S(1)} collective-permute-done((bf16[128,4096]{1,0:T(8,128)(2,1)}, bf16[128,4096]{1,0:T(8,128)(2,1)S(1)}, u32[]{:S(2)}, u32[]{:S(2)}) %collective-permute-start.4) | collective-permute-done | bytes 1048608 | tf_op jit(solution)/shard_map/ppermute | solution.py:215
  119.3 0.0 collective-permute-done.5
  119.3 0.0 copy-done
  119.3 1.9 %convert_add_fusion = f32[128,4096]{1,0:T(8,128)} fusion(bf16[128,4096]{1,0:T(8,128)(2,1)S(1)} %collective-permute-done.5, bf16[128,4096]{1,0:T(8,128)(2,1)S(1)} %collective-permute-done.4, bf16[128,4096]{1,0:T(8,128)(2,1)S(1)} %collective-permute-done.3, bf16[128,4096]{1,0:T(8,128)(2,1)S(1)} %copy-done), kind=kLoop, calls=%fused_computation.1 | loop fusion | flops 3670016 | bytes 6291456 | tf_op jit(solution)/shard_map/add | solution.py:222
  121.2 0.0 copy-start.2
  121.2 0.0 copy-start.3
  121.2 0.0 reduce-scatter.5.cloned.1.call-update
  121.3 0.7 copy-done.2
  121.9 0.1 reshape.85
  122.0 0.0 copy-done.3
  122.0 0.1 iota_compare_fusion
  122.1 0.0 reduce-scatter.3.cloned.1.call-done.p0_ref
  122.1 40.5 %reduce-scatter.5.cloned.1.call-done.p1_ref = f32[16,4096]{1,0:T(8,128)} async-done(((f32[128,4096]{1,0:T(8,128)}), f32[16,4096]{1,0:T(8,128)}) %reduce-scatter.5.cloned.1.call-update) | async-done | bytes 262160 | tf_op jit(solution)/shard_map/reduce_scatter | solution.py:250
  162.6 3.2 %shard_map.122 = (f32[32,4096]{1,0:T(8,128)}, f32[32,4096]{1,0:T(8,128)}, f32[32,4096]{1,0:T(8,128)}, bf16[32,4096]{1,0:T(8,128)(2,1)}) custom-call(f32[16,4096]{1,0:T(8,128)} %reduce-scatter.3.cloned.1.call-done.p0_ref, f32[16,4096]{1,0:T(8,128)} %reduce-scatter.5.cloned.1.call-done.p1_ref, f32[32,4096]{1,0:T(8,128)} %bitcast.31, f32[32,4096]{1,0:T(8,128)} %bitcast.32, ...), custom_call_target="tpu_custom_call" | custom-call | flops 100663296 | bytes 4194304 | tf_op jit(solution)/shard_map/pallas_call | solution.py:200
  165.8 1.0 copy.16
  166.8 1.3 gather_fusion
  168.1 0.1 select_select_fusion
  168.2 14.3 %all_to_all.5 = bf16[8,16,512]{2,1,0:T(8,128)(2,1)S(1)} all-to-all(bf16[8,16,512]{2,1,0:T(8,128)(2,1)S(1)} %select_select_fusion), channel_id=1, replica_groups=mesh['wx'=4,'wz'=8,'tensor'=8] {'tensor'}, dimensions={0} | all-to-all | bytes 262144 | tf_op jit(solution)/shard_map/all_to_all | solution.py:263
  182.5 0.7 copy.18
  (1 shorter events, 0.0 us)
Async XLA Ops:
  7.2 114.9 %reduce-scatter.3.cloned.1.call-start = ((), (), s32[]{:S(2)}) async-start(), calls=%async_computation.3 | async-start | bytes 2359296 | tf_op jit(solution)/shard_map/reduce_scatter | solution.py:250
  16.7 24.2 %collective-permute-start = (bf16[128,4096]{1,0:T(8,128)(2,1)}, bf16[128,4096]{1,0:T(8,128)(2,1)S(1)}, u32[]{:S(2)}, u32[]{:S(2)}) collective-permute-start(bf16[128,4096]{1,0:T(8,128)(2,1)} %get-tuple-element.25), channel_id=1, source_target_pairs={{0,64},{64,128},{128,192},{192,0},{1,65},{65,129},{129,193},{193,1... | collective-permute-start | bytes 3145736 | tf_op jit(solution)/shard_map/ppermute | solution.py:215
  18.7 47.7 %collective-permute-start.1 = (bf16[128,4096]{1,0:T(8,128)(2,1)}, bf16[128,4096]{1,0:T(8,128)(2,1)S(1)}, u32[]{:S(2)}, u32[]{:S(2)}) collective-permute-start(bf16[128,4096]{1,0:T(8,128)(2,1)} %get-tuple-element.26), channel_id=1, source_target_pairs={{0,128},{64,192},{128,0},{192,64},{1,129},{65,193},{129,1},{193,65... | collective-permute-start | bytes 3145736 | tf_op jit(solution)/shard_map/ppermute | solution.py:215
  21.1 45.3 %copy-start.1 = (bf16[128,4096]{1,0:T(8,128)(2,1)S(1)}, bf16[128,4096]{1,0:T(8,128)(2,1)}, u32[]{:S(2)}) copy-start(bf16[128,4096]{1,0:T(8,128)(2,1)} %get-tuple-element.32) | copy-start | bytes 3145732
  21.1 45.3 %collective-permute-start.2 = (bf16[128,4096]{1,0:T(8,128)(2,1)}, bf16[128,4096]{1,0:T(8,128)(2,1)}, u32[]{:S(2)}, u32[]{:S(2)}) collective-permute-start(bf16[128,4096]{1,0:T(8,128)(2,1)} %get-tuple-element.27), channel_id=1, source_target_pairs={{0,192},{64,0},{128,64},{192,128},{1,193},{65,1},{129,65},{193,129... | collective-permute-start | bytes 3145736 | tf_op jit(solution)/shard_map/ppermute | solution.py:215
  69.6 4.3 %copy-start.4 = (bf16[128,4096]{1,0:T(8,128)(2,1)S(1)}, bf16[128,4096]{1,0:T(8,128)(2,1)}, u32[]{:S(2)}) copy-start(bf16[128,4096]{1,0:T(8,128)(2,1)} %get-tuple-element.39) | copy-start | bytes 3145732
  69.6 49.7 %copy-start = (bf16[128,4096]{1,0:T(8,128)(2,1)S(1)}, bf16[128,4096]{1,0:T(8,128)(2,1)}, u32[]{:S(2)}) copy-start(bf16[128,4096]{1,0:T(8,128)(2,1)} %get-tuple-element.36) | copy-start | bytes 3145732
  69.6 92.9 %reduce-scatter.5.cloned.1.call-start = ((), (), s32[]{:S(2)}) async-start(), calls=%async_computation.4 | async-start | bytes 2359296 | tf_op jit(solution)/shard_map/reduce_scatter | solution.py:250
  69.7 25.3 %collective-permute-start.3 = (bf16[128,4096]{1,0:T(8,128)(2,1)}, bf16[128,4096]{1,0:T(8,128)(2,1)S(1)}, u32[]{:S(2)}, u32[]{:S(2)}) collective-permute-start(bf16[128,4096]{1,0:T(8,128)(2,1)} %get-tuple-element.37), channel_id=1, source_target_pairs={{0,64},{64,128},{128,192},{192,0},{1,65},{65,129},{129,193},{193,1... | collective-permute-start | bytes 3145736 | tf_op jit(solution)/shard_map/ppermute | solution.py:215
  70.9 48.4 %collective-permute-start.4 = (bf16[128,4096]{1,0:T(8,128)(2,1)}, bf16[128,4096]{1,0:T(8,128)(2,1)S(1)}, u32[]{:S(2)}, u32[]{:S(2)}) collective-permute-start(bf16[128,4096]{1,0:T(8,128)(2,1)} %get-tuple-element.38), channel_id=1, source_target_pairs={{0,128},{64,192},{128,0},{192,64},{1,129},{65,193},{129,1},{193,65... | collective-permute-start | bytes 3145736 | tf_op jit(solution)/shard_map/ppermute | solution.py:215
  73.9 45.4 %collective-permute-start.5 = (bf16[128,4096]{1,0:T(8,128)(2,1)S(1)}, bf16[128,4096]{1,0:T(8,128)(2,1)S(1)}, u32[]{:S(2)}, u32[]{:S(2)}) collective-permute-start(bf16[128,4096]{1,0:T(8,128)(2,1)S(1)} %copy-done.4), channel_id=1, source_target_pairs={{0,192},{64,0},{128,64},{192,128},{1,193},{65,1},{129,65},{193,129... | collective-permute-start | bytes 3145736 | tf_op jit(solution)/shard_map/ppermute | solution.py:215
  121.2 0.7 copy-start.2
  121.2 0.8 copy-start.3
Sparse Core Ops, SparseCore 0:
  69.7 42.0 reduce-scatter.2
  121.4 41.1 reduce-scatter.4

commit v11 on v10

--- a/solution.py
+++ b/solution.py
@@ -191,15 +191,17 @@
             step = blocks[a] * (1.0 / math.sqrt(HA * HB)) * sign
             updated = w_ref[g * 8:g * 8 + 8, cols] - learn_rate * step
             nw_ref[g * 8:g * 8 + 8, cols] = updated
-            nb_ref[g * 8:g * 8 + 8, cols] = updated.astype(nb_ref.dtype)
-
-
-def adam_update(pieces, first_rows, second_rows, weight_rows, signs, walsh, workers):
+            per_owner = nb_ref.shape[2] // HB
+            owner_cols = slice((a % per_owner) * HB, (a % per_owner + 1) * HB)
+            nb_ref[a // per_owner, g * 8:g * 8 + 8, owner_cols] = updated.astype(nb_ref.dtype)
+
+
+def adam_update(pieces, first_rows, second_rows, weight_rows, signs, walsh, workers, owners):
     rows, width = first_rows.shape
     f32 = jax.ShapeDtypeStruct((rows, width), jnp.float32)
     nf, ns, nw, nb = pl.pallas_call(
         functools.partial(update_kernel, workers),
-        out_shape=[f32, f32, f32, jax.ShapeDtypeStruct((rows, width), jnp.bfloat16)],
+        out_shape=[f32, f32, f32, jax.ShapeDtypeStruct((owners, rows, width // owners), jnp.bfloat16)],
         scratch_shapes=[pltpu.VMEM((rows, width), jnp.float32), pltpu.VMEM((rows * HA, HB), jnp.float32)],
         cost_estimate=pl.CostEstimate(
             flops=6 * rows * width * HB, transcendentals=rows * width, bytes_accessed=rows * width * 32
@@ -250,13 +252,10 @@
         pieces.append(lax.psum_scatter(partial, "wz", scatter_dimension=0, tiled=True))
         if part < PARTS:
             arrived = send_along_x(terms, x_size)
-    new_first, new_second, new_weights, narrow_weights = adam_update(
-        pieces, first[0], second[0], weights[0], signs, walsh, workers
-    )
     owners = lax.axis_size("tensor")
-    piece_width = new_weights.shape[1] // owners
-    narrow = narrow_weights.reshape(blocks, owners, piece_width)
-    slab_view = jnp.transpose(narrow, (1, 0, 2))
+    new_first, new_second, new_weights, slab_view = adam_update(
+        pieces, first[0], second[0], weights[0], signs, walsh, workers, owners
+    )
     slot_lists = slots[0, 0]
     used_counts = counts[0, 0]
     chosen_pieces = select_pieces(slab_view, slot_lists, used_counts)

time: 190 us -> 190 us (level)
  no operation moved by 1% of the time
where the time goes in v11:
time: 190 us
  waiting for transfers between devices  120 us (63%)
  Pallas kernels  22.1 us (12%)
  blocking collectives  14.3 us (8%)
  between operations  14.1 us (7%)
  starting transfers between devices  10.1 us (5%)
  other arithmetic  5.31 us (3%)
  local copies, waits for them, and re-layouts  3.68 us (2%)
    ppermute x6, waiting for transfers between devices, send_along_x(): arrived.append(lax.ppermute(terms[step], 'wx', pairs))  79.9 us
    reduce_scatter x2, waiting for transfers between devices, per_device(): lax.psum_scatter(partial, 'wz', scatter_dimension=0, tiled=True)  40.5 us
    pallas_call x2, Pallas kernels, decoded_terms(): pl.pallas_call(functools.partial(code_kernel, part, x_size), grid_spec=pl...  18.9 us
    all_to_all x1, blocking collectives, per_device(): lax.all_to_all(chosen_pieces, 'tensor', split_axis=0, concat_axis=0, tile...  14.3 us
    ppermute x6, starting transfers between devices, send_along_x(): arrived.append(lax.ppermute(terms[step], 'wx', pairs))  10 us
    add x2, other arithmetic, sum_arrived(): partial = partial + piece.astype(jnp.float32)  5.13 us
  transfers between devices with their start and end apart: 8, of which 5 were waited for; matrix products, arithmetic and copies ran while one was open for 1% of the time, Pallas kernels for 5%

profile of v11, /device:TPU:1, one launch (start us, length us, event | category | flops | bytes accessed | tf_op | source)
XLA Modules:
  0.0 190.0 jit_solution(17958900585240897760)
XLA Ops:
  7.2 0.0 reduce-scatter.3.cloned.1.call-start
  7.2 9.4 %shard_map.120 = (bf16[128,4096]{1,0:T(8,128)(2,1)}, bf16[128,4096]{1,0:T(8,128)(2,1)}, bf16[128,4096]{1,0:T(8,128)(2,1)}, bf16[128,4096]{1,0:T(8,128)(2,1)}) custom-call(s32[1]{0:T(128)} %bitcast.mx_ref, s32[1,1,1024]{2,1,0:T(1,128)} %sh_ref.3, bf16[32,2,16,4096]{3,2,1,0:T(8,128)(2,1)} %bitcast.19, s32[1,4096]{1,0:T(1,128)} %sg_ref.5, ...), custom_call_target="tpu_custom_call" | custom-call | flops 553648128 | bytes 8388608 | tf_op jit(solution)/shard_map/pallas_call | solution.py:141
  16.7 2.0 %collective-permute-start = (bf16[128,4096]{1,0:T(8,128)(2,1)}, bf16[128,4096]{1,0:T(8,128)(2,1)S(1)}, u32[]{:S(2)}, u32[]{:S(2)}) collective-permute-start(bf16[128,4096]{1,0:T(8,128)(2,1)} %get-tuple-element.25), channel_id=1, source_target_pairs={{0,64},{64,128},{128,192},{192,0},{1,65},{65,129},{129,193},{193,1... | collective-permute-start | bytes 3145736 | tf_op jit(solution)/shard_map/ppermute | solution.py:217
  18.7 2.4 %collective-permute-start.1 = (bf16[128,4096]{1,0:T(8,128)(2,1)}, bf16[128,4096]{1,0:T(8,128)(2,1)S(1)}, u32[]{:S(2)}, u32[]{:S(2)}) collective-permute-start(bf16[128,4096]{1,0:T(8,128)(2,1)} %get-tuple-element.26), channel_id=1, source_target_pairs={{0,128},{64,192},{128,0},{192,64},{1,129},{65,193},{129,1},{193,65... | collective-permute-start | bytes 3145736 | tf_op jit(solution)/shard_map/ppermute | solution.py:217
  21.1 0.0 copy-start.1
  21.1 1.2 collective-permute-start.2
  22.3 9.4 %shard_map.121 = (bf16[128,4096]{1,0:T(8,128)(2,1)}, bf16[128,4096]{1,0:T(8,128)(2,1)}, bf16[128,4096]{1,0:T(8,128)(2,1)}, bf16[128,4096]{1,0:T(8,128)(2,1)}) custom-call(s32[1]{0:T(128)} %bitcast.mx_ref, s32[1,1,1024]{2,1,0:T(1,128)} %sh_ref.3, bf16[32,2,16,4096]{3,2,1,0:T(8,128)(2,1)} %bitcast.20, s32[1,4096]{1,0:T(1,128)} %sg_ref.5, ...), custom_call_target="tpu_custom_call" | custom-call | flops 553648128 | bytes 8388608 | tf_op jit(solution)/shard_map/pallas_call | solution.py:141
  31.7 9.1 %collective-permute-done = bf16[128,4096]{1,0:T(8,128)(2,1)S(1)} collective-permute-done((bf16[128,4096]{1,0:T(8,128)(2,1)}, bf16[128,4096]{1,0:T(8,128)(2,1)S(1)}, u32[]{:S(2)}, u32[]{:S(2)}) %collective-permute-start) | collective-permute-done | bytes 1048608 | tf_op jit(solution)/shard_map/ppermute | solution.py:217
  40.8 25.6 %collective-permute-done.1 = bf16[128,4096]{1,0:T(8,128)(2,1)S(1)} collective-permute-done((bf16[128,4096]{1,0:T(8,128)(2,1)}, bf16[128,4096]{1,0:T(8,128)(2,1)S(1)}, u32[]{:S(2)}, u32[]{:S(2)}) %collective-permute-start.1) | collective-permute-done | bytes 1048608 | tf_op jit(solution)/shard_map/ppermute | solution.py:217
  66.4 0.0 collective-permute-done.2
  66.4 0.0 copy-done.1
  66.4 3.2 %convert_add_fusion.1 = f32[128,4096]{1,0:T(8,128)} fusion(bf16[128,4096]{1,0:T(8,128)(2,1)} %collective-permute-done.2, bf16[128,4096]{1,0:T(8,128)(2,1)S(1)} %collective-permute-done.1, bf16[128,4096]{1,0:T(8,128)(2,1)S(1)} %collective-permute-done, bf16[128,4096]{1,0:T(8,128)(2,1)S(1)} %copy-done.1), kind=kLoop, calls=%fused_computation.2 | loop fusion | flops 3670016 | bytes 6291456 | tf_op jit(solution)/shard_map/add | solution.py:224
  69.6 0.0 copy-start.4
  69.6 0.0 copy-start
  69.6 0.0 reduce-scatter.3.cloned.1.call-update
  69.6 0.0 reduce-scatter.5.cloned.1.call-start
  69.7 1.2 collective-permute-start.3
  70.9 3.0 %collective-permute-start.4 = (bf16[128,4096]{1,0:T(8,128)(2,1)}, bf16[128,4096]{1,0:T(8,128)(2,1)S(1)}, u32[]{:S(2)}, u32[]{:S(2)}) collective-permute-start(bf16[128,4096]{1,0:T(8,128)(2,1)} %get-tuple-element.38), channel_id=1, source_target_pairs={{0,128},{64,192},{128,0},{192,64},{1,129},{65,193},{129,1},{193,65... | collective-permute-start | bytes 3145736 | tf_op jit(solution)/shard_map/ppermute | solution.py:217
  73.9 0.0 copy-done.4
  73.9 0.2 collective-permute-start.5
  74.1 20.9 %collective-permute-done.3 = bf16[128,4096]{1,0:T(8,128)(2,1)S(1)} collective-permute-done((bf16[128,4096]{1,0:T(8,128)(2,1)}, bf16[128,4096]{1,0:T(8,128)(2,1)S(1)}, u32[]{:S(2)}, u32[]{:S(2)}) %collective-permute-start.3) | collective-permute-done | bytes 1048608 | tf_op jit(solution)/shard_map/ppermute | solution.py:217
  95.0 24.3 %collective-permute-done.4 = bf16[128,4096]{1,0:T(8,128)(2,1)S(1)} collective-permute-done((bf16[128,4096]{1,0:T(8,128)(2,1)}, bf16[128,4096]{1,0:T(8,128)(2,1)S(1)}, u32[]{:S(2)}, u32[]{:S(2)}) %collective-permute-start.4) | collective-permute-done | bytes 1048608 | tf_op jit(solution)/shard_map/ppermute | solution.py:217
  119.3 0.0 collective-permute-done.5
  119.3 0.0 copy-done
  119.3 1.9 %convert_add_fusion = f32[128,4096]{1,0:T(8,128)} fusion(bf16[128,4096]{1,0:T(8,128)(2,1)S(1)} %collective-permute-done.5, bf16[128,4096]{1,0:T(8,128)(2,1)S(1)} %collective-permute-done.4, bf16[128,4096]{1,0:T(8,128)(2,1)S(1)} %collective-permute-done.3, bf16[128,4096]{1,0:T(8,128)(2,1)S(1)} %copy-done), kind=kLoop, calls=%fused_computation.1 | loop fusion | flops 3670016 | bytes 6291456 | tf_op jit(solution)/shard_map/add | solution.py:224
  121.2 0.0 copy-start.2
  121.2 0.0 copy-start.3
  121.2 0.0 reduce-scatter.5.cloned.1.call-update
  121.3 0.7 copy-done.2
  121.9 0.1 reshape.81
  122.0 0.0 copy-done.3
  122.0 0.1 iota_compare_fusion
  122.1 0.0 reduce-scatter.3.cloned.1.call-done.p0_ref
  122.1 40.5 %reduce-scatter.5.cloned.1.call-done.p1_ref = f32[16,4096]{1,0:T(8,128)} async-done(((f32[128,4096]{1,0:T(8,128)}), f32[16,4096]{1,0:T(8,128)}) %reduce-scatter.5.cloned.1.call-update) | async-done | bytes 262160 | tf_op jit(solution)/shard_map/reduce_scatter | solution.py:252
  162.6 3.2 %shard_map.122 = (f32[32,4096]{1,0:T(8,128)}, f32[32,4096]{1,0:T(8,128)}, f32[32,4096]{1,0:T(8,128)}, bf16[8,32,512]{2,1,0:T(8,128)(2,1)}) custom-call(f32[16,4096]{1,0:T(8,128)} %reduce-scatter.3.cloned.1.call-done.p0_ref, f32[16,4096]{1,0:T(8,128)} %reduce-scatter.5.cloned.1.call-done.p1_ref, f32[32,4096]{1,0:T(8,128)} %bitcast.23, f32[32,4096]{1,0:T(8,128)} %bitcast.24, ...), custom_call_target="tpu_custom_call" | custom-call | flops 100663296 | bytes 4194304 | tf_op jit(solution)/shard_map/pallas_call | solution.py:202
  165.8 2.3 %gather_fusion = bf16[128,512]{1,0:T(8,128)(2,1)S(1)} fusion(bf16[8,32,512]{2,1,0:T(8,128)(2,1)} %get-tuple-element.43, s32[128]{0:T(128)S(1)} %reshape.81), kind=kCustom, calls=%fused_computation | custom fusion | bytes 263168 | tf_op jit(solution)/shard_map/jit(take_along_axis)/gather | solution.py:229
  168.1 0.1 select_select_fusion
  168.2 14.3 %all_to_all.5 = bf16[8,16,512]{2,1,0:T(8,128)(2,1)S(1)} all-to-all(bf16[8,16,512]{2,1,0:T(8,128)(2,1)S(1)} %select_select_fusion), channel_id=1, replica_groups=mesh['wx'=4,'wz'=8,'tensor'=8] {'tensor'}, dimensions={0} | all-to-all | bytes 262144 | tf_op jit(solution)/shard_map/all_to_all | solution.py:262
  182.5 0.7 copy.14
  (1 shorter events, 0.0 us)
Async XLA Ops:
  7.2 114.9 %reduce-scatter.3.cloned.1.call-start = ((), (), s32[]{:S(2)}) async-start(), calls=%async_computation.3 | async-start | bytes 2359296 | tf_op jit(solution)/shard_map/reduce_scatter | solution.py:252
  16.7 24.2 %collective-permute-start = (bf16[128,4096]{1,0:T(8,128)(2,1)}, bf16[128,4096]{1,0:T(8,128)(2,1)S(1)}, u32[]{:S(2)}, u32[]{:S(2)}) collective-permute-start(bf16[128,4096]{1,0:T(8,128)(2,1)} %get-tuple-element.25), channel_id=1, source_target_pairs={{0,64},{64,128},{128,192},{192,0},{1,65},{65,129},{129,193},{193,1... | collective-permute-start | bytes 3145736 | tf_op jit(solution)/shard_map/ppermute | solution.py:217
  18.7 47.7 %collective-permute-start.1 = (bf16[128,4096]{1,0:T(8,128)(2,1)}, bf16[128,4096]{1,0:T(8,128)(2,1)S(1)}, u32[]{:S(2)}, u32[]{:S(2)}) collective-permute-start(bf16[128,4096]{1,0:T(8,128)(2,1)} %get-tuple-element.26), channel_id=1, source_target_pairs={{0,128},{64,192},{128,0},{192,64},{1,129},{65,193},{129,1},{193,65... | collective-permute-start | bytes 3145736 | tf_op jit(solution)/shard_map/ppermute | solution.py:217
  21.1 45.3 %copy-start.1 = (bf16[128,4096]{1,0:T(8,128)(2,1)S(1)}, bf16[128,4096]{1,0:T(8,128)(2,1)}, u32[]{:S(2)}) copy-start(bf16[128,4096]{1,0:T(8,128)(2,1)} %get-tuple-element.32) | copy-start | bytes 3145732
  21.1 45.3 %collective-permute-start.2 = (bf16[128,4096]{1,0:T(8,128)(2,1)}, bf16[128,4096]{1,0:T(8,128)(2,1)}, u32[]{:S(2)}, u32[]{:S(2)}) collective-permute-start(bf16[128,4096]{1,0:T(8,128)(2,1)} %get-tuple-element.27), channel_id=1, source_target_pairs={{0,192},{64,0},{128,64},{192,128},{1,193},{65,1},{129,65},{193,129... | collective-permute-start | bytes 3145736 | tf_op jit(solution)/shard_map/ppermute | solution.py:217
  69.6 4.3 %copy-start.4 = (bf16[128,4096]{1,0:T(8,128)(2,1)S(1)}, bf16[128,4096]{1,0:T(8,128)(2,1)}, u32[]{:S(2)}) copy-start(bf16[128,4096]{1,0:T(8,128)(2,1)} %get-tuple-element.39) | copy-start | bytes 3145732
  69.6 49.7 %copy-start = (bf16[128,4096]{1,0:T(8,128)(2,1)S(1)}, bf16[128,4096]{1,0:T(8,128)(2,1)}, u32[]{:S(2)}) copy-start(bf16[128,4096]{1,0:T(8,128)(2,1)} %get-tuple-element.36) | copy-start | bytes 3145732
  69.6 92.9 %reduce-scatter.5.cloned.1.call-start = ((), (), s32[]{:S(2)}) async-start(), calls=%async_computation.4 | async-start | bytes 2359296 | tf_op jit(solution)/shard_map/reduce_scatter | solution.py:252
  69.7 25.3 %collective-permute-start.3 = (bf16[128,4096]{1,0:T(8,128)(2,1)}, bf16[128,4096]{1,0:T(8,128)(2,1)S(1)}, u32[]{:S(2)}, u32[]{:S(2)}) collective-permute-start(bf16[128,4096]{1,0:T(8,128)(2,1)} %get-tuple-element.37), channel_id=1, source_target_pairs={{0,64},{64,128},{128,192},{192,0},{1,65},{65,129},{129,193},{193,1... | collective-permute-start | bytes 3145736 | tf_op jit(solution)/shard_map/ppermute | solution.py:217
  70.9 48.4 %collective-permute-start.4 = (bf16[128,4096]{1,0:T(8,128)(2,1)}, bf16[128,4096]{1,0:T(8,128)(2,1)S(1)}, u32[]{:S(2)}, u32[]{:S(2)}) collective-permute-start(bf16[128,4096]{1,0:T(8,128)(2,1)} %get-tuple-element.38), channel_id=1, source_target_pairs={{0,128},{64,192},{128,0},{192,64},{1,129},{65,193},{129,1},{193,65... | collective-permute-start | bytes 3145736 | tf_op jit(solution)/shard_map/ppermute | solution.py:217
  73.9 45.4 %collective-permute-start.5 = (bf16[128,4096]{1,0:T(8,128)(2,1)S(1)}, bf16[128,4096]{1,0:T(8,128)(2,1)S(1)}, u32[]{:S(2)}, u32[]{:S(2)}) collective-permute-start(bf16[128,4096]{1,0:T(8,128)(2,1)S(1)} %copy-done.4), channel_id=1, source_target_pairs={{0,192},{64,0},{128,64},{192,128},{1,193},{65,1},{129,65},{193,129... | collective-permute-start | bytes 3145736 | tf_op jit(solution)/shard_map/ppermute | solution.py:217
  121.2 0.7 copy-start.2
  121.2 0.8 copy-start.3
Sparse Core Ops, SparseCore 0:
  69.7 42.0 reduce-scatter.2
  121.4 41.1 reduce-scatter.4

commit v12 on v11

--- a/solution.py
+++ b/solution.py
@@ -160,8 +160,8 @@
     )(my_x, shifts, grad_groups, signs, walsh)
 
 
-def update_kernel(workers, p0_ref, p1_ref, f_ref, s_ref, w_ref, sg_ref, h_ref,
-                  nf_ref, ns_ref, nw_ref, nb_ref, sd_ref, y_ref):
+def update_kernel(workers, p0_ref, p1_ref, f_ref, s_ref, w_ref, sg_ref, h_ref, sl_ref, ct_ref,
+                  nf_ref, ns_ref, nw_ref, ch_ref, sd_ref, y_ref):
     half = p0_ref.shape[0]
     rows_all = 2 * half
     for part, p_ref in enumerate((p0_ref, p1_ref)):
@@ -191,23 +191,31 @@
             step = blocks[a] * (1.0 / math.sqrt(HA * HB)) * sign
             updated = w_ref[g * 8:g * 8 + 8, cols] - learn_rate * step
             nw_ref[g * 8:g * 8 + 8, cols] = updated
-            per_owner = nb_ref.shape[2] // HB
-            owner_cols = slice((a % per_owner) * HB, (a % per_owner + 1) * HB)
-            nb_ref[a // per_owner, g * 8:g * 8 + 8, owner_cols] = updated.astype(nb_ref.dtype)
-
-
-def adam_update(pieces, first_rows, second_rows, weight_rows, signs, walsh, workers, owners):
+    owners, slots_per_list, piece_width = ch_ref.shape
+    for owner in range(owners):
+        used = ct_ref[0, 0, owner]
+        owner_cols = slice(owner * piece_width, (owner + 1) * piece_width)
+        for slot in range(slots_per_list):
+            piece = nw_ref[pl.ds(sl_ref[0, 0, owner, slot], 1), owner_cols]
+            ch_ref[owner, slot:slot + 1, :] = jnp.where(slot < used, piece, 0.0)
+
+
+def adam_update(pieces, first_rows, second_rows, weight_rows, signs, walsh, workers, slots, counts):
     rows, width = first_rows.shape
+    owners, cap = slots.shape[2], slots.shape[3]
     f32 = jax.ShapeDtypeStruct((rows, width), jnp.float32)
-    nf, ns, nw, nb = pl.pallas_call(
+    vmem = pl.BlockSpec(memory_space=pltpu.VMEM)
+    smem = pl.BlockSpec(memory_space=pltpu.SMEM)
+    return pl.pallas_call(
         functools.partial(update_kernel, workers),
-        out_shape=[f32, f32, f32, jax.ShapeDtypeStruct((owners, rows, width // owners), jnp.bfloat16)],
+        in_specs=[vmem] * 7 + [smem, smem],
+        out_specs=[vmem] * 4,
+        out_shape=[f32, f32, f32, jax.ShapeDtypeStruct((owners, cap, width // owners), jnp.float32)],
         scratch_shapes=[pltpu.VMEM((rows, width), jnp.float32), pltpu.VMEM((rows * HA, HB), jnp.float32)],
         cost_estimate=pl.CostEstimate(
             flops=6 * rows * width * HB, transcendentals=rows * width, bytes_accessed=rows * width * 32
         ),
-    )(pieces[0], pieces[1], first_rows, second_rows, weight_rows, signs, walsh)
-    return nf, ns, nw, nb
+    )(pieces[0], pieces[1], first_rows, second_rows, weight_rows, signs, walsh, slots, counts)
 
 
 def send_along_x(terms, x_size):
@@ -252,13 +260,10 @@
         pieces.append(lax.psum_scatter(partial, "wz", scatter_dimension=0, tiled=True))
         if part < PARTS:
             arrived = send_along_x(terms, x_size)
-    owners = lax.axis_size("tensor")
-    new_first, new_second, new_weights, slab_view = adam_update(
-        pieces, first[0], second[0], weights[0], signs, walsh, workers, owners
-    )
-    slot_lists = slots[0, 0]
-    used_counts = counts[0, 0]
-    chosen_pieces = select_pieces(slab_view, slot_lists, used_counts)
+    new_first, new_second, new_weights, chosen_pieces = adam_update(
+        pieces, first[0], second[0], weights[0], signs, walsh, workers, slots, counts
+    )
+    chosen_pieces = chosen_pieces.astype(jnp.bfloat16)
     arrived = lax.all_to_all(chosen_pieces, "tensor", split_axis=0, concat_axis=0, tiled=True)
     return (new_first[None], new_second[None], new_weights[None], arrived[None, None])
 

time: 190 us -> 189 us (level)
  local copies, waits for them, and re-layouts: 3.68 us -> 0.67 us
    gather x2 -> x0, local copies, waits for them, and re-layouts: 2.35 us -> none  [select_pieces(): gathered = jnp.take_along_axis(slab_view, slot_lists[:, :, None], axis=1)]
where the time goes in v12:
time: 189 us
  waiting for transfers between devices  121 us (64%)
  Pallas kernels  22.2 us (12%)
  blocking collectives  14.3 us (8%)
  between operations  14.1 us (7%)
  starting transfers between devices  10.1 us (5%)
  other arithmetic  6.09 us (3%)
    ppermute x6, waiting for transfers between devices, send_along_x(): arrived.append(lax.ppermute(terms[step], 'wx', pairs))  79.9 us
    reduce_scatter x2, waiting for transfers between devices, per_device(): lax.psum_scatter(partial, 'wz', scatter_dimension=0, tiled=True)  41.3 us
    pallas_call x2, Pallas kernels, decoded_terms(): pl.pallas_call(functools.partial(code_kernel, part, x_size), grid_spec=pl...  18.9 us
    all_to_all x1, blocking collectives, per_device(): lax.all_to_all(chosen_pieces, 'tensor', split_axis=0, concat_axis=0, tile...  14.3 us
    ppermute x6, starting transfers between devices, send_along_x(): arrived.append(lax.ppermute(terms[step], 'wx', pairs))  10 us
    add x2, other arithmetic, sum_arrived(): partial = partial + piece.astype(jnp.float32)  5.12 us
  transfers between devices with their start and end apart: 8, of which 5 were waited for; matrix products, arithmetic and copies ran while one was open for 1% of the time, Pallas kernels for 5%

profile of v12, /device:TPU:1, one launch (start us, length us, event | category | flops | bytes accessed | tf_op | source)
XLA Modules:
  0.0 188.7 jit_solution(14442346714326075955)
XLA Ops:
  7.2 0.0 reduce-scatter.3.cloned.1.call-start
  7.2 9.4 %shard_map.120 = (bf16[128,4096]{1,0:T(8,128)(2,1)}, bf16[128,4096]{1,0:T(8,128)(2,1)}, bf16[128,4096]{1,0:T(8,128)(2,1)}, bf16[128,4096]{1,0:T(8,128)(2,1)}) custom-call(s32[1]{0:T(128)} %bitcast.mx_ref, s32[1,1,1024]{2,1,0:T(1,128)} %sh_ref.3, bf16[32,2,16,4096]{3,2,1,0:T(8,128)(2,1)} %bitcast.9, s32[1,4096]{1,0:T(1,128)} %sg_ref.5, ...), custom_call_target="tpu_custom_call" | custom-call | flops 553648128 | bytes 8388608 | tf_op jit(solution)/shard_map/pallas_call | solution.py:141
  16.7 2.0 %collective-permute-start = (bf16[128,4096]{1,0:T(8,128)(2,1)}, bf16[128,4096]{1,0:T(8,128)(2,1)S(1)}, u32[]{:S(2)}, u32[]{:S(2)}) collective-permute-start(bf16[128,4096]{1,0:T(8,128)(2,1)} %get-tuple-element.25), channel_id=1, source_target_pairs={{0,64},{64,128},{128,192},{192,0},{1,65},{65,129},{129,193},{193,1... | collective-permute-start | bytes 3145736 | tf_op jit(solution)/shard_map/ppermute | solution.py:225
  18.7 2.4 %collective-permute-start.1 = (bf16[128,4096]{1,0:T(8,128)(2,1)}, bf16[128,4096]{1,0:T(8,128)(2,1)S(1)}, u32[]{:S(2)}, u32[]{:S(2)}) collective-permute-start(bf16[128,4096]{1,0:T(8,128)(2,1)} %get-tuple-element.26), channel_id=1, source_target_pairs={{0,128},{64,192},{128,0},{192,64},{1,129},{65,193},{129,1},{193,65... | collective-permute-start | bytes 3145736 | tf_op jit(solution)/shard_map/ppermute | solution.py:225
  21.1 0.0 copy-start.1
  21.1 1.2 collective-permute-start.2
  22.3 9.4 %shard_map.121 = (bf16[128,4096]{1,0:T(8,128)(2,1)}, bf16[128,4096]{1,0:T(8,128)(2,1)}, bf16[128,4096]{1,0:T(8,128)(2,1)}, bf16[128,4096]{1,0:T(8,128)(2,1)}) custom-call(s32[1]{0:T(128)} %bitcast.mx_ref, s32[1,1,1024]{2,1,0:T(1,128)} %sh_ref.3, bf16[32,2,16,4096]{3,2,1,0:T(8,128)(2,1)} %bitcast.10, s32[1,4096]{1,0:T(1,128)} %sg_ref.5, ...), custom_call_target="tpu_custom_call" | custom-call | flops 553648128 | bytes 8388608 | tf_op jit(solution)/shard_map/pallas_call | solution.py:141
  31.7 9.1 %collective-permute-done = bf16[128,4096]{1,0:T(8,128)(2,1)S(1)} collective-permute-done((bf16[128,4096]{1,0:T(8,128)(2,1)}, bf16[128,4096]{1,0:T(8,128)(2,1)S(1)}, u32[]{:S(2)}, u32[]{:S(2)}) %collective-permute-start) | collective-permute-done | bytes 1048608 | tf_op jit(solution)/shard_map/ppermute | solution.py:225
  40.8 25.6 %collective-permute-done.1 = bf16[128,4096]{1,0:T(8,128)(2,1)S(1)} collective-permute-done((bf16[128,4096]{1,0:T(8,128)(2,1)}, bf16[128,4096]{1,0:T(8,128)(2,1)S(1)}, u32[]{:S(2)}, u32[]{:S(2)}) %collective-permute-start.1) | collective-permute-done | bytes 1048608 | tf_op jit(solution)/shard_map/ppermute | solution.py:225
  66.4 0.0 collective-permute-done.2
  66.4 0.0 copy-done.1
  66.4 3.2 %convert_add_fusion.1 = f32[128,4096]{1,0:T(8,128)} fusion(bf16[128,4096]{1,0:T(8,128)(2,1)} %collective-permute-done.2, bf16[128,4096]{1,0:T(8,128)(2,1)S(1)} %collective-permute-done.1, bf16[128,4096]{1,0:T(8,128)(2,1)S(1)} %collective-permute-done, bf16[128,4096]{1,0:T(8,128)(2,1)S(1)} %copy-done.1), kind=kLoop, calls=%fused_computation.1 | loop fusion | flops 3670016 | bytes 6291456 | tf_op jit(solution)/shard_map/add | solution.py:232
  69.6 0.0 copy-start.2
  69.6 0.0 copy-start
  69.6 0.0 reduce-scatter.3.cloned.1.call-update
  69.6 0.0 reduce-scatter.5.cloned.1.call-start
  69.7 1.2 collective-permute-start.3
  70.9 3.0 %collective-permute-start.4 = (bf16[128,4096]{1,0:T(8,128)(2,1)}, bf16[128,4096]{1,0:T(8,128)(2,1)S(1)}, u32[]{:S(2)}, u32[]{:S(2)}) collective-permute-start(bf16[128,4096]{1,0:T(8,128)(2,1)} %get-tuple-element.38), channel_id=1, source_target_pairs={{0,128},{64,192},{128,0},{192,64},{1,129},{65,193},{129,1},{193,65... | collective-permute-start | bytes 3145736 | tf_op jit(solution)/shard_map/ppermute | solution.py:225
  73.8 0.0 copy-done.2
  73.8 0.2 collective-permute-start.5
  74.1 20.9 %collective-permute-done.3 = bf16[128,4096]{1,0:T(8,128)(2,1)S(1)} collective-permute-done((bf16[128,4096]{1,0:T(8,128)(2,1)}, bf16[128,4096]{1,0:T(8,128)(2,1)S(1)}, u32[]{:S(2)}, u32[]{:S(2)}) %collective-permute-start.3) | collective-permute-done | bytes 1048608 | tf_op jit(solution)/shard_map/ppermute | solution.py:225
  95.0 24.3 %collective-permute-done.4 = bf16[128,4096]{1,0:T(8,128)(2,1)S(1)} collective-permute-done((bf16[128,4096]{1,0:T(8,128)(2,1)}, bf16[128,4096]{1,0:T(8,128)(2,1)S(1)}, u32[]{:S(2)}, u32[]{:S(2)}) %collective-permute-start.4) | collective-permute-done | bytes 1048608 | tf_op jit(solution)/shard_map/ppermute | solution.py:225
  119.3 0.0 collective-permute-done.5
  119.3 0.0 copy-done
  119.3 1.9 %convert_add_fusion = f32[128,4096]{1,0:T(8,128)} fusion(bf16[128,4096]{1,0:T(8,128)(2,1)S(1)} %collective-permute-done.5, bf16[128,4096]{1,0:T(8,128)(2,1)S(1)} %collective-permute-done.4, bf16[128,4096]{1,0:T(8,128)(2,1)S(1)} %collective-permute-done.3, bf16[128,4096]{1,0:T(8,128)(2,1)S(1)} %copy-done), kind=kLoop, calls=%fused_computation | loop fusion | flops 3670016 | bytes 6291456 | tf_op jit(solution)/shard_map/add | solution.py:232
  121.2 0.0 reduce-scatter.5.cloned.1.call-update
  121.3 0.0 reduce-scatter.3.cloned.1.call-done.p0_ref
  121.3 41.2 %reduce-scatter.5.cloned.1.call-done.p1_ref = f32[16,4096]{1,0:T(8,128)} async-done(((f32[128,4096]{1,0:T(8,128)}), f32[16,4096]{1,0:T(8,128)}) %reduce-scatter.5.cloned.1.call-update) | async-done | bytes 262160 | tf_op jit(solution)/shard_map/reduce_scatter | solution.py:260
  162.5 3.3 %shard_map.122 = (f32[32,4096]{1,0:T(8,128)}, f32[32,4096]{1,0:T(8,128)}, f32[32,4096]{1,0:T(8,128)}, f32[8,16,512]{2,1,0:T(8,128)}) custom-call(f32[16,4096]{1,0:T(8,128)} %reduce-scatter.3.cloned.1.call-done.p0_ref, f32[16,4096]{1,0:T(8,128)} %reduce-scatter.5.cloned.1.call-done.p1_ref, f32[32,4096]{1,0:T(8,128)} %bitcast.11, f32[32,4096]{1,0:T(8,128)} %bitcast.12, ...), custom_call_target="tpu_custom_call" | custom-call | flops 100663296 | bytes 4194304 | tf_op jit(solution)/shard_map/pallas_call | solution.py:209
  165.8 1.0 convert_element_type.35
  166.8 14.3 %all_to_all.5 = bf16[8,16,512]{2,1,0:T(8,128)(2,1)S(1)} all-to-all(bf16[8,16,512]{2,1,0:T(8,128)(2,1)S(1)} %convert_element_type.35), channel_id=1, replica_groups=mesh['wx'=4,'wz'=8,'tensor'=8] {'tensor'}, dimensions={0} | all-to-all | bytes 262144 | tf_op jit(solution)/shard_map/all_to_all | solution.py:267
  181.2 0.7 copy.14
Async XLA Ops:
  7.2 114.1 %reduce-scatter.3.cloned.1.call-start = ((), (), s32[]{:S(2)}) async-start(), calls=%async_computation.3 | async-start | bytes 2359296 | tf_op jit(solution)/shard_map/reduce_scatter | solution.py:260
  16.7 24.2 %collective-permute-start = (bf16[128,4096]{1,0:T(8,128)(2,1)}, bf16[128,4096]{1,0:T(8,128)(2,1)S(1)}, u32[]{:S(2)}, u32[]{:S(2)}) collective-permute-start(bf16[128,4096]{1,0:T(8,128)(2,1)} %get-tuple-element.25), channel_id=1, source_target_pairs={{0,64},{64,128},{128,192},{192,0},{1,65},{65,129},{129,193},{193,1... | collective-permute-start | bytes 3145736 | tf_op jit(solution)/shard_map/ppermute | solution.py:225
  18.7 47.7 %collective-permute-start.1 = (bf16[128,4096]{1,0:T(8,128)(2,1)}, bf16[128,4096]{1,0:T(8,128)(2,1)S(1)}, u32[]{:S(2)}, u32[]{:S(2)}) collective-permute-start(bf16[128,4096]{1,0:T(8,128)(2,1)} %get-tuple-element.26), channel_id=1, source_target_pairs={{0,128},{64,192},{128,0},{192,64},{1,129},{65,193},{129,1},{193,65... | collective-permute-start | bytes 3145736 | tf_op jit(solution)/shard_map/ppermute | solution.py:225
  21.1 45.3 %copy-start.1 = (bf16[128,4096]{1,0:T(8,128)(2,1)S(1)}, bf16[128,4096]{1,0:T(8,128)(2,1)}, u32[]{:S(2)}) copy-start(bf16[128,4096]{1,0:T(8,128)(2,1)} %get-tuple-element.32) | copy-start | bytes 3145732
  21.1 45.3 %collective-permute-start.2 = (bf16[128,4096]{1,0:T(8,128)(2,1)}, bf16[128,4096]{1,0:T(8,128)(2,1)}, u32[]{:S(2)}, u32[]{:S(2)}) collective-permute-start(bf16[128,4096]{1,0:T(8,128)(2,1)} %get-tuple-element.27), channel_id=1, source_target_pairs={{0,192},{64,0},{128,64},{192,128},{1,193},{65,1},{129,65},{193,129... | collective-permute-start | bytes 3145736 | tf_op jit(solution)/shard_map/ppermute | solution.py:225
  69.6 4.3 %copy-start.2 = (bf16[128,4096]{1,0:T(8,128)(2,1)S(1)}, bf16[128,4096]{1,0:T(8,128)(2,1)}, u32[]{:S(2)}) copy-start(bf16[128,4096]{1,0:T(8,128)(2,1)} %get-tuple-element.39) | copy-start | bytes 3145732
  69.6 49.7 %copy-start = (bf16[128,4096]{1,0:T(8,128)(2,1)S(1)}, bf16[128,4096]{1,0:T(8,128)(2,1)}, u32[]{:S(2)}) copy-start(bf16[128,4096]{1,0:T(8,128)(2,1)} %get-tuple-element.36) | copy-start | bytes 3145732
  69.6 92.9 %reduce-scatter.5.cloned.1.call-start = ((), (), s32[]{:S(2)}) async-start(), calls=%async_computation.4 | async-start | bytes 2359296 | tf_op jit(solution)/shard_map/reduce_scatter | solution.py:260
  69.7 25.3 %collective-permute-start.3 = (bf16[128,4096]{1,0:T(8,128)(2,1)}, bf16[128,4096]{1,0:T(8,128)(2,1)S(1)}, u32[]{:S(2)}, u32[]{:S(2)}) collective-permute-start(bf16[128,4096]{1,0:T(8,128)(2,1)} %get-tuple-element.37), channel_id=1, source_target_pairs={{0,64},{64,128},{128,192},{192,0},{1,65},{65,129},{129,193},{193,1... | collective-permute-start | bytes 3145736 | tf_op jit(solution)/shard_map/ppermute | solution.py:225
  70.9 48.4 %collective-permute-start.4 = (bf16[128,4096]{1,0:T(8,128)(2,1)}, bf16[128,4096]{1,0:T(8,128)(2,1)S(1)}, u32[]{:S(2)}, u32[]{:S(2)}) collective-permute-start(bf16[128,4096]{1,0:T(8,128)(2,1)} %get-tuple-element.38), channel_id=1, source_target_pairs={{0,128},{64,192},{128,0},{192,64},{1,129},{65,193},{129,1},{193,65... | collective-permute-start | bytes 3145736 | tf_op jit(solution)/shard_map/ppermute | solution.py:225
  73.8 45.4 %collective-permute-start.5 = (bf16[128,4096]{1,0:T(8,128)(2,1)S(1)}, bf16[128,4096]{1,0:T(8,128)(2,1)S(1)}, u32[]{:S(2)}, u32[]{:S(2)}) collective-permute-start(bf16[128,4096]{1,0:T(8,128)(2,1)S(1)} %copy-done.2), channel_id=1, source_target_pairs={{0,192},{64,0},{128,64},{192,128},{1,193},{65,1},{129,65},{193,129... | collective-permute-start | bytes 3145736 | tf_op jit(solution)/shard_map/ppermute | solution.py:225
Sparse Core Ops, SparseCore 0:
  69.7 42.0 reduce-scatter.2
  121.4 41.1 reduce-scatter.4

commit v13 on v12

--- a/solution.py
+++ b/solution.py
@@ -195,9 +195,11 @@
     for owner in range(owners):
         used = ct_ref[0, 0, owner]
         owner_cols = slice(owner * piece_width, (owner + 1) * piece_width)
+        listed = []
         for slot in range(slots_per_list):
             piece = nw_ref[pl.ds(sl_ref[0, 0, owner, slot], 1), owner_cols]
-            ch_ref[owner, slot:slot + 1, :] = jnp.where(slot < used, piece, 0.0)
+            listed.append(jnp.where(slot < used, piece, 0.0))
+        ch_ref[owner] = jnp.concatenate(listed, axis=0).astype(ch_ref.dtype)
 
 
 def adam_update(pieces, first_rows, second_rows, weight_rows, signs, walsh, workers, slots, counts):
@@ -210,7 +212,7 @@
         functools.partial(update_kernel, workers),
         in_specs=[vmem] * 7 + [smem, smem],
         out_specs=[vmem] * 4,
-        out_shape=[f32, f32, f32, jax.ShapeDtypeStruct((owners, cap, width // owners), jnp.float32)],
+        out_shape=[f32, f32, f32, jax.ShapeDtypeStruct((owners, cap, width // owners), jnp.bfloat16)],
         scratch_shapes=[pltpu.VMEM((rows, width), jnp.float32), pltpu.VMEM((rows * HA, HB), jnp.float32)],
         cost_estimate=pl.CostEstimate(
             flops=6 * rows * width * HB, transcendentals=rows * width, bytes_accessed=rows * width * 32
@@ -263,7 +265,6 @@
     new_first, new_second, new_weights, chosen_pieces = adam_update(
         pieces, first[0], second[0], weights[0], signs, walsh, workers, slots, counts
     )
-    chosen_pieces = chosen_pieces.astype(jnp.bfloat16)
     arrived = lax.all_to_all(chosen_pieces, "tensor", split_axis=0, concat_axis=0, tiled=True)
     return (new_first[None], new_second[None], new_weights[None], arrived[None, None])
 

time: 189 us -> 188 us (level)
  no operation moved by 1% of the time
where the time goes in v13:
time: 188 us
  waiting for transfers between devices  121 us (64%)
  Pallas kernels  22.1 us (12%)
  blocking collectives  14.7 us (8%)
  between operations  14.1 us (8%)
  starting transfers between devices  10.1 us (5%)
  other arithmetic  5.12 us (3%)
    ppermute x6, waiting for transfers between devices, send_along_x(): arrived.append(lax.ppermute(terms[step], 'wx', pairs))  79.9 us
    reduce_scatter x2, waiting for transfers between devices, per_device(): lax.psum_scatter(partial, 'wz', scatter_dimension=0, tiled=True)  41 us
    pallas_call x2, Pallas kernels, decoded_terms(): pl.pallas_call(functools.partial(code_kernel, part, x_size), grid_spec=pl...  18.9 us
    all_to_all x1, blocking collectives, per_device(): lax.all_to_all(chosen_pieces, 'tensor', split_axis=0, concat_axis=0, tile...  14.7 us
    ppermute x6, starting transfers between devices, send_along_x(): arrived.append(lax.ppermute(terms[step], 'wx', pairs))  10 us
    add x2, other arithmetic, sum_arrived(): partial = partial + piece.astype(jnp.float32)  5.12 us
  transfers between devices with their start and end apart: 8, of which 5 were waited for; matrix products, arithmetic and copies ran while one was open for 1% of the time, Pallas kernels for 5%

profile of v13, /device:TPU:1, one launch (start us, length us, event | category | flops | bytes accessed | tf_op | source)
XLA Modules:
  0.0 187.8 jit_solution(3477080937345034045)
XLA Ops:
  7.2 0.0 reduce-scatter.3.cloned.1.call-start
  7.2 9.4 %shard_map.120 = (bf16[128,4096]{1,0:T(8,128)(2,1)}, bf16[128,4096]{1,0:T(8,128)(2,1)}, bf16[128,4096]{1,0:T(8,128)(2,1)}, bf16[128,4096]{1,0:T(8,128)(2,1)}) custom-call(s32[1]{0:T(128)} %bitcast.mx_ref, s32[1,1,1024]{2,1,0:T(1,128)} %sh_ref.3, bf16[32,2,16,4096]{3,2,1,0:T(8,128)(2,1)} %bitcast.9, s32[1,4096]{1,0:T(1,128)} %sg_ref.5, ...), custom_call_target="tpu_custom_call" | custom-call | flops 553648128 | bytes 8388608 | tf_op jit(solution)/shard_map/pallas_call | solution.py:141
  16.6 2.0 %collective-permute-start = (bf16[128,4096]{1,0:T(8,128)(2,1)}, bf16[128,4096]{1,0:T(8,128)(2,1)S(1)}, u32[]{:S(2)}, u32[]{:S(2)}) collective-permute-start(bf16[128,4096]{1,0:T(8,128)(2,1)} %get-tuple-element.25), channel_id=1, source_target_pairs={{0,64},{64,128},{128,192},{192,0},{1,65},{65,129},{129,193},{193,1... | collective-permute-start | bytes 3145736 | tf_op jit(solution)/shard_map/ppermute | solution.py:227
  18.7 2.4 %collective-permute-start.1 = (bf16[128,4096]{1,0:T(8,128)(2,1)}, bf16[128,4096]{1,0:T(8,128)(2,1)S(1)}, u32[]{:S(2)}, u32[]{:S(2)}) collective-permute-start(bf16[128,4096]{1,0:T(8,128)(2,1)} %get-tuple-element.26), channel_id=1, source_target_pairs={{0,128},{64,192},{128,0},{192,64},{1,129},{65,193},{129,1},{193,65... | collective-permute-start | bytes 3145736 | tf_op jit(solution)/shard_map/ppermute | solution.py:227
  21.1 0.0 copy-start.1
  21.1 1.2 collective-permute-start.2
  22.3 9.4 %shard_map.121 = (bf16[128,4096]{1,0:T(8,128)(2,1)}, bf16[128,4096]{1,0:T(8,128)(2,1)}, bf16[128,4096]{1,0:T(8,128)(2,1)}, bf16[128,4096]{1,0:T(8,128)(2,1)}) custom-call(s32[1]{0:T(128)} %bitcast.mx_ref, s32[1,1,1024]{2,1,0:T(1,128)} %sh_ref.3, bf16[32,2,16,4096]{3,2,1,0:T(8,128)(2,1)} %bitcast.10, s32[1,4096]{1,0:T(1,128)} %sg_ref.5, ...), custom_call_target="tpu_custom_call" | custom-call | flops 553648128 | bytes 8388608 | tf_op jit(solution)/shard_map/pallas_call | solution.py:141
  31.7 9.1 %collective-permute-done = bf16[128,4096]{1,0:T(8,128)(2,1)S(1)} collective-permute-done((bf16[128,4096]{1,0:T(8,128)(2,1)}, bf16[128,4096]{1,0:T(8,128)(2,1)S(1)}, u32[]{:S(2)}, u32[]{:S(2)}) %collective-permute-start) | collective-permute-done | bytes 1048608 | tf_op jit(solution)/shard_map/ppermute | solution.py:227
  40.8 25.6 %collective-permute-done.1 = bf16[128,4096]{1,0:T(8,128)(2,1)S(1)} collective-permute-done((bf16[128,4096]{1,0:T(8,128)(2,1)}, bf16[128,4096]{1,0:T(8,128)(2,1)S(1)}, u32[]{:S(2)}, u32[]{:S(2)}) %collective-permute-start.1) | collective-permute-done | bytes 1048608 | tf_op jit(solution)/shard_map/ppermute | solution.py:227
  66.4 0.0 collective-permute-done.2
  66.4 0.0 copy-done.1
  66.4 3.2 %convert_add_fusion.1 = f32[128,4096]{1,0:T(8,128)} fusion(bf16[128,4096]{1,0:T(8,128)(2,1)} %collective-permute-done.2, bf16[128,4096]{1,0:T(8,128)(2,1)S(1)} %collective-permute-done.1, bf16[128,4096]{1,0:T(8,128)(2,1)S(1)} %collective-permute-done, bf16[128,4096]{1,0:T(8,128)(2,1)S(1)} %copy-done.1), kind=kLoop, calls=%fused_computation.1 | loop fusion | flops 3670016 | bytes 6291456 | tf_op jit(solution)/shard_map/add | solution.py:234
  69.6 0.0 copy-start.2
  69.6 0.0 copy-start
  69.6 0.0 reduce-scatter.3.cloned.1.call-update
  69.6 0.0 reduce-scatter.5.cloned.1.call-start
  69.7 1.2 collective-permute-start.3
  70.9 3.0 %collective-permute-start.4 = (bf16[128,4096]{1,0:T(8,128)(2,1)}, bf16[128,4096]{1,0:T(8,128)(2,1)S(1)}, u32[]{:S(2)}, u32[]{:S(2)}) collective-permute-start(bf16[128,4096]{1,0:T(8,128)(2,1)} %get-tuple-element.38), channel_id=1, source_target_pairs={{0,128},{64,192},{128,0},{192,64},{1,129},{65,193},{129,1},{193,65... | collective-permute-start | bytes 3145736 | tf_op jit(solution)/shard_map/ppermute | solution.py:227
  73.8 0.0 copy-done.2
  73.8 0.2 collective-permute-start.5
  74.1 20.9 %collective-permute-done.3 = bf16[128,4096]{1,0:T(8,128)(2,1)S(1)} collective-permute-done((bf16[128,4096]{1,0:T(8,128)(2,1)}, bf16[128,4096]{1,0:T(8,128)(2,1)S(1)}, u32[]{:S(2)}, u32[]{:S(2)}) %collective-permute-start.3) | collective-permute-done | bytes 1048608 | tf_op jit(solution)/shard_map/ppermute | solution.py:227
  95.0 24.3 %collective-permute-done.4 = bf16[128,4096]{1,0:T(8,128)(2,1)S(1)} collective-permute-done((bf16[128,4096]{1,0:T(8,128)(2,1)}, bf16[128,4096]{1,0:T(8,128)(2,1)S(1)}, u32[]{:S(2)}, u32[]{:S(2)}) %collective-permute-start.4) | collective-permute-done | bytes 1048608 | tf_op jit(solution)/shard_map/ppermute | solution.py:227
  119.3 0.0 collective-permute-done.5
  119.3 0.0 copy-done
  119.3 1.9 %convert_add_fusion = f32[128,4096]{1,0:T(8,128)} fusion(bf16[128,4096]{1,0:T(8,128)(2,1)S(1)} %collective-permute-done.5, bf16[128,4096]{1,0:T(8,128)(2,1)S(1)} %collective-permute-done.4, bf16[128,4096]{1,0:T(8,128)(2,1)S(1)} %collective-permute-done.3, bf16[128,4096]{1,0:T(8,128)(2,1)S(1)} %copy-done), kind=kLoop, calls=%fused_computation | loop fusion | flops 3670016 | bytes 6291456 | tf_op jit(solution)/shard_map/add | solution.py:234
  121.2 0.0 reduce-scatter.5.cloned.1.call-update
  121.3 0.0 reduce-scatter.3.cloned.1.call-done.p0_ref
  121.3 41.0 %reduce-scatter.5.cloned.1.call-done.p1_ref = f32[16,4096]{1,0:T(8,128)} async-done(((f32[128,4096]{1,0:T(8,128)}), f32[16,4096]{1,0:T(8,128)}) %reduce-scatter.5.cloned.1.call-update) | async-done | bytes 262160 | tf_op jit(solution)/shard_map/reduce_scatter | solution.py:262
  162.3 3.3 %shard_map.122 = (f32[32,4096]{1,0:T(8,128)}, f32[32,4096]{1,0:T(8,128)}, f32[32,4096]{1,0:T(8,128)}, bf16[8,16,512]{2,1,0:T(8,128)(2,1)}) custom-call(f32[16,4096]{1,0:T(8,128)} %reduce-scatter.3.cloned.1.call-done.p0_ref, f32[16,4096]{1,0:T(8,128)} %reduce-scatter.5.cloned.1.call-done.p1_ref, f32[32,4096]{1,0:T(8,128)} %bitcast.11, f32[32,4096]{1,0:T(8,128)} %bitcast.12, ...), custom_call_target="tpu_custom_call" | custom-call | flops 100663296 | bytes 4194304 | tf_op jit(solution)/shard_map/pallas_call | solution.py:211
  165.6 14.7 %all_to_all.5 = bf16[8,16,512]{2,1,0:T(8,128)(2,1)S(1)} all-to-all(bf16[8,16,512]{2,1,0:T(8,128)(2,1)} %get-tuple-element.43), channel_id=1, replica_groups=mesh['wx'=4,'wz'=8,'tensor'=8] {'tensor'}, dimensions={0} | all-to-all | bytes 262144 | tf_op jit(solution)/shard_map/all_to_all | solution.py:268
  180.3 0.7 copy.14
Async XLA Ops:
  7.2 114.1 %reduce-scatter.3.cloned.1.call-start = ((), (), s32[]{:S(2)}) async-start(), calls=%async_computation.3 | async-start | bytes 2359296 | tf_op jit(solution)/shard_map/reduce_scatter | solution.py:262
  16.6 24.2 %collective-permute-start = (bf16[128,4096]{1,0:T(8,128)(2,1)}, bf16[128,4096]{1,0:T(8,128)(2,1)S(1)}, u32[]{:S(2)}, u32[]{:S(2)}) collective-permute-start(bf16[128,4096]{1,0:T(8,128)(2,1)} %get-tuple-element.25), channel_id=1, source_target_pairs={{0,64},{64,128},{128,192},{192,0},{1,65},{65,129},{129,193},{193,1... | collective-permute-start | bytes 3145736 | tf_op jit(solution)/shard_map/ppermute | solution.py:227
  18.7 47.7 %collective-permute-start.1 = (bf16[128,4096]{1,0:T(8,128)(2,1)}, bf16[128,4096]{1,0:T(8,128)(2,1)S(1)}, u32[]{:S(2)}, u32[]{:S(2)}) collective-permute-start(bf16[128,4096]{1,0:T(8,128)(2,1)} %get-tuple-element.26), channel_id=1, source_target_pairs={{0,128},{64,192},{128,0},{192,64},{1,129},{65,193},{129,1},{193,65... | collective-permute-start | bytes 3145736 | tf_op jit(solution)/shard_map/ppermute | solution.py:227
  21.1 45.3 %copy-start.1 = (bf16[128,4096]{1,0:T(8,128)(2,1)S(1)}, bf16[128,4096]{1,0:T(8,128)(2,1)}, u32[]{:S(2)}) copy-start(bf16[128,4096]{1,0:T(8,128)(2,1)} %get-tuple-element.32) | copy-start | bytes 3145732
  21.1 45.3 %collective-permute-start.2 = (bf16[128,4096]{1,0:T(8,128)(2,1)}, bf16[128,4096]{1,0:T(8,128)(2,1)}, u32[]{:S(2)}, u32[]{:S(2)}) collective-permute-start(bf16[128,4096]{1,0:T(8,128)(2,1)} %get-tuple-element.27), channel_id=1, source_target_pairs={{0,192},{64,0},{128,64},{192,128},{1,193},{65,1},{129,65},{193,129... | collective-permute-start | bytes 3145736 | tf_op jit(solution)/shard_map/ppermute | solution.py:227
  69.6 4.3 %copy-start.2 = (bf16[128,4096]{1,0:T(8,128)(2,1)S(1)}, bf16[128,4096]{1,0:T(8,128)(2,1)}, u32[]{:S(2)}) copy-start(bf16[128,4096]{1,0:T(8,128)(2,1)} %get-tuple-element.39) | copy-start | bytes 3145732
  69.6 49.7 %copy-start = (bf16[128,4096]{1,0:T(8,128)(2,1)S(1)}, bf16[128,4096]{1,0:T(8,128)(2,1)}, u32[]{:S(2)}) copy-start(bf16[128,4096]{1,0:T(8,128)(2,1)} %get-tuple-element.36) | copy-start | bytes 3145732
  69.6 92.7 %reduce-scatter.5.cloned.1.call-start = ((), (), s32[]{:S(2)}) async-start(), calls=%async_computation.4 | async-start | bytes 2359296 | tf_op jit(solution)/shard_map/reduce_scatter | solution.py:262
  69.7 25.3 %collective-permute-start.3 = (bf16[128,4096]{1,0:T(8,128)(2,1)}, bf16[128,4096]{1,0:T(8,128)(2,1)S(1)}, u32[]{:S(2)}, u32[]{:S(2)}) collective-permute-start(bf16[128,4096]{1,0:T(8,128)(2,1)} %get-tuple-element.37), channel_id=1, source_target_pairs={{0,64},{64,128},{128,192},{192,0},{1,65},{65,129},{129,193},{193,1... | collective-permute-start | bytes 3145736 | tf_op jit(solution)/shard_map/ppermute | solution.py:227
  70.9 48.4 %collective-permute-start.4 = (bf16[128,4096]{1,0:T(8,128)(2,1)}, bf16[128,4096]{1,0:T(8,128)(2,1)S(1)}, u32[]{:S(2)}, u32[]{:S(2)}) collective-permute-start(bf16[128,4096]{1,0:T(8,128)(2,1)} %get-tuple-element.38), channel_id=1, source_target_pairs={{0,128},{64,192},{128,0},{192,64},{1,129},{65,193},{129,1},{193,65... | collective-permute-start | bytes 3145736 | tf_op jit(solution)/shard_map/ppermute | solution.py:227
  73.8 45.4 %collective-permute-start.5 = (bf16[128,4096]{1,0:T(8,128)(2,1)S(1)}, bf16[128,4096]{1,0:T(8,128)(2,1)S(1)}, u32[]{:S(2)}, u32[]{:S(2)}) collective-permute-start(bf16[128,4096]{1,0:T(8,128)(2,1)S(1)} %copy-done.2), channel_id=1, source_target_pairs={{0,192},{64,0},{128,64},{192,128},{1,193},{65,1},{129,65},{193,129... | collective-permute-start | bytes 3145736 | tf_op jit(solution)/shard_map/ppermute | solution.py:227
Sparse Core Ops, SparseCore 0:
  69.7 42.0 reduce-scatter.2
  121.4 40.8 reduce-scatter.4

commit v14 on v13

--- a/solution.py
+++ b/solution.py
@@ -221,8 +221,9 @@
 
 
 def send_along_x(terms, x_size):
+    far = x_size // 2
     arrived = [terms[0]]
-    for step in range(1, x_size):
+    for step in [far] + [k for k in range(1, x_size) if k != far]:
         pairs = [(i, (i + step) % x_size) for i in range(x_size)]
         arrived.append(lax.ppermute(terms[step], "wx", pairs))
     return arrived

time: 188 us -> 188 us (level)
  no operation moved by 1% of the time
where the time goes in v14:
time: 188 us
  waiting for transfers between devices  121 us (64%)
  Pallas kernels  22.2 us (12%)
  blocking collectives  14.6 us (8%)
  between operations  14.1 us (8%)
  starting transfers between devices  10.4 us (6%)
  other arithmetic  5.12 us (3%)
    ppermute x6, waiting for transfers between devices, send_along_x(): arrived.append(lax.ppermute(terms[step], 'wx', pairs))  79.4 us
    reduce_scatter x2, waiting for transfers between devices, per_device(): lax.psum_scatter(partial, 'wz', scatter_dimension=0, tiled=True)  41.3 us
    pallas_call x2, Pallas kernels, decoded_terms(): pl.pallas_call(functools.partial(code_kernel, part, x_size), grid_spec=pl...  18.9 us
    all_to_all x1, blocking collectives, per_device(): lax.all_to_all(chosen_pieces, 'tensor', split_axis=0, concat_axis=0, tile...  14.6 us
    ppermute x6, starting transfers between devices, send_along_x(): arrived.append(lax.ppermute(terms[step], 'wx', pairs))  10.3 us
    add x2, other arithmetic, sum_arrived(): partial = partial + piece.astype(jnp.float32)  5.12 us
  transfers between devices with their start and end apart: 8, of which 5 were waited for; matrix products, arithmetic and copies ran while one was open for 1% of the time, Pallas kernels for 5%

profile of v14, /device:TPU:1, one launch (start us, length us, event | category | flops | bytes accessed | tf_op | source)
XLA Modules:
  0.0 187.8 jit_solution(17021906635417635789)
XLA Ops:
  7.2 0.0 reduce-scatter.3.cloned.1.call-start
  7.2 9.4 %shard_map.120 = (bf16[128,4096]{1,0:T(8,128)(2,1)}, bf16[128,4096]{1,0:T(8,128)(2,1)}, bf16[128,4096]{1,0:T(8,128)(2,1)}, bf16[128,4096]{1,0:T(8,128)(2,1)}) custom-call(s32[1]{0:T(128)} %bitcast.mx_ref, s32[1,1,1024]{2,1,0:T(1,128)} %sh_ref.3, bf16[32,2,16,4096]{3,2,1,0:T(8,128)(2,1)} %bitcast.9, s32[1,4096]{1,0:T(1,128)} %sg_ref.5, ...), custom_call_target="tpu_custom_call" | custom-call | flops 553648128 | bytes 8388608 | tf_op jit(solution)/shard_map/pallas_call | solution.py:141
  16.6 3.6 %collective-permute-start = (bf16[128,4096]{1,0:T(8,128)(2,1)}, bf16[128,4096]{1,0:T(8,128)(2,1)S(1)}, u32[]{:S(2)}, u32[]{:S(2)}) collective-permute-start(bf16[128,4096]{1,0:T(8,128)(2,1)} %get-tuple-element.25), channel_id=1, source_target_pairs={{0,128},{64,192},{128,0},{192,64},{1,129},{65,193},{129,1},{193,65... | collective-permute-start | bytes 3145736 | tf_op jit(solution)/shard_map/ppermute | solution.py:228
  20.2 0.3 collective-permute-start.1
  20.5 0.0 copy-start.1
  20.5 2.4 %collective-permute-start.2 = (bf16[128,4096]{1,0:T(8,128)(2,1)}, bf16[128,4096]{1,0:T(8,128)(2,1)}, u32[]{:S(2)}, u32[]{:S(2)}) collective-permute-start(bf16[128,4096]{1,0:T(8,128)(2,1)} %get-tuple-element.27), channel_id=1, source_target_pairs={{0,192},{64,0},{128,64},{192,128},{1,193},{65,1},{129,65},{193,129... | collective-permute-start | bytes 3145736 | tf_op jit(solution)/shard_map/ppermute | solution.py:228
  22.9 9.4 %shard_map.121 = (bf16[128,4096]{1,0:T(8,128)(2,1)}, bf16[128,4096]{1,0:T(8,128)(2,1)}, bf16[128,4096]{1,0:T(8,128)(2,1)}, bf16[128,4096]{1,0:T(8,128)(2,1)}) custom-call(s32[1]{0:T(128)} %bitcast.mx_ref, s32[1,1,1024]{2,1,0:T(1,128)} %sh_ref.3, bf16[32,2,16,4096]{3,2,1,0:T(8,128)(2,1)} %bitcast.10, s32[1,4096]{1,0:T(1,128)} %sg_ref.5, ...), custom_call_target="tpu_custom_call" | custom-call | flops 553648128 | bytes 8388608 | tf_op jit(solution)/shard_map/pallas_call | solution.py:141
  32.3 10.1 %collective-permute-done = bf16[128,4096]{1,0:T(8,128)(2,1)S(1)} collective-permute-done((bf16[128,4096]{1,0:T(8,128)(2,1)}, bf16[128,4096]{1,0:T(8,128)(2,1)S(1)}, u32[]{:S(2)}, u32[]{:S(2)}) %collective-permute-start) | collective-permute-done | bytes 1048608 | tf_op jit(solution)/shard_map/ppermute | solution.py:228
  42.5 24.1 %collective-permute-done.1 = bf16[128,4096]{1,0:T(8,128)(2,1)S(1)} collective-permute-done((bf16[128,4096]{1,0:T(8,128)(2,1)}, bf16[128,4096]{1,0:T(8,128)(2,1)S(1)}, u32[]{:S(2)}, u32[]{:S(2)}) %collective-permute-start.1) | collective-permute-done | bytes 1048608 | tf_op jit(solution)/shard_map/ppermute | solution.py:228
  66.5 0.0 collective-permute-done.2
  66.5 0.0 copy-done.1
  66.5 3.2 %convert_add_fusion.1 = f32[128,4096]{1,0:T(8,128)} fusion(bf16[128,4096]{1,0:T(8,128)(2,1)} %collective-permute-done.2, bf16[128,4096]{1,0:T(8,128)(2,1)S(1)} %collective-permute-done.1, bf16[128,4096]{1,0:T(8,128)(2,1)S(1)} %collective-permute-done, bf16[128,4096]{1,0:T(8,128)(2,1)S(1)} %copy-done.1), kind=kLoop, calls=%fused_computation.1 | loop fusion | flops 3670016 | bytes 6291456 | tf_op jit(solution)/shard_map/add | solution.py:235
  69.7 0.0 copy-start.2
  69.7 0.0 copy-start
  69.7 0.0 reduce-scatter.3.cloned.1.call-update
  69.7 0.0 reduce-scatter.5.cloned.1.call-start
  69.8 1.4 collective-permute-start.3
  71.2 2.1 %collective-permute-start.4 = (bf16[128,4096]{1,0:T(8,128)(2,1)}, bf16[128,4096]{1,0:T(8,128)(2,1)S(1)}, u32[]{:S(2)}, u32[]{:S(2)}) collective-permute-start(bf16[128,4096]{1,0:T(8,128)(2,1)} %get-tuple-element.38), channel_id=1, source_target_pairs={{0,64},{64,128},{128,192},{192,0},{1,65},{65,129},{129,193},{193,1... | collective-permute-start | bytes 3145736 | tf_op jit(solution)/shard_map/ppermute | solution.py:228
  73.2 0.0 copy-done.2
  73.2 0.6 collective-permute-start.5
  73.9 21.5 %collective-permute-done.3 = bf16[128,4096]{1,0:T(8,128)(2,1)S(1)} collective-permute-done((bf16[128,4096]{1,0:T(8,128)(2,1)}, bf16[128,4096]{1,0:T(8,128)(2,1)S(1)}, u32[]{:S(2)}, u32[]{:S(2)}) %collective-permute-start.3) | collective-permute-done | bytes 1048608 | tf_op jit(solution)/shard_map/ppermute | solution.py:228
  95.4 23.7 %collective-permute-done.4 = bf16[128,4096]{1,0:T(8,128)(2,1)S(1)} collective-permute-done((bf16[128,4096]{1,0:T(8,128)(2,1)}, bf16[128,4096]{1,0:T(8,128)(2,1)S(1)}, u32[]{:S(2)}, u32[]{:S(2)}) %collective-permute-start.4) | collective-permute-done | bytes 1048608 | tf_op jit(solution)/shard_map/ppermute | solution.py:228
  119.1 0.0 collective-permute-done.5
  119.1 0.0 copy-done
  119.1 1.9 %convert_add_fusion = f32[128,4096]{1,0:T(8,128)} fusion(bf16[128,4096]{1,0:T(8,128)(2,1)S(1)} %collective-permute-done.5, bf16[128,4096]{1,0:T(8,128)(2,1)S(1)} %collective-permute-done.4, bf16[128,4096]{1,0:T(8,128)(2,1)S(1)} %collective-permute-done.3, bf16[128,4096]{1,0:T(8,128)(2,1)S(1)} %copy-done), kind=kLoop, calls=%fused_computation | loop fusion | flops 3670016 | bytes 6291456 | tf_op jit(solution)/shard_map/add | solution.py:235
  121.1 0.0 reduce-scatter.5.cloned.1.call-update
  121.1 0.0 reduce-scatter.3.cloned.1.call-done.p0_ref
  121.1 41.3 %reduce-scatter.5.cloned.1.call-done.p1_ref = f32[16,4096]{1,0:T(8,128)} async-done(((f32[128,4096]{1,0:T(8,128)}), f32[16,4096]{1,0:T(8,128)}) %reduce-scatter.5.cloned.1.call-update) | async-done | bytes 262160 | tf_op jit(solution)/shard_map/reduce_scatter | solution.py:263
  162.4 3.3 %shard_map.122 = (f32[32,4096]{1,0:T(8,128)}, f32[32,4096]{1,0:T(8,128)}, f32[32,4096]{1,0:T(8,128)}, bf16[8,16,512]{2,1,0:T(8,128)(2,1)}) custom-call(f32[16,4096]{1,0:T(8,128)} %reduce-scatter.3.cloned.1.call-done.p0_ref, f32[16,4096]{1,0:T(8,128)} %reduce-scatter.5.cloned.1.call-done.p1_ref, f32[32,4096]{1,0:T(8,128)} %bitcast.11, f32[32,4096]{1,0:T(8,128)} %bitcast.12, ...), custom_call_target="tpu_custom_call" | custom-call | flops 100663296 | bytes 4194304 | tf_op jit(solution)/shard_map/pallas_call | solution.py:211
  165.7 14.6 %all_to_all.5 = bf16[8,16,512]{2,1,0:T(8,128)(2,1)S(1)} all-to-all(bf16[8,16,512]{2,1,0:T(8,128)(2,1)} %get-tuple-element.43), channel_id=1, replica_groups=mesh['wx'=4,'wz'=8,'tensor'=8] {'tensor'}, dimensions={0} | all-to-all | bytes 262144 | tf_op jit(solution)/shard_map/all_to_all | solution.py:269
  180.3 0.7 copy.14
Async XLA Ops:
  7.2 114.0 %reduce-scatter.3.cloned.1.call-start = ((), (), s32[]{:S(2)}) async-start(), calls=%async_computation.3 | async-start | bytes 2359296 | tf_op jit(solution)/shard_map/reduce_scatter | solution.py:263
  16.6 25.8 %collective-permute-start = (bf16[128,4096]{1,0:T(8,128)(2,1)}, bf16[128,4096]{1,0:T(8,128)(2,1)S(1)}, u32[]{:S(2)}, u32[]{:S(2)}) collective-permute-start(bf16[128,4096]{1,0:T(8,128)(2,1)} %get-tuple-element.25), channel_id=1, source_target_pairs={{0,128},{64,192},{128,0},{192,64},{1,129},{65,193},{129,1},{193,65... | collective-permute-start | bytes 3145736 | tf_op jit(solution)/shard_map/ppermute | solution.py:228
  20.2 46.3 %collective-permute-start.1 = (bf16[128,4096]{1,0:T(8,128)(2,1)}, bf16[128,4096]{1,0:T(8,128)(2,1)S(1)}, u32[]{:S(2)}, u32[]{:S(2)}) collective-permute-start(bf16[128,4096]{1,0:T(8,128)(2,1)} %get-tuple-element.26), channel_id=1, source_target_pairs={{0,64},{64,128},{128,192},{192,0},{1,65},{65,129},{129,193},{193,1... | collective-permute-start | bytes 3145736 | tf_op jit(solution)/shard_map/ppermute | solution.py:228
  20.5 46.0 %copy-start.1 = (bf16[128,4096]{1,0:T(8,128)(2,1)S(1)}, bf16[128,4096]{1,0:T(8,128)(2,1)}, u32[]{:S(2)}) copy-start(bf16[128,4096]{1,0:T(8,128)(2,1)} %get-tuple-element.32) | copy-start | bytes 3145732
  20.5 46.0 %collective-permute-start.2 = (bf16[128,4096]{1,0:T(8,128)(2,1)}, bf16[128,4096]{1,0:T(8,128)(2,1)}, u32[]{:S(2)}, u32[]{:S(2)}) collective-permute-start(bf16[128,4096]{1,0:T(8,128)(2,1)} %get-tuple-element.27), channel_id=1, source_target_pairs={{0,192},{64,0},{128,64},{192,128},{1,193},{65,1},{129,65},{193,129... | collective-permute-start | bytes 3145736 | tf_op jit(solution)/shard_map/ppermute | solution.py:228
  69.7 3.5 %copy-start.2 = (bf16[128,4096]{1,0:T(8,128)(2,1)S(1)}, bf16[128,4096]{1,0:T(8,128)(2,1)}, u32[]{:S(2)}) copy-start(bf16[128,4096]{1,0:T(8,128)(2,1)} %get-tuple-element.39) | copy-start | bytes 3145732
  69.7 49.4 %copy-start = (bf16[128,4096]{1,0:T(8,128)(2,1)S(1)}, bf16[128,4096]{1,0:T(8,128)(2,1)}, u32[]{:S(2)}) copy-start(bf16[128,4096]{1,0:T(8,128)(2,1)} %get-tuple-element.36) | copy-start | bytes 3145732
  69.7 92.7 %reduce-scatter.5.cloned.1.call-start = ((), (), s32[]{:S(2)}) async-start(), calls=%async_computation.4 | async-start | bytes 2359296 | tf_op jit(solution)/shard_map/reduce_scatter | solution.py:263
  69.8 25.6 %collective-permute-start.3 = (bf16[128,4096]{1,0:T(8,128)(2,1)}, bf16[128,4096]{1,0:T(8,128)(2,1)S(1)}, u32[]{:S(2)}, u32[]{:S(2)}) collective-permute-start(bf16[128,4096]{1,0:T(8,128)(2,1)} %get-tuple-element.37), channel_id=1, source_target_pairs={{0,128},{64,192},{128,0},{192,64},{1,129},{65,193},{129,1},{193,65... | collective-permute-start | bytes 3145736 | tf_op jit(solution)/shard_map/ppermute | solution.py:228
  71.2 47.9 %collective-permute-start.4 = (bf16[128,4096]{1,0:T(8,128)(2,1)}, bf16[128,4096]{1,0:T(8,128)(2,1)S(1)}, u32[]{:S(2)}, u32[]{:S(2)}) collective-permute-start(bf16[128,4096]{1,0:T(8,128)(2,1)} %get-tuple-element.38), channel_id=1, source_target_pairs={{0,64},{64,128},{128,192},{192,0},{1,65},{65,129},{129,193},{193,1... | collective-permute-start | bytes 3145736 | tf_op jit(solution)/shard_map/ppermute | solution.py:228
  73.2 45.9 %collective-permute-start.5 = (bf16[128,4096]{1,0:T(8,128)(2,1)S(1)}, bf16[128,4096]{1,0:T(8,128)(2,1)S(1)}, u32[]{:S(2)}, u32[]{:S(2)}) collective-permute-start(bf16[128,4096]{1,0:T(8,128)(2,1)S(1)} %copy-done.2), channel_id=1, source_target_pairs={{0,192},{64,0},{128,64},{192,128},{1,193},{65,1},{129,65},{193,129... | collective-permute-start | bytes 3145736 | tf_op jit(solution)/shard_map/ppermute | solution.py:228
Sparse Core Ops, SparseCore 0:
  69.9 41.2 reduce-scatter.2
  121.2 41.1 reduce-scatter.4
